TPU v7x, 32 devices: a whole 2x2x4 slice. The times are simulated.
32 devices in a mesh: views: 4 (over y, x), depth: 4 (over z), lat: 2 (over core).
Axes of the slice: x: 2, y: 2, z: 4, core: 2. Of those that a mesh axis runs over, the one named last changes fastest.
Arguments:
- density: bfloat16 [64, 2, 16, 1024], P(None, None, 'depth', 'lat'), may hold values from 0 to 3, as said below
- measured: float32 [16, 64, 1024], P('views', None, 'lat'), may hold values from 0 to 4
- shear_shift: int32 [16, 16], P('views', 'depth'), may hold values from -64 to 63
- shear_frac: float32 [16, 16], P('views', 'depth'), may hold values from 0 to 1
- spectrum: float32 [64], replicated, may hold values from 0.05 to 1
- attenuation: float32 [2, 64], replicated, may hold values from 0.3 to 6
Outputs:
- density_gradient: float32 [64, 2, 16, 1024], P('views', None, 'depth', 'lat')
Inputs may be any that keep to these rules, and one draw needn't show every extreme that they name: `density`: densities are non-negative.
All inputs are finite; a program needn't handle non-finite values.
Results may differ from a plain program's by a relative error of at most 0.0016.
Values may be sent and summed in bfloat16 or wider, within the bound.
No kernel may reach another device: no remote copies, remote signals or barrier semaphores. Data moves between devices by JAX's collectives and lax.ppermute only.
A program may use at most 64 MiB of HBM per device.

v0:
```python
import jax
import jax.numpy as jnp
from jax import lax
from jax.sharding import PartitionSpec as P

HALO = 64


def with_halo(x, sides, width):
    for axis, dim in sides:
        size, length = (lax.axis_size(axis), x.shape[dim])
        up = [(i, (i + 1) % size) for i in range(size - 1)]
        down = [(j, i) for i, j in up]
        last = lax.slice_in_dim(x, length - width, length, axis=dim)
        first = lax.slice_in_dim(x, 0, width, axis=dim)
        before = lax.ppermute(last, axis, up)
        after = lax.ppermute(first, axis, down)
        x = jnp.concatenate([before, x, after], axis=dim)
    return x


def band_forward(shear_shift, lower_weight, upper_weight, window, block_width):
    band_shape = (shear_shift.shape[1], window, shear_shift.shape[0], block_width)
    tap_index = lax.broadcasted_iota(jnp.int32, band_shape, 1)
    column = lax.broadcasted_iota(jnp.int32, band_shape, 3)
    anchor = (shear_shift.T + HALO)[:, None, :, None]
    nothing = jnp.zeros((), jnp.bfloat16)
    lower_part = jnp.where(tap_index == column + anchor, lower_weight.T[:, None, :, None], nothing)
    upper_part = jnp.where(
        tap_index == column + anchor + 1, upper_weight.T[:, None, :, None], nothing
    )
    return lower_part + upper_part


def band_backward(shear_shift, lower_weight, upper_weight, window, block_width):
    band_shape = (shear_shift.shape[0], window, shear_shift.shape[1], block_width)
    tap_index = lax.broadcasted_iota(jnp.int32, band_shape, 1)
    column = lax.broadcasted_iota(jnp.int32, band_shape, 3)
    anchor = (HALO - shear_shift)[:, None, :, None]
    nothing = jnp.zeros((), jnp.bfloat16)
    lower_part = jnp.where(tap_index == column + anchor, lower_weight[:, None, :, None], nothing)
    upper_part = jnp.where(
        tap_index == column + anchor - 1, upper_weight[:, None, :, None], nothing
    )
    return lower_part + upper_part


def spectral(path_sums, observed, spectrum, attenuation, views_all):
    view_count, row_count, materials, tile_width = path_sums.shape
    block_pixels = 4096
    path_water = path_sums[:, :, 0, :].reshape(-1, block_pixels)
    path_bone = path_sums[:, :, 1, :].reshape(-1, block_pixels)
    target_flat = observed.reshape(-1, block_pixels)
    coefficients = jnp.concatenate(
        [jnp.ones((1, spectrum.shape[0]), jnp.float32), attenuation], axis=0
    )
    emitted = jnp.log(jnp.sum(spectrum))

    def one_block(inputs):
        water_block, bone_block, target_block = inputs
        exponent = (
            attenuation[0][:, None] * water_block[None, :]
            + attenuation[1][:, None] * bone_block[None, :]
        )
        counts = spectrum[:, None] * jnp.exp(-exponent)
        moments = jnp.dot(coefficients, counts, precision=lax.Precision.HIGHEST)
        intensity = moments[0]
        residual = emitted - jnp.log(intensity) - target_block
        factor = residual / intensity / views_all
        return (moments[1:] * factor[None, :]).astype(jnp.bfloat16)

    stacked = lax.map(one_block, (path_water, path_bone, target_flat))
    gradients = jnp.swapaxes(stacked, 0, 1).reshape(materials, view_count, row_count, tile_width)
    return jnp.transpose(gradients, (1, 2, 0, 3))


def per_device(density, measured, shear_shift, shear_frac, spectrum, attenuation):
    row_total, materials, depth_here, tile_width = density.shape
    block_width = min(128, tile_width)
    block_count = tile_width // block_width
    window = block_width + 2 * HALO
    views_all = measured.shape[0] * lax.axis_size("views")
    depth_all = depth_here * lax.axis_size("depth")
    rows_out = row_total // lax.axis_size("views")
    lower_weight = (1.0 - shear_frac).astype(jnp.bfloat16)
    upper_weight = shear_frac.astype(jnp.bfloat16)
    rows_here = density.shape[0]
    padded = with_halo(density, (("lat", 3),), HALO)
    framed = jnp.stack(
        [
            padded[:, :, :, number * block_width : number * block_width + window]
            for number in range(block_count)
        ],
        axis=2,
    )
    forward_band = band_forward(shear_shift, lower_weight, upper_weight, window, block_width)
    partial_value = jnp.einsum(
        "ymnzi,zivc->vymnc", framed, forward_band, preferred_element_type=jnp.float32
    )
    partial_value = partial_value.reshape(shear_shift.shape[0], rows_here, materials, tile_width)
    shares = lax.psum_scatter(partial_value, "depth", scatter_dimension=3, tiled=True) / depth_all
    share_cols = shares.shape[3]
    observed = lax.dynamic_slice_in_dim(
        measured, lax.axis_index("depth") * share_cols, share_cols, 2
    )
    share_grads = spectral(shares, observed, spectrum, attenuation, views_all)
    path_grads = lax.all_gather(share_grads, "depth", axis=3, tiled=True)
    padded_grads = with_halo(path_grads, (("lat", 3),), HALO)
    framed_grads = jnp.stack(
        [
            padded_grads[:, :, :, number * block_width : number * block_width + window]
            for number in range(block_count)
        ],
        axis=3,
    )
    backward_band = band_backward(shear_shift, lower_weight, upper_weight, window, block_width)
    product = jnp.einsum(
        "vymni,vizc->ymznc", framed_grads, backward_band, preferred_element_type=jnp.float32
    )
    return lax.psum_scatter(
        product.reshape(rows_out * lax.axis_size("views"), materials, depth_here, tile_width),
        "views",
        scatter_dimension=0,
        tiled=True,
    )


def solution(mesh):
    in_specs = (
        P(None, None, "depth", "lat"),
        P("views", None, "lat"),
        P("views", "depth"),
        P("views", "depth"),
        P(),
        P(),
    )
    out_specs = P("views", None, "depth", "lat")
    return jax.shard_map(
        per_device, mesh=mesh, in_specs=in_specs, out_specs=out_specs, check_vma=False
    )
```

profile of v0, /device:TPU:0, one launch (start us, length us, event | category | flops | bytes accessed | tf_op | source)
XLA Modules:
  0.0 114.8 jit_solution(7488364449556810122)
XLA Ops:
  6.5 1.3 %copy.23 = bf16[64,2,4,512]{3,0,2,1:T(8,128)(2,1)S(1)} copy(bf16[64,2,4,512]{3,2,1,0:T(4,128)(2,1)} %param.8) | data formatting | bytes 1048576 | tf_op args[0]
  7.8 0.1 fusion.62
  7.9 2.4 %collective-permute-start = (bf16[64,2,4,64]{3,0,2,1:T(8,128)(2,1)S(1)}, bf16[64,2,4,64]{3,0,2,1:T(8,128)(2,1)S(1)}, u32[]{:S(2)}, u32[]{:S(2)}) collective-permute-start(bf16[64,2,4,64]{3,0,2,1:T(8,128)(2,1)S(1)} %get-tuple-element.85), channel_id=1, source_target_pairs={{0,1},{2,3},{4,5},{6,7},{8,9},{10,11},{12,13},{14,15},{16,17},{18,... | collective-permute-start | bytes 196616 | tf_op jit(solution)/shard_map/ppermute | solution.py:16
  10.3 1.3 %collective-permute-start.1 = (bf16[64,2,4,64]{3,0,2,1:T(8,128)(2,1)S(1)}, bf16[64,2,4,64]{3,0,2,1:T(8,128)(2,1)S(1)}, u32[]{:S(2)}, u32[]{:S(2)}) collective-permute-start(bf16[64,2,4,64]{3,0,2,1:T(8,128)(2,1)S(1)} %get-tuple-element.86), channel_id=1, source_target_pairs={{1,0},{3,2},{5,4},{7,6},{9,8},{11,10},{13,12},{15,14},{17,16},{19,... | collective-permute-start | bytes 196616 | tf_op jit(solution)/shard_map/ppermute | solution.py:17
  11.7 1.9 %collective-permute-done.1 = bf16[64,2,4,64]{3,0,2,1:T(8,128)(2,1)S(1)} collective-permute-done((bf16[64,2,4,64]{3,0,2,1:T(8,128)(2,1)S(1)}, bf16[64,2,4,64]{3,0,2,1:T(8,128)(2,1)S(1)}, u32[]{:S(2)}, u32[]{:S(2)}) %collective-permute-start.1) | collective-permute-done | bytes 65568 | tf_op jit(solution)/shard_map/ppermute | solution.py:17
  13.6 0.6 fusion.54
  14.1 1.1 convolution_bitcast_fusion.2
  15.3 1.1 copy.42
  16.6 0.5 copy-done.4
  17.0 0.7 reduce_sum.9
  18.4 27.5 %reduce-scatter.3.cloned.1.call-done = f32[4,64,2,128]{3,1,2,0:T(8,128)} async-done(((f32[4,64,2,512]{3,1,2,0:T(8,128)}), f32[4,64,2,128]{3,1,2,0:T(8,128)}) %reduce-scatter.3.cloned.1.call-update) | async-done | bytes 262160 | tf_op jit(solution)/shard_map/reduce_scatter | solution.py:101
  45.9 1.0 broadcast_multiply_fusion
  47.0 8.8 %while.10 = (s32[]{:T(128)}, bf16[8,2,4096]{2,1,0:T(2,128)(2,1)S(1)}, f32[64]{0:T(128)S(1)}, f32[2,64]{1,0:T(2,128)S(1)}, f32[8,4096]{1,0:T(8,128)S(1)}, /*index...) while((s32[]{:T(128)}, ...), condition=%wide.region_3.4_spmd, body=%wide.region_2.3_spmd.sunk | while | flops 10780674 | bytes 264821 | solution.py:72
  47.1 0.9 convolution_bitcast_fusion.4
  48.2 0.9 convolution_bitcast_fusion.4
  49.3 0.9 convolution_bitcast_fusion.4
  50.4 0.9 convolution_bitcast_fusion.4
  51.5 0.9 convolution_bitcast_fusion.4
  52.6 0.9 convolution_bitcast_fusion.4
  53.7 0.9 convolution_bitcast_fusion.4
  54.8 0.9 convolution_bitcast_fusion.4
  56.0 15.2 %all_gather.3 = bf16[4,64,2,512]{3,1,0,2:T(8,128)(2,1)S(1)} all-gather(bf16[4,64,2,128]{3,1,0,2:T(8,128)(2,1)S(1)} %bitcast.98), channel_id=1, replica_groups=mesh['views'=4,'depth'=4,'lat'=2] {'depth'}, dimensions={3}, use_global_device_ids=true | all-gather | bytes 655360 | tf_op jit(solution)/shard_map/all_gather | solution.py:107
  71.2 0.1 fusion.61
  71.3 1.3 %collective-permute-start.2 = (bf16[4,64,2,64]{3,1,0,2:T(8,128)(2,1)S(1)}, bf16[4,64,2,64]{3,1,0,2:T(8,128)(2,1)S(1)}, u32[]{:S(2)}, u32[]{:S(2)}) collective-permute-start(bf16[4,64,2,64]{3,1,0,2:T(8,128)(2,1)S(1)} %get-tuple-element.79), channel_id=1, source_target_pairs={{0,1},{2,3},{4,5},{6,7},{8,9},{10,11},{12,13},{14,15},{16,17},{18,... | collective-permute-start | bytes 196616 | tf_op jit(solution)/shard_map/ppermute | solution.py:16
  72.6 1.3 %collective-permute-start.3 = (bf16[4,64,2,64]{3,1,0,2:T(8,128)(2,1)S(1)}, bf16[4,64,2,64]{3,1,0,2:T(8,128)(2,1)S(1)}, u32[]{:S(2)}, u32[]{:S(2)}) collective-permute-start(bf16[4,64,2,64]{3,1,0,2:T(8,128)(2,1)S(1)} %get-tuple-element.80), channel_id=1, source_target_pairs={{1,0},{3,2},{5,4},{7,6},{9,8},{11,10},{13,12},{15,14},{17,16},{19,... | collective-permute-start | bytes 196616 | tf_op jit(solution)/shard_map/ppermute | solution.py:17
  74.2 1.6 %collective-permute-done.3 = bf16[4,64,2,64]{3,1,0,2:T(8,128)(2,1)S(1)} collective-permute-done((bf16[4,64,2,64]{3,1,0,2:T(8,128)(2,1)S(1)}, bf16[4,64,2,64]{3,1,0,2:T(8,128)(2,1)S(1)}, u32[]{:S(2)}, u32[]{:S(2)}) %collective-permute-start.3) | collective-permute-done | bytes 65568 | tf_op jit(solution)/shard_map/ppermute | solution.py:17
  75.8 0.6 fusion.52
  76.4 1.1 convolution_bitcast_fusion.1
  77.5 0.7 copy.34
  78.2 1.4 %reshape.24 = f32[64,2,4,512]{3,0,2,1:T(8,128)} reshape(f32[64,2,4,4,128]{4,3,0,2,1:T(4,128)S(1)} %copy.34) | data formatting | bytes 2097152 | tf_op jit(solution)/shard_map/reshape | solution.py:121
  79.6 26.5 %reduce-scatter.5.cloned.1.call-done = f32[16,2,4,512]{3,0,2,1:T(8,128)} async-done(((f32[64,2,4,512]{3,0,2,1:T(8,128)}), f32[16,2,4,512]{3,0,2,1:T(8,128)}) %reduce-scatter.5.cloned.1.call-update) | async-done | bytes 262160 | tf_op jit(solution)/shard_map/reduce_scatter | solution.py:120
  106.2 1.8 %copy.35 = f32[16,2,4,512]{3,2,1,0:T(4,128)} copy(f32[16,2,4,512]{3,0,2,1:T(8,128)} %reduce-scatter.5.cloned.1.call-done) | data formatting | bytes 524288 | tf_op jit(solution)/shard_map/reduce_scatter | solution.py:120
  (61 shorter events, 1.8 us)
Async XLA Ops:
  6.5 10.0 %copy-start = (f32[4,64,512]{2,1,0:T(8,128)S(1)}, f32[4,64,512]{2,1,0:T(8,128)}, u32[]{:S(2)}) copy-start(f32[4,64,512]{2,1,0:T(8,128)} %param.9) | copy-start | bytes 1572868
  6.5 5.1 %copy-start.2 = (s32[4,4]{1,0:T(4,128)S(1)}, s32[4,4]{1,0:T(4,128)}, u32[]{:S(2)}) copy-start(s32[4,4]{1,0:T(4,128)} %param.10) | copy-start | bytes 196
  6.5 5.1 %copy-start.3 = (f32[4,4]{1,0:T(4,128)S(1)}, f32[4,4]{1,0:T(4,128)}, u32[]{:S(2)}) copy-start(f32[4,4]{1,0:T(4,128)} %param.11) | copy-start | bytes 196
  6.5 39.4 %reduce-scatter.3.cloned.1.call-start = ((), (), s32[]{:S(2)}) async-start(), calls=%async_computation.2 | async-start | bytes 1310720 | tf_op jit(solution)/shard_map/reduce_scatter | solution.py:101
  7.9 3.8 %collective-permute-start = (bf16[64,2,4,64]{3,0,2,1:T(8,128)(2,1)S(1)}, bf16[64,2,4,64]{3,0,2,1:T(8,128)(2,1)S(1)}, u32[]{:S(2)}, u32[]{:S(2)}) collective-permute-start(bf16[64,2,4,64]{3,0,2,1:T(8,128)(2,1)S(1)} %get-tuple-element.85), channel_id=1, source_target_pairs={{0,1},{2,3},{4,5},{6,7},{8,9},{10,11},{12,13},{14,15},{16,17},{18,... | collective-permute-start | bytes 196616 | tf_op jit(solution)/shard_map/ppermute | solution.py:16
  10.3 3.2 %collective-permute-start.1 = (bf16[64,2,4,64]{3,0,2,1:T(8,128)(2,1)S(1)}, bf16[64,2,4,64]{3,0,2,1:T(8,128)(2,1)S(1)}, u32[]{:S(2)}, u32[]{:S(2)}) collective-permute-start(bf16[64,2,4,64]{3,0,2,1:T(8,128)(2,1)S(1)} %get-tuple-element.86), channel_id=1, source_target_pairs={{1,0},{3,2},{5,4},{7,6},{9,8},{11,10},{13,12},{15,14},{17,16},{19,... | collective-permute-start | bytes 196616 | tf_op jit(solution)/shard_map/ppermute | solution.py:17
  16.4 0.7 copy-start.4
  16.4 2.0 %copy-start.1 = (f32[2,64]{1,0:T(2,128)S(1)}, f32[2,64]{1,0:T(2,128)}, u32[]{:S(2)}) copy-start(f32[2,64]{1,0:T(2,128)} %param.13) | copy-start | bytes 1540
  16.4 89.7 %reduce-scatter.5.cloned.1.call-start = ((), (), s32[]{:S(2)}) async-start(), calls=%async_computation.3 | async-start | bytes 1310720 | tf_op jit(solution)/shard_map/reduce_scatter | solution.py:120
  71.3 2.9 %collective-permute-start.2 = (bf16[4,64,2,64]{3,1,0,2:T(8,128)(2,1)S(1)}, bf16[4,64,2,64]{3,1,0,2:T(8,128)(2,1)S(1)}, u32[]{:S(2)}, u32[]{:S(2)}) collective-permute-start(bf16[4,64,2,64]{3,1,0,2:T(8,128)(2,1)S(1)} %get-tuple-element.79), channel_id=1, source_target_pairs={{0,1},{2,3},{4,5},{6,7},{8,9},{10,11},{12,13},{14,15},{16,17},{18,... | collective-permute-start | bytes 196616 | tf_op jit(solution)/shard_map/ppermute | solution.py:16
  72.6 3.2 %collective-permute-start.3 = (bf16[4,64,2,64]{3,1,0,2:T(8,128)(2,1)S(1)}, bf16[4,64,2,64]{3,1,0,2:T(8,128)(2,1)S(1)}, u32[]{:S(2)}, u32[]{:S(2)}) collective-permute-start(bf16[4,64,2,64]{3,1,0,2:T(8,128)(2,1)S(1)} %get-tuple-element.80), channel_id=1, source_target_pairs={{1,0},{3,2},{5,4},{7,6},{9,8},{11,10},{13,12},{15,14},{17,16},{19,... | collective-permute-start | bytes 196616 | tf_op jit(solution)/shard_map/ppermute | solution.py:17
Sparse Core Ops, SparseCore 0:
  16.5 29.3 reduce-scatter.2
  79.8 26.3 reduce-scatter.4
where the time goes:
time: 115 us
  waiting for transfers between devices  57.6 us (50%)
  blocking collectives  15.2 us (13%)
  between operations  14.3 us (12%)
  matrix products  9.67 us (8%)
  local copies, waits for them, and re-layouts  7.82 us (7%)
  starting transfers between devices  6.33 us (6%)
  other arithmetic  3.57 us (3%)
    reduce_scatter x1, waiting for transfers between devices, per_device(): lax.psum_scatter(partial_value, 'depth', scatter_dimension=3, tiled=True)  27.5 us
    reduce_scatter x1, waiting for transfers between devices, per_device(): lax.psum_scatter(product.reshape(rows_out * lax.axis_size('views'), mater...  26.5 us
    all_gather x1, blocking collectives, per_device(): path_grads = lax.all_gather(share_grads, 'depth', axis=3, tiled=True)  15.2 us
    dot_general x8, matrix products, one_block(): moments = jnp.dot(coefficients, counts, precision=lax.Precision.HIGHEST)  7.39 us
    ppermute x2, starting transfers between devices, with_halo(): before = lax.ppermute(last, axis, up)  3.7 us
    ppermute x2, waiting for transfers between devices, with_halo(): after = lax.ppermute(first, axis, down)  3.52 us
    ppermute x2, starting transfers between devices, with_halo(): after = lax.ppermute(first, axis, down)  2.58 us
  transfers between devices with their start and end apart: 6, of which 4 were waited for; matrix products, arithmetic and copies ran while one was open for 1% of the time, Pallas kernels for 0%

commit v1 on v0

--- a/solution.py
+++ b/solution.py
@@ -2,6 +2,8 @@
 import jax.numpy as jnp
 from jax import lax
 from jax.sharding import PartitionSpec as P
+from jax.experimental import pallas as pl
+from jax.experimental.pallas import tpu as pltpu
 
 HALO = 64
 
@@ -125,6 +127,123 @@
     )
 
 
+LANES = 128
+INTERPRET = False
+
+
+def shear_kernel(rot_ref, thr_ref, wa_ref, wb_ref, src_ref, out_ref):
+    outer_count, channels, width = src_ref.shape
+    inner_count, _, out_width = out_ref.shape
+    pieces = width // LANES
+    out_pieces = out_width // LANES
+    out_ref[...] = jnp.zeros(out_ref.shape, jnp.float32)
+    lane = lax.broadcasted_iota(jnp.int32, (channels, LANES), 1)
+
+    def outer(o, carry):
+        cols = [src_ref[o, :, k * LANES : (k + 1) * LANES] for k in range(pieces)]
+        turned = [pltpu.roll(c, LANES - 1, 1) for c in cols]
+        nexts = [
+            jnp.where(lane < LANES - 1, turned[k], turned[k + 1]) for k in range(pieces - 1)
+        ] + [turned[pieces - 1]]
+        for i in range(inner_count):
+            wa = wa_ref[o, i]
+            wb = wb_ref[o, i]
+            mixed = [wa * cols[k] + wb * nexts[k] for k in range(pieces)]
+            rolled = [pltpu.roll(m, rot_ref[o, i], 1) for m in mixed]
+            keep = lane < thr_ref[o, i]
+            for j in range(out_pieces):
+                out_ref[i, :, j * LANES : (j + 1) * LANES] += jnp.where(
+                    keep, rolled[j], rolled[j + 1]
+                )
+        return carry
+
+    lax.fori_loop(0, outer_count, outer, 0)
+
+
+def shear_apply(offset, wa, wb, src, out_width):
+    outer_count, channels, width = src.shape
+    inner_count = offset.shape[1]
+    rot = (LANES - offset) % LANES
+    thr = LANES - offset
+    smem = pl.BlockSpec(memory_space=pltpu.SMEM)
+    vmem = pl.BlockSpec(memory_space=pltpu.VMEM)
+    return pl.pallas_call(
+        shear_kernel,
+        out_shape=jax.ShapeDtypeStruct((inner_count, channels, out_width), jnp.float32),
+        in_specs=[smem, smem, smem, smem, vmem],
+        out_specs=vmem,
+        interpret=INTERPRET,
+    )(rot.astype(jnp.int32), thr.astype(jnp.int32), wa, wb, src)
+
+
+def rows_fit(density, measured):
+    rows = density.shape[0]
+    groups = lax.axis_size("views")
+    depth = lax.axis_size("depth")
+    tile_width = density.shape[3]
+    return (
+        rows % groups == 0
+        and (rows // groups) % depth == 0
+        and tile_width % LANES == 0
+        and 2 * HALO <= LANES
+        and tile_width >= HALO
+    )
+
+
+def per_device_rows(density, measured, shear_shift, shear_frac, spectrum, attenuation):
+    row_total, materials, depth_here, tile_width = density.shape
+    groups = lax.axis_size("views")
+    depth_count = lax.axis_size("depth")
+    views_here = measured.shape[0]
+    views_all = views_here * groups
+    depth_all = depth_here * depth_count
+    rows_group = row_total // groups
+    rows_here = rows_group // depth_count
+    group = lax.axis_index("views")
+    slab = lax.axis_index("depth")
+
+    lower_weight = (1.0 - shear_frac).astype(jnp.bfloat16).astype(jnp.float32)
+    upper_weight = shear_frac.astype(jnp.bfloat16).astype(jnp.float32)
+    table = jnp.stack([shear_shift.astype(jnp.float32), lower_weight, upper_weight])
+    table = lax.all_gather(table, ("views", "depth"), axis=0, tiled=False)
+    table = table.reshape(groups, depth_count, 3, views_here, depth_here)
+    table = jnp.transpose(table, (2, 0, 3, 1, 4)).reshape(3, views_all, depth_all)
+    shift_all = table[0].astype(jnp.int32)
+    lower_all = table[1]
+    upper_all = table[2]
+
+    observed = measured.reshape(views_here, groups, rows_group, tile_width)
+    observed = lax.dynamic_slice_in_dim(observed, slab * rows_here, rows_here, 2)
+    observed = lax.all_to_all(observed, "views", 1, 0, tiled=True)
+    observed = observed.reshape(views_all, rows_here, tile_width)
+
+    mine = lax.dynamic_slice_in_dim(density, group * rows_group, rows_group, 0)
+    mine = jnp.transpose(mine, (2, 0, 1, 3))
+    mine = lax.all_to_all(mine, "depth", 1, 0, tiled=True)
+    mine = mine.reshape(depth_all, rows_here * materials, tile_width)
+    padded = with_halo(mine, (("lat", 2),), HALO).astype(jnp.float32)
+
+    sums = shear_apply(
+        (shift_all + HALO).T, lower_all.T, upper_all.T, padded, tile_width
+    )
+    sums = (sums / depth_all).reshape(views_all, rows_here, materials, tile_width)
+    grads = spectral(sums, observed, spectrum, attenuation, views_all)
+    grads = grads.reshape(views_all, rows_here * materials, tile_width)
+    padded_grads = with_halo(grads, (("lat", 2),), HALO).astype(jnp.float32)
+    layers = shear_apply(
+        HALO - 1 - shift_all, upper_all, lower_all, padded_grads, tile_width
+    )
+    layers = layers.reshape(depth_all, rows_here, materials, tile_width)
+    layers = lax.all_to_all(layers, "depth", 0, 1, tiled=True)
+    return jnp.transpose(layers, (1, 2, 0, 3))
+
+
+def per_device_any(density, measured, shear_shift, shear_frac, spectrum, attenuation):
+    if rows_fit(density, measured):
+        return per_device_rows(density, measured, shear_shift, shear_frac, spectrum, attenuation)
+    return per_device(density, measured, shear_shift, shear_frac, spectrum, attenuation)
+
+
 def solution(mesh):
     in_specs = (
         P(None, None, "depth", "lat"),
@@ -136,5 +255,5 @@
     )
     out_specs = P("views", None, "depth", "lat")
     return jax.shard_map(
-        per_device, mesh=mesh, in_specs=in_specs, out_specs=out_specs, check_vma=False
-    )
+        per_device_any, mesh=mesh, in_specs=in_specs, out_specs=out_specs, check_vma=False
+    )

time: 115 us -> 108 us (0.939)
  waiting for transfers between devices: 57.6 us -> 0.24 us
  blocking collectives: 15.2 us -> 54.3 us
  between operations: 14.3 us -> 0.91 us
  starting transfers between devices: 6.33 us -> 18.3 us
  Pallas kernels: 0 us -> 11.1 us
  matrix products: 9.67 us -> 7.39 us
  other arithmetic: 3.57 us -> 5.3 us
  local copies, waits for them, and re-layouts: 7.82 us -> 9.28 us
    reduce_scatter x2 -> x0, waiting for transfers between devices: 54 us -> none  [the longest x1 27.5 us: per_device(): lax.psum_scatter(partial_value, 'depth', scatter_dimension=3, tiled=True)]
    all_gather x1, blocking collectives: 15.2 us -> 42.2 us  [per_device_rows(): table = lax.all_gather(table, ('views', 'depth'), axis=0, tiled=False)]
    all_to_all x0 -> x1, blocking collectives: none -> 12.1 us  [per_device_rows(): layers = lax.all_to_all(layers, 'depth', 0, 1, tiled=True)]
    pallas_call x0 -> x2, Pallas kernels: none -> 11.1 us  [shear_apply(): pl.pallas_call(shear_kernel, out_shape=jax.ShapeDtypeStruct((inner_count,...]
    all_to_all x0 -> x2, starting transfers between devices: none -> 9.68 us  [the longest x1 6.35 us: per_device_rows(): mine = lax.all_to_all(mine, 'depth', 1, 0, tiled=True)]
    ppermute x2, waiting for transfers between devices: 3.52 us -> 0.01 us  [with_halo(): after = lax.ppermute(first, axis, down)]
    ppermute x2, starting transfers between devices: 3.7 us -> 6.06 us  [with_halo(): before = lax.ppermute(last, axis, up)]
    dot_general x2 -> x0, matrix products: 2.29 us -> none  [the longest x1 1.14 us: per_device(): jnp.einsum('ymnzi,zivc->vymnc', framed, forward_band, preferred_element_t...]
  transfers between devices with their start and end apart: 6 -> 6, of which waited for: 4 -> 1; matrix products, arithmetic and copies ran while one was open for 1% -> 4% of each run, Pallas kernels for 0% -> 0%
where the time goes in v1:
time: 108 us; the launch traced here: 107 us
  blocking collectives  54.3 us (50%)
  starting transfers between devices  18.3 us (17%)
  Pallas kernels  11.1 us (10%)
  local copies, waits for them, and re-layouts  9.28 us (9%)
  matrix products  7.39 us (7%)
  other arithmetic  5.3 us (5%)
    all_gather x1, blocking collectives, per_device_rows(): table = lax.all_gather(table, ('views', 'depth'), axis=0, tiled=False)  42.2 us
    all_to_all x1, blocking collectives, per_device_rows(): layers = lax.all_to_all(layers, 'depth', 0, 1, tiled=True)  12.1 us
    pallas_call x2, Pallas kernels, shear_apply(): pl.pallas_call(shear_kernel, out_shape=jax.ShapeDtypeStruct((inner_count,...  11.1 us
    dot_general x8, matrix products, one_block(): moments = jnp.dot(coefficients, counts, precision=lax.Precision.HIGHEST)  7.39 us
    all_to_all x1, starting transfers between devices, per_device_rows(): mine = lax.all_to_all(mine, 'depth', 1, 0, tiled=True)  6.35 us
    ppermute x2, starting transfers between devices, with_halo(): before = lax.ppermute(last, axis, up)  6.06 us
    all_to_all x1, starting transfers between devices, per_device_rows(): observed = lax.all_to_all(observed, 'views', 1, 0, tiled=True)  3.33 us
    ppermute x2, starting transfers between devices, with_halo(): after = lax.ppermute(first, axis, down)  2.56 us
  transfers between devices with their start and end apart: 6, of which 1 were waited for; matrix products, arithmetic and copies ran while one was open for 4% of the time, Pallas kernels for 0%

profile of v1, /device:TPU:0, one launch (start us, length us, event | category | flops | bytes accessed | tf_op | source)
XLA Modules:
  0.0 107.1 jit_solution(12698678587014280705)
XLA Ops:
  0.0 1.7 %dynamic-slice_bitcast_fusion = bf16[4,16,2,512]{3,0,2,1:T(4,128)(2,1)} fusion(bf16[64,2,4,512]{3,2,1,0:T(4,128)(2,1)} %param.8, s32[]{:T(128)S(6)} %select_n.19), kind=kLoop, calls=%fused_computation.28 | loop fusion | bytes 262148 | tf_op jit(solution)/shard_map/transpose | solution.py:221
  1.7 6.3 %all-to-all-start = ((bf16[4,16,2,512]{3,0,2,1:T(4,128)(2,1)}), bf16[4,16,2,512]{3,0,2,1:T(4,128)(2,1)S(1)}, u32[]{:S(2)}, u32[]{:S(2)}) async-start(bf16[4,16,2,512]{3,0,2,1:T(4,128)(2,1)} %dynamic-slice_bitcast_fusion), calls=%async_computation | async-start | bytes 262144 | tf_op jit(solution)/shard_map/all_to_all | solution.py:222
  8.0 0.7 copy-done.6
  8.7 0.7 copy-done.7
  9.4 42.2 %all-gather = f32[48,4,4]{2,1,0:T(4,128)S(1)} all-gather(f32[3,4,4]{2,1,0:T(4,128)S(1)} %pad_maximum_fusion), channel_id=2, replica_groups=mesh['views'=4,'depth'=4,'lat'=2] {'views','depth'}, dimensions={0}, use_global_device_ids=true | all-gather | bytes 3264 | tf_op jit(solution)/shard_map/all_gather | solution.py:208
  51.9 0.7 copy.22
  52.5 3.3 %all-to-all-start.1 = ((f32[4,4,4,512]{3,2,0,1:T(4,128)}), f32[4,4,4,512]{3,2,0,1:T(4,128)S(1)}, u32[]{:S(2)}, u32[]{:S(2)}) async-start(f32[4,4,4,512]{3,2,0,1:T(4,128)} %copy.22), calls=%async_computation.1 | async-start | bytes 262144 | tf_op jit(solution)/shard_map/all_to_all | solution.py:217
  56.1 1.3 %collective-permute-start.1 = (bf16[16,8,64]{2,1,0:T(8,128)(2,1)S(1)}, bf16[16,8,64]{2,1,0:T(8,128)(2,1)S(1)}, u32[]{:S(2)}, u32[]{:S(2)}) collective-permute-start(bf16[16,8,64]{2,1,0:T(8,128)(2,1)S(1)} %get-tuple-element.80), channel_id=1, source_target_pairs={{1,0},{3,2},{5,4},{7,6},{9,8},{11,10},{13,12},{15,14},{17,16},{19,... | collective-permute-start | bytes 49160 | tf_op jit(solution)/shard_map/ppermute | solution.py:19
  57.4 3.0 %collective-permute-start = (bf16[16,8,64]{2,1,0:T(8,128)(2,1)S(1)}, bf16[16,8,64]{2,1,0:T(8,128)(2,1)S(1)}, u32[]{:S(2)}, u32[]{:S(2)}) collective-permute-start(bf16[16,8,64]{2,1,0:T(8,128)(2,1)S(1)} %get-tuple-element.79), channel_id=1, source_target_pairs={{0,1},{2,3},{4,5},{6,7},{8,9},{10,11},{12,13},{14,15},{16,17},{18,... | collective-permute-start | bytes 49160 | tf_op jit(solution)/shard_map/ppermute | solution.py:18
  61.3 0.7 copy.17.wa_ref
  62.0 0.7 copy.18.wb_ref
  64.1 0.8 maximum_convert_fusion.src_ref
  65.0 5.5 %shard_map.64 = f32[16,8,512]{2,1,0:T(8,128)} custom-call(s32[16,16]{1,0:T(8,128)} %add_select_fusion.rot_ref, s32[16,16]{1,0:T(8,128)} %bitcast.83, f32[16,16]{1,0:T(8,128)} %copy.17.wa_ref, f32[16,16]{1,0:T(8,128)} %copy.18.wb_ref, f32[16,8,640]{2,1,0:T(8,128)} %maximum_convert_fusion.src_ref), custom_call_target="tpu_custom_call" | custom-call | tf_op jit(solution)/shard_map/pallas_call | solution.py:170
  70.5 1.0 broadcast_multiply_fusion
  71.7 0.7 slice_reduce_fusion
  72.6 8.8 %while.10 = (s32[]{:T(128)}, bf16[8,2,4096]{2,1,0:T(2,128)(2,1)S(1)}, f32[64]{0:T(128)S(1)}, f32[2,64]{1,0:T(2,128)S(1)}, f32[8,4096]{1,0:T(8,128)S(1)}, /*index...) while((s32[]{:T(128)}, ...), condition=%wide.region_2.3_spmd, body=%wide.region_1.2_spmd.sunk | while | flops 10780674 | bytes 264829 | solution.py:74
  72.6 0.9 convolution_bitcast_fusion.2
  73.7 0.9 convolution_bitcast_fusion.2
  74.8 0.9 convolution_bitcast_fusion.2
  75.9 0.9 convolution_bitcast_fusion.2
  77.0 0.9 convolution_bitcast_fusion.2
  78.1 0.9 convolution_bitcast_fusion.2
  79.2 0.9 convolution_bitcast_fusion.2
  80.3 0.9 convolution_bitcast_fusion.2
  81.5 1.3 %collective-permute-start.3 = (bf16[16,8,64]{2,1,0:T(8,128)(2,1)S(1)}, bf16[16,8,64]{2,1,0:T(8,128)(2,1)S(1)}, u32[]{:S(2)}, u32[]{:S(2)}) collective-permute-start(bf16[16,8,64]{2,1,0:T(8,128)(2,1)S(1)} %get-tuple-element.78), channel_id=1, source_target_pairs={{1,0},{3,2},{5,4},{7,6},{9,8},{11,10},{13,12},{15,14},{17,16},{19,... | collective-permute-start | bytes 49160 | tf_op jit(solution)/shard_map/ppermute | solution.py:19
  82.8 3.0 %collective-permute-start.2 = (bf16[16,8,64]{2,1,0:T(8,128)(2,1)S(1)}, bf16[16,8,64]{2,1,0:T(8,128)(2,1)S(1)}, u32[]{:S(2)}, u32[]{:S(2)}) collective-permute-start(bf16[16,8,64]{2,1,0:T(8,128)(2,1)S(1)} %get-tuple-element.77), channel_id=1, source_target_pairs={{0,1},{2,3},{4,5},{6,7},{8,9},{10,11},{12,13},{14,15},{16,17},{18,... | collective-permute-start | bytes 49160 | tf_op jit(solution)/shard_map/ppermute | solution.py:18
  85.9 0.6 add_select_fusion.1.rot_ref
  86.7 0.8 maximum_convert_fusion.1.src_ref
  87.5 5.5 %shard_map.65 = f32[16,8,512]{2,1,0:T(8,128)} custom-call(s32[16,16]{1,0:T(8,128)} %add_select_fusion.1.rot_ref, s32[16,16]{1,0:T(8,128)} %copy-done.1, f32[16,16]{1,0:T(8,128)} %copy-done.2, f32[16,16]{1,0:T(8,128)} %copy-done.3, f32[16,8,640]{2,1,0:T(8,128)} %maximum_convert_fusion.1.src_ref), custom_call_target="tpu_custom_call" | custom-call | tf_op jit(solution)/shard_map/pallas_call | solution.py:170
  93.1 1.1 %reshape.48 = f32[16,4,2,512]{3,2,1,0:T(2,128)S(1)} reshape(f32[16,8,512]{2,1,0:T(8,128)} %shard_map.65) | data formatting | bytes 524288 | tf_op jit(solution)/shard_map/reshape | solution.py:236
  94.2 12.1 %all_to_all.48 = f32[16,4,2,512]{3,2,1,0:T(2,128)S(1)} all-to-all(f32[16,4,2,512]{3,2,1,0:T(2,128)S(1)} %reshape.48), channel_id=1, replica_groups=mesh['views'=4,'depth'=4,'lat'=2] {'depth'}, dimensions={0} | all-to-all | bytes 524288 | tf_op jit(solution)/shard_map/all_to_all | solution.py:237
  106.2 0.9 copy.20
  (79 shorter events, 3.8 us)
Async XLA Ops:
  0.0 51.8 %copy-start = (f32[4,64,512]{2,1,0:T(8,128)S(1)}, f32[4,64,512]{2,1,0:T(8,128)}, u32[]{:S(2)}) copy-start(f32[4,64,512]{2,1,0:T(8,128)} %param.9) | copy-start | bytes 1572868
  1.7 50.9 %all-to-all-start = ((bf16[4,16,2,512]{3,0,2,1:T(4,128)(2,1)}), bf16[4,16,2,512]{3,0,2,1:T(4,128)(2,1)S(1)}, u32[]{:S(2)}, u32[]{:S(2)}) async-start(bf16[4,16,2,512]{3,0,2,1:T(4,128)(2,1)} %dynamic-slice_bitcast_fusion), calls=%async_computation | async-start | bytes 262144 | tf_op jit(solution)/shard_map/all_to_all | solution.py:222
  8.0 0.7 copy-start.6
  8.7 0.7 copy-start.7
  51.8 8.6 %copy-start.4 = (s32[16,16]{0,1:T(8,128)}, s32[16,16]{0,1:T(8,128)S(1)}, u32[]{:S(2)}) copy-start(s32[16,16]{0,1:T(8,128)S(1)} %copy.21) | copy-start | bytes 3076
  52.5 11.5 %all-to-all-start.1 = ((f32[4,4,4,512]{3,2,0,1:T(4,128)}), f32[4,4,4,512]{3,2,0,1:T(4,128)S(1)}, u32[]{:S(2)}, u32[]{:S(2)}) async-start(f32[4,4,4,512]{3,2,0,1:T(4,128)} %copy.22), calls=%async_computation.1 | async-start | bytes 262144 | tf_op jit(solution)/shard_map/all_to_all | solution.py:217
  56.1 8.0 %collective-permute-start.1 = (bf16[16,8,64]{2,1,0:T(8,128)(2,1)S(1)}, bf16[16,8,64]{2,1,0:T(8,128)(2,1)S(1)}, u32[]{:S(2)}, u32[]{:S(2)}) collective-permute-start(bf16[16,8,64]{2,1,0:T(8,128)(2,1)S(1)} %get-tuple-element.80), channel_id=1, source_target_pairs={{1,0},{3,2},{5,4},{7,6},{9,8},{11,10},{13,12},{15,14},{17,16},{19,... | collective-permute-start | bytes 49160 | tf_op jit(solution)/shard_map/ppermute | solution.py:19
  57.4 6.7 %collective-permute-start = (bf16[16,8,64]{2,1,0:T(8,128)(2,1)S(1)}, bf16[16,8,64]{2,1,0:T(8,128)(2,1)S(1)}, u32[]{:S(2)}, u32[]{:S(2)}) collective-permute-start(bf16[16,8,64]{2,1,0:T(8,128)(2,1)S(1)} %get-tuple-element.79), channel_id=1, source_target_pairs={{0,1},{2,3},{4,5},{6,7},{8,9},{10,11},{12,13},{14,15},{16,17},{18,... | collective-permute-start | bytes 49160 | tf_op jit(solution)/shard_map/ppermute | solution.py:18
  61.2 24.7 %copy-start.1 = (s32[16,16]{1,0:T(8,128)}, s32[16,16]{1,0:T(8,128)S(1)}, u32[]{:S(2)}) copy-start(s32[16,16]{1,0:T(8,128)S(1)} %sub.39.thr_ref) | copy-start | bytes 3076
  61.2 0.8 copy-start.2
  61.3 0.7 copy-start.3
  62.0 0.7 copy-start.8
  63.3 0.7 copy-start.5
  81.5 4.9 %collective-permute-start.3 = (bf16[16,8,64]{2,1,0:T(8,128)(2,1)S(1)}, bf16[16,8,64]{2,1,0:T(8,128)(2,1)S(1)}, u32[]{:S(2)}, u32[]{:S(2)}) collective-permute-start(bf16[16,8,64]{2,1,0:T(8,128)(2,1)S(1)} %get-tuple-element.78), channel_id=1, source_target_pairs={{1,0},{3,2},{5,4},{7,6},{9,8},{11,10},{13,12},{15,14},{17,16},{19,... | collective-permute-start | bytes 49160 | tf_op jit(solution)/shard_map/ppermute | solution.py:19
  82.8 3.9 %collective-permute-start.2 = (bf16[16,8,64]{2,1,0:T(8,128)(2,1)S(1)}, bf16[16,8,64]{2,1,0:T(8,128)(2,1)S(1)}, u32[]{:S(2)}, u32[]{:S(2)}) collective-permute-start(bf16[16,8,64]{2,1,0:T(8,128)(2,1)S(1)} %get-tuple-element.77), channel_id=1, source_target_pairs={{0,1},{2,3},{4,5},{6,7},{8,9},{10,11},{12,13},{14,15},{16,17},{18,... | collective-permute-start | bytes 49160 | tf_op jit(solution)/shard_map/ppermute | solution.py:18

commit v2 on v1

--- a/solution.py
+++ b/solution.py
@@ -187,6 +187,7 @@
         and tile_width % LANES == 0
         and 2 * HALO <= LANES
         and tile_width >= HALO
+        and tile_width >= 3 * measured.shape[0] * density.shape[2] * groups
     )
 
 
@@ -205,22 +206,34 @@
     lower_weight = (1.0 - shear_frac).astype(jnp.bfloat16).astype(jnp.float32)
     upper_weight = shear_frac.astype(jnp.bfloat16).astype(jnp.float32)
     table = jnp.stack([shear_shift.astype(jnp.float32), lower_weight, upper_weight])
-    table = lax.all_gather(table, ("views", "depth"), axis=0, tiled=False)
-    table = table.reshape(groups, depth_count, 3, views_here, depth_here)
-    table = jnp.transpose(table, (2, 0, 3, 1, 4)).reshape(3, views_all, depth_all)
+    entries = table.size
+    observed = measured.reshape(views_here, groups, rows_group, tile_width)
+    observed = lax.dynamic_slice_in_dim(observed, slab * rows_here, rows_here, 2)
+    observed = jnp.transpose(observed, (1, 0, 2, 3)).reshape(groups, views_here * rows_here, tile_width)
+    extra = jnp.pad(table.reshape(1, entries), ((0, 0), (0, tile_width - entries)))
+    extra = jnp.broadcast_to(extra[None], (groups, 1, tile_width))
+    observed = jnp.concatenate([observed, extra], axis=1)
+    observed = lax.all_to_all(observed, "views", 0, 0, tiled=True)
+    table = observed[:, views_here * rows_here, :entries].reshape(groups, 3, views_here, depth_here)
+    table = jnp.transpose(table, (1, 0, 2, 3)).reshape(3, views_all, depth_here)
+    observed = observed[:, : views_here * rows_here].reshape(views_all, rows_here, tile_width)
+
+    channels = rows_here * materials
+    mine = lax.dynamic_slice_in_dim(density, group * rows_group, rows_group, 0)
+    mine = mine.reshape(depth_count, rows_here, materials, depth_here, tile_width)
+    mine = jnp.transpose(mine, (0, 3, 1, 2, 4)).reshape(depth_count, depth_here * channels, tile_width)
+    wide = table.size
+    extra = jnp.pad(table.reshape(1, wide), ((0, 0), (0, tile_width - wide))).astype(jnp.bfloat16)
+    extra = jnp.broadcast_to(extra[None], (depth_count, 1, tile_width))
+    mine = jnp.concatenate([mine, extra], axis=1)
+    mine = lax.all_to_all(mine, "depth", 0, 0, tiled=True)
+    table = mine[:, depth_here * channels, :wide].astype(jnp.float32)
+    table = table.reshape(depth_count, 3, views_all, depth_here)
+    table = jnp.transpose(table, (1, 2, 0, 3)).reshape(3, views_all, depth_all)
     shift_all = table[0].astype(jnp.int32)
     lower_all = table[1]
     upper_all = table[2]
-
-    observed = measured.reshape(views_here, groups, rows_group, tile_width)
-    observed = lax.dynamic_slice_in_dim(observed, slab * rows_here, rows_here, 2)
-    observed = lax.all_to_all(observed, "views", 1, 0, tiled=True)
-    observed = observed.reshape(views_all, rows_here, tile_width)
-
-    mine = lax.dynamic_slice_in_dim(density, group * rows_group, rows_group, 0)
-    mine = jnp.transpose(mine, (2, 0, 1, 3))
-    mine = lax.all_to_all(mine, "depth", 1, 0, tiled=True)
-    mine = mine.reshape(depth_all, rows_here * materials, tile_width)
+    mine = mine[:, : depth_here * channels].reshape(depth_all, channels, tile_width)
     padded = with_halo(mine, (("lat", 2),), HALO).astype(jnp.float32)
 
     sums = shear_apply(

time: 108 us -> 74.9 us (0.69)
  blocking collectives: 54.3 us -> 13 us
  waiting for transfers between devices: 0.24 us -> 9.22 us
  starting transfers between devices: 18.3 us -> 16 us
    all_gather x1 -> x0, blocking collectives: 42.2 us -> none  [per_device_rows(): table = lax.all_gather(table, ('views', 'depth'), axis=0, tiled=False)]
    all_to_all x2, waiting for transfers between devices: 0.01 us -> 8.1 us  [the longest x1 4.13 us: per_device_rows(): observed = lax.all_to_all(observed, 'views', 0, 0, tiled=True)]
    ppermute x2, starting transfers between devices: 6.06 us -> 3.34 us  [with_halo(): before = lax.ppermute(last, axis, up)]
    transpose x3 -> x5, local copies, waits for them, and re-layouts: 3 us -> 0.39 us  [the longest x2 0.24 us: per_device_rows(): table = jnp.transpose(table, (1, 2, 0, 3)).reshape(3, views_all, depth_all)]
    ppermute x2, waiting for transfers between devices: 0.01 us -> 1.12 us  [with_halo(): after = lax.ppermute(first, axis, down)]
  transfers between devices with their start and end apart: 6 -> 6, of which waited for: 1 -> 3; matrix products, arithmetic and copies ran while one was open for 4% -> 6% of each run, Pallas kernels for 0% -> 0%
where the time goes in v2:
time: 74.9 us; the launch traced here: 74.2 us
  starting transfers between devices  16 us (21%)
  blocking collectives  13 us (17%)
  Pallas kernels  11.1 us (15%)
  local copies, waits for them, and re-layouts  10.2 us (14%)
  waiting for transfers between devices  9.22 us (12%)
  matrix products  7.39 us (10%)
  other arithmetic  6.14 us (8%)
  between operations  0.91 us (1%)
    all_to_all x1, blocking collectives, per_device_rows(): layers = lax.all_to_all(layers, 'depth', 0, 1, tiled=True)  13 us
    pallas_call x2, Pallas kernels, shear_apply(): pl.pallas_call(shear_kernel, out_shape=jax.ShapeDtypeStruct((inner_count,...  11.1 us
    dot_general x8, matrix products, one_block(): moments = jnp.dot(coefficients, counts, precision=lax.Precision.HIGHEST)  7.39 us
    all_to_all x1, starting transfers between devices, per_device_rows(): observed = lax.all_to_all(observed, 'views', 0, 0, tiled=True)  5.19 us
    all_to_all x1, starting transfers between devices, per_device_rows(): mine = lax.all_to_all(mine, 'depth', 0, 0, tiled=True)  4.87 us
    all_to_all x1, waiting for transfers between devices, per_device_rows(): observed = lax.all_to_all(observed, 'views', 0, 0, tiled=True)  4.13 us
    all_to_all x1, waiting for transfers between devices, per_device_rows(): mine = lax.all_to_all(mine, 'depth', 0, 0, tiled=True)  3.97 us
    ppermute x2, starting transfers between devices, with_halo(): before = lax.ppermute(last, axis, up)  3.34 us
  transfers between devices with their start and end apart: 6, of which 3 were waited for; matrix products, arithmetic and copies ran while one was open for 6% of the time, Pallas kernels for 0%

profile of v2, /device:TPU:0, one launch (start us, length us, event | category | flops | bytes accessed | tf_op | source)
XLA Modules:
  0.0 74.2 jit_solution(2249372631230182499)
XLA Ops:
  0.0 0.7 copy-done.7
  0.7 0.7 copy-done.6
  1.7 0.7 pad_maximum_fusion
  2.4 5.2 %all-to-all-start = ((f32[4,17,512]{2,1,0:T(8,128)}), f32[4,17,512]{2,1,0:T(8,128)S(1)}, u32[]{:S(2)}, u32[]{:S(2)}) async-start(f32[4,17,512]{2,1,0:T(8,128)} %pad_maximum_fusion), calls=%async_computation | async-start | bytes 393216 | tf_op jit(solution)/shard_map/all_to_all | solution.py:216
  7.6 0.9 %constant_dynamic-slice_fusion.3 = bf16[16,2,4,512]{3,2,1,0:T(4,128)(2,1)S(1)} fusion(bf16[64,2,4,512]{3,2,1,0:T(4,128)(2,1)} %param.8, s32[]{:T(128)S(6)} %select_n.17), kind=kLoop, calls=%fused_computation.53 | loop fusion | bytes 262148 | tf_op jit(solution)/shard_map/dynamic_slice | solution.py:222
  8.6 4.1 %all-to-all-done = f32[4,17,512]{2,1,0:T(8,128)S(1)} async-done(((f32[4,17,512]{2,1,0:T(8,128)}), f32[4,17,512]{2,1,0:T(8,128)S(1)}, u32[]{:S(2)}, u32[]{:S(2)}) %all-to-all-start) | async-done | bytes 139296 | tf_op jit(solution)/shard_map/all_to_all | solution.py:216
  13.1 0.7 copy.61
  13.8 4.9 %all-to-all-start.1 = ((bf16[4,33,512]{2,1,0:T(8,128)(2,1)}), bf16[4,33,512]{2,1,0:T(8,128)(2,1)S(1)}, u32[]{:S(2)}, u32[]{:S(2)}) async-start(bf16[4,33,512]{2,1,0:T(8,128)(2,1)} %copy.61), calls=%async_computation.1 | async-start | bytes 327680 | tf_op jit(solution)/shard_map/all_to_all | solution.py:229
  20.7 4.0 %all-to-all-done.1 = bf16[4,33,512]{2,1,0:T(8,128)(2,1)S(1)} async-done(((bf16[4,33,512]{2,1,0:T(8,128)(2,1)}), bf16[4,33,512]{2,1,0:T(8,128)(2,1)S(1)}, u32[]{:S(2)}, u32[]{:S(2)}) %all-to-all-start.1) | async-done | bytes 135200 | tf_op jit(solution)/shard_map/all_to_all | solution.py:229
  25.7 1.3 %collective-permute-start = (bf16[16,8,64]{2,1,0:T(8,128)(2,1)S(1)}, bf16[16,8,64]{2,1,0:T(8,128)(2,1)S(1)}, u32[]{:S(2)}, u32[]{:S(2)}) collective-permute-start(bf16[16,8,64]{2,1,0:T(8,128)(2,1)S(1)} %get-tuple-element.79), channel_id=1, source_target_pairs={{0,1},{2,3},{4,5},{6,7},{8,9},{10,11},{12,13},{14,15},{16,17},{18,... | collective-permute-start | bytes 49160 | tf_op jit(solution)/shard_map/ppermute | solution.py:18
  27.0 1.3 %collective-permute-start.1 = (bf16[16,8,64]{2,1,0:T(8,128)(2,1)S(1)}, bf16[16,8,64]{2,1,0:T(8,128)(2,1)S(1)}, u32[]{:S(2)}, u32[]{:S(2)}) collective-permute-start(bf16[16,8,64]{2,1,0:T(8,128)(2,1)S(1)} %get-tuple-element.80), channel_id=1, source_target_pairs={{1,0},{3,2},{5,4},{7,6},{9,8},{11,10},{13,12},{15,14},{17,16},{19,... | collective-permute-start | bytes 49160 | tf_op jit(solution)/shard_map/ppermute | solution.py:19
  29.0 1.1 %collective-permute-done.1 = bf16[16,8,64]{2,1,0:T(8,128)(2,1)S(1)} collective-permute-done((bf16[16,8,64]{2,1,0:T(8,128)(2,1)S(1)}, bf16[16,8,64]{2,1,0:T(8,128)(2,1)S(1)}, u32[]{:S(2)}, u32[]{:S(2)}) %collective-permute-start.1) | collective-permute-done | bytes 16416 | tf_op jit(solution)/shard_map/ppermute | solution.py:19
  30.1 0.8 %maximum_convert_fusion.src_ref = f32[16,8,640]{2,1,0:T(8,128)} fusion(bf16[16,8,64]{2,1,0:T(8,128)(2,1)S(1)} %collective-permute-done.1, bf16[16,8,512]{2,1,0:T(8,128)(2,1)S(1)} %bitcast.74, bf16[16,8,64]{2,1,0:T(8,128)(2,1)S(1)} %collective-permute-done), kind=kLoop, calls=%fused_computation.23 | loop fusion | flops 491520 | bytes 491520 | tf_op jit(solution)/shard_map/convert_element_type | solution.py:237
  31.0 5.5 %shard_map.64 = f32[16,8,512]{2,1,0:T(8,128)} custom-call(s32[16,16]{1,0:T(8,128)} %add_select_fusion.rot_ref, s32[16,16]{1,0:T(8,128)} %bitcast.83, f32[16,16]{1,0:T(8,128)} %bitcast.84, f32[16,16]{1,0:T(8,128)} %bitcast.86, f32[16,8,640]{2,1,0:T(8,128)} %maximum_convert_fusion.src_ref), custom_call_target="tpu_custom_call" | custom-call | tf_op jit(solution)/shard_map/pallas_call | solution.py:170
  36.5 1.0 %broadcast_multiply_fusion = f32[16,8,512]{2,1,0:T(8,128)S(1)} fusion(f32[16,8,512]{2,1,0:T(8,128)} %shard_map.64), kind=kLoop, calls=%fused_computation.29 | loop fusion | flops 65536 | bytes 524288 | tf_op jit(solution)/shard_map/div | solution.py:242
  37.6 0.7 slice_reduce_fusion
  38.5 8.8 %while.10 = (s32[]{:T(128)}, bf16[8,2,4096]{2,1,0:T(2,128)(2,1)S(1)}, f32[64]{0:T(128)S(1)}, f32[2,64]{1,0:T(2,128)S(1)}, f32[8,4096]{1,0:T(8,128)S(1)}, /*index...) while((s32[]{:T(128)}, ...), condition=%wide.region_2.3_spmd, body=%wide.region_1.2_spmd.sunk | while | flops 10780674 | bytes 264829 | solution.py:74
  38.6 0.9 %convolution_bitcast_fusion.2 = f32[3,4096]{1,0:T(4,128)S(1)} fusion(f32[3,64]{1,0:T(4,128)S(1)} %get-tuple-element.176, f32[4096]{0:T(1024)S(1)} %bitcast.77, f32[64]{0:T(128)S(1)} %get-tuple-element.147, f32[4096]{0:T(1024)S(1)} %bitcast.78, f32[64]{0:T(128)S(1)} %get-tuple-element.149, f32[64]{0:T(128)S(1)} %get-tuple-element.172), kind=kOutput, calls=%fused_computation.clone.1 | convolution fusion | flops 10747904 | bytes 83456 | tf_op jit(solution)/shard_map/while/body/eval_jaxpr/dot_general | solution.py:68
  39.7 0.9 %convolution_bitcast_fusion.2 = f32[3,4096]{1,0:T(4,128)S(1)} fusion(f32[3,64]{1,0:T(4,128)S(1)} %get-tuple-element.176, f32[4096]{0:T(1024)S(1)} %bitcast.77, f32[64]{0:T(128)S(1)} %get-tuple-element.147, f32[4096]{0:T(1024)S(1)} %bitcast.78, f32[64]{0:T(128)S(1)} %get-tuple-element.149, f32[64]{0:T(128)S(1)} %get-tuple-element.172), kind=kOutput, calls=%fused_computation.clone.1 | convolution fusion | flops 10747904 | bytes 83456 | tf_op jit(solution)/shard_map/while/body/eval_jaxpr/dot_general | solution.py:68
  40.8 0.9 %convolution_bitcast_fusion.2 = f32[3,4096]{1,0:T(4,128)S(1)} fusion(f32[3,64]{1,0:T(4,128)S(1)} %get-tuple-element.176, f32[4096]{0:T(1024)S(1)} %bitcast.77, f32[64]{0:T(128)S(1)} %get-tuple-element.147, f32[4096]{0:T(1024)S(1)} %bitcast.78, f32[64]{0:T(128)S(1)} %get-tuple-element.149, f32[64]{0:T(128)S(1)} %get-tuple-element.172), kind=kOutput, calls=%fused_computation.clone.1 | convolution fusion | flops 10747904 | bytes 83456 | tf_op jit(solution)/shard_map/while/body/eval_jaxpr/dot_general | solution.py:68
  41.9 0.9 %convolution_bitcast_fusion.2 = f32[3,4096]{1,0:T(4,128)S(1)} fusion(f32[3,64]{1,0:T(4,128)S(1)} %get-tuple-element.176, f32[4096]{0:T(1024)S(1)} %bitcast.77, f32[64]{0:T(128)S(1)} %get-tuple-element.147, f32[4096]{0:T(1024)S(1)} %bitcast.78, f32[64]{0:T(128)S(1)} %get-tuple-element.149, f32[64]{0:T(128)S(1)} %get-tuple-element.172), kind=kOutput, calls=%fused_computation.clone.1 | convolution fusion | flops 10747904 | bytes 83456 | tf_op jit(solution)/shard_map/while/body/eval_jaxpr/dot_general | solution.py:68
  43.0 0.9 %convolution_bitcast_fusion.2 = f32[3,4096]{1,0:T(4,128)S(1)} fusion(f32[3,64]{1,0:T(4,128)S(1)} %get-tuple-element.176, f32[4096]{0:T(1024)S(1)} %bitcast.77, f32[64]{0:T(128)S(1)} %get-tuple-element.147, f32[4096]{0:T(1024)S(1)} %bitcast.78, f32[64]{0:T(128)S(1)} %get-tuple-element.149, f32[64]{0:T(128)S(1)} %get-tuple-element.172), kind=kOutput, calls=%fused_computation.clone.1 | convolution fusion | flops 10747904 | bytes 83456 | tf_op jit(solution)/shard_map/while/body/eval_jaxpr/dot_general | solution.py:68
  44.1 0.9 %convolution_bitcast_fusion.2 = f32[3,4096]{1,0:T(4,128)S(1)} fusion(f32[3,64]{1,0:T(4,128)S(1)} %get-tuple-element.176, f32[4096]{0:T(1024)S(1)} %bitcast.77, f32[64]{0:T(128)S(1)} %get-tuple-element.147, f32[4096]{0:T(1024)S(1)} %bitcast.78, f32[64]{0:T(128)S(1)} %get-tuple-element.149, f32[64]{0:T(128)S(1)} %get-tuple-element.172), kind=kOutput, calls=%fused_computation.clone.1 | convolution fusion | flops 10747904 | bytes 83456 | tf_op jit(solution)/shard_map/while/body/eval_jaxpr/dot_general | solution.py:68
  45.2 0.9 %convolution_bitcast_fusion.2 = f32[3,4096]{1,0:T(4,128)S(1)} fusion(f32[3,64]{1,0:T(4,128)S(1)} %get-tuple-element.176, f32[4096]{0:T(1024)S(1)} %bitcast.77, f32[64]{0:T(128)S(1)} %get-tuple-element.147, f32[4096]{0:T(1024)S(1)} %bitcast.78, f32[64]{0:T(128)S(1)} %get-tuple-element.149, f32[64]{0:T(128)S(1)} %get-tuple-element.172), kind=kOutput, calls=%fused_computation.clone.1 | convolution fusion | flops 10747904 | bytes 83456 | tf_op jit(solution)/shard_map/while/body/eval_jaxpr/dot_general | solution.py:68
  46.3 0.9 %convolution_bitcast_fusion.2 = f32[3,4096]{1,0:T(4,128)S(1)} fusion(f32[3,64]{1,0:T(4,128)S(1)} %get-tuple-element.176, f32[4096]{0:T(1024)S(1)} %bitcast.77, f32[64]{0:T(128)S(1)} %get-tuple-element.147, f32[4096]{0:T(1024)S(1)} %bitcast.78, f32[64]{0:T(128)S(1)} %get-tuple-element.149, f32[64]{0:T(128)S(1)} %get-tuple-element.172), kind=kOutput, calls=%fused_computation.clone.1 | convolution fusion | flops 10747904 | bytes 83456 | tf_op jit(solution)/shard_map/while/body/eval_jaxpr/dot_general | solution.py:68
  47.5 2.1 %collective-permute-start.2 = (bf16[16,8,64]{2,1,0:T(8,128)(2,1)S(1)}, bf16[16,8,64]{2,1,0:T(8,128)(2,1)S(1)}, u32[]{:S(2)}, u32[]{:S(2)}) collective-permute-start(bf16[16,8,64]{2,1,0:T(8,128)(2,1)S(1)} %get-tuple-element.77), channel_id=1, source_target_pairs={{0,1},{2,3},{4,5},{6,7},{8,9},{10,11},{12,13},{14,15},{16,17},{18,... | collective-permute-start | bytes 49160 | tf_op jit(solution)/shard_map/ppermute | solution.py:18
  49.6 1.3 %collective-permute-start.3 = (bf16[16,8,64]{2,1,0:T(8,128)(2,1)S(1)}, bf16[16,8,64]{2,1,0:T(8,128)(2,1)S(1)}, u32[]{:S(2)}, u32[]{:S(2)}) collective-permute-start(bf16[16,8,64]{2,1,0:T(8,128)(2,1)S(1)} %get-tuple-element.78), channel_id=1, source_target_pairs={{1,0},{3,2},{5,4},{7,6},{9,8},{11,10},{13,12},{15,14},{17,16},{19,... | collective-permute-start | bytes 49160 | tf_op jit(solution)/shard_map/ppermute | solution.py:19
  52.9 0.8 %maximum_convert_fusion.1.src_ref = f32[16,8,640]{2,1,0:T(8,128)} fusion(bf16[16,8,64]{2,1,0:T(8,128)(2,1)S(1)} %collective-permute-done.3, bf16[16,8,512]{2,1,0:T(8,128)(2,1)S(1)} %reshape.67, bf16[16,8,64]{2,1,0:T(8,128)(2,1)S(1)} %collective-permute-done.2), kind=kLoop, calls=%fused_computation.24 | loop fusion | flops 491520 | bytes 491520 | tf_op jit(solution)/shard_map/convert_element_type | solution.py:245
  53.7 5.5 %shard_map.65 = f32[16,8,512]{2,1,0:T(8,128)} custom-call(s32[16,16]{1,0:T(8,128)} %add_select_fusion.1.rot_ref, s32[16,16]{1,0:T(8,128)} %copy-done.2, f32[16,16]{1,0:T(8,128)} %copy.67.wa_ref, f32[16,16]{1,0:T(8,128)} %copy.68.wb_ref, f32[16,8,640]{2,1,0:T(8,128)} %maximum_convert_fusion.1.src_ref), custom_call_target="tpu_custom_call" | custom-call | tf_op jit(solution)/shard_map/pallas_call | solution.py:170
  59.2 1.1 %reshape.68 = f32[16,4,2,512]{3,2,1,0:T(2,128)S(1)} reshape(f32[16,8,512]{2,1,0:T(8,128)} %shard_map.65) | data formatting | bytes 524288 | tf_op jit(solution)/shard_map/reshape | solution.py:249
  60.3 13.0 %all_to_all.28 = f32[16,4,2,512]{3,2,1,0:T(2,128)S(1)} all-to-all(f32[16,4,2,512]{3,2,1,0:T(2,128)S(1)} %reshape.68), channel_id=1, replica_groups=mesh['views'=4,'depth'=4,'lat'=2] {'depth'}, dimensions={0} | all-to-all | bytes 524288 | tf_op jit(solution)/shard_map/all_to_all | solution.py:250
  73.3 0.9 %copy.69 = f32[4,4,4,2,512]{4,1,3,2,0:T(4,128)} copy(f32[4,4,4,2,512]{4,3,2,1,0:T(2,128)S(1)} %bitcast.72) | data formatting | bytes 524288 | tf_op jit(solution)/shard_map/all_to_all | solution.py:250
  (89 shorter events, 7.2 us)
Async XLA Ops:
  0.0 1.5 %copy-start = (f32[4,64,512]{2,1,0:T(8,128)S(1)}, f32[4,64,512]{2,1,0:T(8,128)}, u32[]{:S(2)}) copy-start(f32[4,64,512]{2,1,0:T(8,128)} %param.9) | copy-start | bytes 1572868
  0.0 0.7 copy-start.7
  0.7 0.7 copy-start.6
  2.4 10.4 %all-to-all-start = ((f32[4,17,512]{2,1,0:T(8,128)}), f32[4,17,512]{2,1,0:T(8,128)S(1)}, u32[]{:S(2)}, u32[]{:S(2)}) async-start(f32[4,17,512]{2,1,0:T(8,128)} %pad_maximum_fusion), calls=%async_computation | async-start | bytes 393216 | tf_op jit(solution)/shard_map/all_to_all | solution.py:216
  13.8 10.9 %all-to-all-start.1 = ((bf16[4,33,512]{2,1,0:T(8,128)(2,1)}), bf16[4,33,512]{2,1,0:T(8,128)(2,1)S(1)}, u32[]{:S(2)}, u32[]{:S(2)}) async-start(bf16[4,33,512]{2,1,0:T(8,128)(2,1)} %copy.61), calls=%async_computation.1 | async-start | bytes 327680 | tf_op jit(solution)/shard_map/all_to_all | solution.py:229
  18.7 0.7 copy-start.8
  20.0 0.7 copy-start.5
  25.6 2.7 %copy-start.1 = (s32[1,16,4,4]{1,3,2,0:T(4,128)}, s32[1,16,4,4]{1,3,2,0:T(4,128)S(1)}, u32[]{:S(2)}) copy-start(s32[1,16,4,4]{1,3,2,0:T(4,128)S(1)} %get-tuple-element.81) | copy-start | bytes 3076
  25.7 3.3 %collective-permute-start = (bf16[16,8,64]{2,1,0:T(8,128)(2,1)S(1)}, bf16[16,8,64]{2,1,0:T(8,128)(2,1)S(1)}, u32[]{:S(2)}, u32[]{:S(2)}) collective-permute-start(bf16[16,8,64]{2,1,0:T(8,128)(2,1)S(1)} %get-tuple-element.79), channel_id=1, source_target_pairs={{0,1},{2,3},{4,5},{6,7},{8,9},{10,11},{12,13},{14,15},{16,17},{18,... | collective-permute-start | bytes 49160 | tf_op jit(solution)/shard_map/ppermute | solution.py:18
  27.0 3.1 %collective-permute-start.1 = (bf16[16,8,64]{2,1,0:T(8,128)(2,1)S(1)}, bf16[16,8,64]{2,1,0:T(8,128)(2,1)S(1)}, u32[]{:S(2)}, u32[]{:S(2)}) collective-permute-start(bf16[16,8,64]{2,1,0:T(8,128)(2,1)S(1)} %get-tuple-element.80), channel_id=1, source_target_pairs={{1,0},{3,2},{5,4},{7,6},{9,8},{11,10},{13,12},{15,14},{17,16},{19,... | collective-permute-start | bytes 49160 | tf_op jit(solution)/shard_map/ppermute | solution.py:19
  29.0 21.9 %copy-start.2 = (s32[16,16]{1,0:T(8,128)}, s32[16,16]{1,0:T(8,128)S(1)}, u32[]{:S(2)}) copy-start(s32[16,16]{1,0:T(8,128)S(1)} %copy.63.thr_ref) | copy-start | bytes 3076
  47.5 5.4 %collective-permute-start.2 = (bf16[16,8,64]{2,1,0:T(8,128)(2,1)S(1)}, bf16[16,8,64]{2,1,0:T(8,128)(2,1)S(1)}, u32[]{:S(2)}, u32[]{:S(2)}) collective-permute-start(bf16[16,8,64]{2,1,0:T(8,128)(2,1)S(1)} %get-tuple-element.77), channel_id=1, source_target_pairs={{0,1},{2,3},{4,5},{6,7},{8,9},{10,11},{12,13},{14,15},{16,17},{18,... | collective-permute-start | bytes 49160 | tf_op jit(solution)/shard_map/ppermute | solution.py:18
  49.6 1.9 %copy-start.4 = (f32[1,16,4,4]{1,3,2,0:T(4,128)S(1)}, f32[1,16,4,4]{1,3,2,0:T(4,128)}, u32[]{:S(2)}) copy-start(f32[1,16,4,4]{1,3,2,0:T(4,128)} %get-tuple-element.84) | copy-start | bytes 3076
  49.6 3.3 %collective-permute-start.3 = (bf16[16,8,64]{2,1,0:T(8,128)(2,1)S(1)}, bf16[16,8,64]{2,1,0:T(8,128)(2,1)S(1)}, u32[]{:S(2)}, u32[]{:S(2)}) collective-permute-start(bf16[16,8,64]{2,1,0:T(8,128)(2,1)S(1)} %get-tuple-element.78), channel_id=1, source_target_pairs={{1,0},{3,2},{5,4},{7,6},{9,8},{11,10},{13,12},{15,14},{17,16},{19,... | collective-permute-start | bytes 49160 | tf_op jit(solution)/shard_map/ppermute | solution.py:19
  51.5 0.7 copy-start.3

commit v3 on v2

--- a/solution.py
+++ b/solution.py
@@ -19,6 +19,18 @@
         after = lax.ppermute(first, axis, down)
         x = jnp.concatenate([before, x, after], axis=dim)
     return x
+
+
+def exchange(x, axis):
+    count = lax.axis_size(axis)
+    me = lax.axis_index(axis)
+    result = x
+    for step in range(1, count):
+        pairs = [(i, (i + step) % count) for i in range(count)]
+        part = lax.dynamic_index_in_dim(x, (me + step) % count, 0, keepdims=True)
+        part = lax.ppermute(part, axis, pairs)
+        result = lax.dynamic_update_index_in_dim(result, part, (me - step) % count, 0)
+    return result
 
 
 def band_forward(shear_shift, lower_weight, upper_weight, window, block_width):
@@ -246,9 +258,9 @@
     layers = shear_apply(
         HALO - 1 - shift_all, upper_all, lower_all, padded_grads, tile_width
     )
-    layers = layers.reshape(depth_all, rows_here, materials, tile_width)
-    layers = lax.all_to_all(layers, "depth", 0, 1, tiled=True)
-    return jnp.transpose(layers, (1, 2, 0, 3))
+    layers = layers.reshape(depth_count, depth_here, rows_here, materials, tile_width)
+    layers = exchange(layers, "depth")
+    return jnp.transpose(layers, (0, 2, 3, 1, 4)).reshape(rows_group, materials, depth_here, tile_width)
 
 
 def per_device_any(density, measured, shear_shift, shear_frac, spectrum, attenuation):

time: 74.9 us -> 74.7 us (level)
  blocking collectives: 13 us -> 0 us
  waiting for transfers between devices: 9.22 us -> 17.7 us
  starting transfers between devices: 16 us -> 19.5 us
    all_to_all x1 -> x0, blocking collectives: 13 us -> none  [per_device_rows(): layers = lax.all_to_all(layers, 'depth', 0, 1, tiled=True)]
    ppermute x0 -> x3, waiting for transfers between devices: none -> 9.07 us  [exchange(): part = lax.ppermute(part, axis, pairs)]
    ppermute x0 -> x3, starting transfers between devices: none -> 3.51 us  [exchange(): part = lax.ppermute(part, axis, pairs)]
    transpose x0 -> x1, local copies, waits for them, and re-layouts: none -> 0.87 us  [per_device_rows(): jnp.transpose(layers, (0, 2, 3, 1, 4))]
    all_to_all x1 -> x0, local copies, waits for them, and re-layouts: 0.87 us -> none  [per_device_rows(): layers = lax.all_to_all(layers, 'depth', 0, 1, tiled=True)]
  transfers between devices with their start and end apart: 6 -> 9, of which waited for: 3 -> 5; matrix products, arithmetic and copies ran while one was open for 6% -> 6% of each run, Pallas kernels for 0% -> 0%
where the time goes in v3:
time: 74.7 us; the launch traced here: 74 us
  starting transfers between devices  19.5 us (26%)
  waiting for transfers between devices  17.7 us (24%)
  Pallas kernels  11.1 us (15%)
  local copies, waits for them, and re-layouts  10.9 us (15%)
  matrix products  7.39 us (10%)
  other arithmetic  6.11 us (8%)
  between operations  0.94 us (1%)
    pallas_call x2, Pallas kernels, shear_apply(): pl.pallas_call(shear_kernel, out_shape=jax.ShapeDtypeStruct((inner_count,...  11.1 us
    ppermute x3, waiting for transfers between devices, exchange(): part = lax.ppermute(part, axis, pairs)  9.07 us
    dot_general x8, matrix products, one_block(): moments = jnp.dot(coefficients, counts, precision=lax.Precision.HIGHEST)  7.39 us
    all_to_all x1, starting transfers between devices, per_device_rows(): observed = lax.all_to_all(observed, 'views', 0, 0, tiled=True)  5.19 us
    all_to_all x1, starting transfers between devices, per_device_rows(): mine = lax.all_to_all(mine, 'depth', 0, 0, tiled=True)  4.87 us
    all_to_all x1, waiting for transfers between devices, per_device_rows(): observed = lax.all_to_all(observed, 'views', 0, 0, tiled=True)  4.13 us
    ppermute x3, starting transfers between devices, exchange(): part = lax.ppermute(part, axis, pairs)  3.51 us
    all_to_all x1, waiting for transfers between devices, per_device_rows(): mine = lax.all_to_all(mine, 'depth', 0, 0, tiled=True)  3.41 us
  transfers between devices with their start and end apart: 9, of which 5 were waited for; matrix products, arithmetic and copies ran while one was open for 6% of the time, Pallas kernels for 0%

profile of v3, /device:TPU:0, one launch (start us, length us, event | category | flops | bytes accessed | tf_op | source)
XLA Modules:
  0.0 74.0 jit_solution(12343876864575546615)
XLA Ops:
  0.0 0.7 copy-done.7
  2.4 5.2 %all-to-all-start = ((f32[4,17,512]{2,1,0:T(8,128)}), f32[4,17,512]{2,1,0:T(8,128)S(1)}, u32[]{:S(2)}, u32[]{:S(2)}) async-start(f32[4,17,512]{2,1,0:T(8,128)} %pad_maximum_fusion), calls=%async_computation | async-start | bytes 393216 | tf_op jit(solution)/shard_map/all_to_all | solution.py:228
  7.6 0.9 %constant_dynamic-slice_fusion.6 = bf16[16,2,4,512]{3,2,1,0:T(4,128)(2,1)S(1)} fusion(bf16[64,2,4,512]{3,2,1,0:T(4,128)(2,1)} %param.8, s32[]{:T(128)S(6)} %select_n.63), kind=kLoop, calls=%fused_computation.56 | loop fusion | bytes 262148 | tf_op jit(solution)/shard_map/dynamic_slice | solution.py:234
  8.6 4.1 %all-to-all-done = f32[4,17,512]{2,1,0:T(8,128)S(1)} async-done(((f32[4,17,512]{2,1,0:T(8,128)}), f32[4,17,512]{2,1,0:T(8,128)S(1)}, u32[]{:S(2)}, u32[]{:S(2)}) %all-to-all-start) | async-done | bytes 139296 | tf_op jit(solution)/shard_map/all_to_all | solution.py:228
  13.8 4.9 %all-to-all-start.1 = ((bf16[4,33,512]{2,1,0:T(8,128)(2,1)}), bf16[4,33,512]{2,1,0:T(8,128)(2,1)S(1)}, u32[]{:S(2)}, u32[]{:S(2)}) async-start(bf16[4,33,512]{2,1,0:T(8,128)(2,1)} %copy.61), calls=%async_computation.1 | async-start | bytes 327680 | tf_op jit(solution)/shard_map/all_to_all | solution.py:241
  21.3 3.4 %all-to-all-done.1 = bf16[4,33,512]{2,1,0:T(8,128)(2,1)S(1)} async-done(((bf16[4,33,512]{2,1,0:T(8,128)(2,1)}), bf16[4,33,512]{2,1,0:T(8,128)(2,1)S(1)}, u32[]{:S(2)}, u32[]{:S(2)}) %all-to-all-start.1) | async-done | bytes 135200 | tf_op jit(solution)/shard_map/all_to_all | solution.py:241
  25.7 1.3 %collective-permute-start = (bf16[16,8,64]{2,1,0:T(8,128)(2,1)S(1)}, bf16[16,8,64]{2,1,0:T(8,128)(2,1)S(1)}, u32[]{:S(2)}, u32[]{:S(2)}) collective-permute-start(bf16[16,8,64]{2,1,0:T(8,128)(2,1)S(1)} %get-tuple-element.82), channel_id=1, source_target_pairs={{0,1},{2,3},{4,5},{6,7},{8,9},{10,11},{12,13},{14,15},{16,17},{18,... | collective-permute-start | bytes 49160 | tf_op jit(solution)/shard_map/ppermute | solution.py:18
  27.0 1.3 %collective-permute-start.1 = (bf16[16,8,64]{2,1,0:T(8,128)(2,1)S(1)}, bf16[16,8,64]{2,1,0:T(8,128)(2,1)S(1)}, u32[]{:S(2)}, u32[]{:S(2)}) collective-permute-start(bf16[16,8,64]{2,1,0:T(8,128)(2,1)S(1)} %get-tuple-element.83), channel_id=1, source_target_pairs={{1,0},{3,2},{5,4},{7,6},{9,8},{11,10},{13,12},{15,14},{17,16},{19,... | collective-permute-start | bytes 49160 | tf_op jit(solution)/shard_map/ppermute | solution.py:19
  29.0 1.1 %collective-permute-done.1 = bf16[16,8,64]{2,1,0:T(8,128)(2,1)S(1)} collective-permute-done((bf16[16,8,64]{2,1,0:T(8,128)(2,1)S(1)}, bf16[16,8,64]{2,1,0:T(8,128)(2,1)S(1)}, u32[]{:S(2)}, u32[]{:S(2)}) %collective-permute-start.1) | collective-permute-done | bytes 16416 | tf_op jit(solution)/shard_map/ppermute | solution.py:19
  30.1 0.8 %maximum_convert_fusion.src_ref = f32[16,8,640]{2,1,0:T(8,128)} fusion(bf16[16,8,64]{2,1,0:T(8,128)(2,1)S(1)} %collective-permute-done.1, bf16[16,8,512]{2,1,0:T(8,128)(2,1)S(1)} %bitcast.70, bf16[16,8,64]{2,1,0:T(8,128)(2,1)S(1)} %collective-permute-done), kind=kLoop, calls=%fused_computation.23 | loop fusion | flops 491520 | bytes 491520 | tf_op jit(solution)/shard_map/convert_element_type | solution.py:249
  31.0 5.5 %shard_map.64 = f32[16,8,512]{2,1,0:T(8,128)} custom-call(s32[16,16]{1,0:T(8,128)} %add_select_fusion.rot_ref, s32[16,16]{1,0:T(8,128)} %bitcast.79, f32[16,16]{1,0:T(8,128)} %bitcast.80, f32[16,16]{1,0:T(8,128)} %bitcast.82, f32[16,8,640]{2,1,0:T(8,128)} %maximum_convert_fusion.src_ref), custom_call_target="tpu_custom_call" | custom-call | tf_op jit(solution)/shard_map/pallas_call | solution.py:182
  36.5 1.0 %broadcast_multiply_fusion = f32[16,8,512]{2,1,0:T(8,128)S(1)} fusion(f32[16,8,512]{2,1,0:T(8,128)} %shard_map.64), kind=kLoop, calls=%fused_computation.29 | loop fusion | flops 65536 | bytes 524288 | tf_op jit(solution)/shard_map/div | solution.py:254
  37.6 0.7 slice_reduce_fusion
  38.5 8.8 %while.10 = (s32[]{:T(128)}, bf16[8,2,4096]{2,1,0:T(2,128)(2,1)S(1)}, f32[64]{0:T(128)S(1)}, f32[2,64]{1,0:T(2,128)S(1)}, f32[8,4096]{1,0:T(8,128)S(1)}, /*index...) while((s32[]{:T(128)}, ...), condition=%wide.region_2.3_spmd, body=%wide.region_1.2_spmd.sunk | while | flops 10780674 | bytes 264829 | solution.py:86
  38.6 0.9 %convolution_bitcast_fusion.2 = f32[3,4096]{1,0:T(4,128)S(1)} fusion(f32[3,64]{1,0:T(4,128)S(1)} %get-tuple-element.179, f32[4096]{0:T(1024)S(1)} %bitcast.73, f32[64]{0:T(128)S(1)} %get-tuple-element.150, f32[4096]{0:T(1024)S(1)} %bitcast.74, f32[64]{0:T(128)S(1)} %get-tuple-element.152, f32[64]{0:T(128)S(1)} %get-tuple-element.175), kind=kOutput, calls=%fused_computation.clone.1 | convolution fusion | flops 10747904 | bytes 83456 | tf_op jit(solution)/shard_map/while/body/eval_jaxpr/dot_general | solution.py:80
  39.7 0.9 %convolution_bitcast_fusion.2 = f32[3,4096]{1,0:T(4,128)S(1)} fusion(f32[3,64]{1,0:T(4,128)S(1)} %get-tuple-element.179, f32[4096]{0:T(1024)S(1)} %bitcast.73, f32[64]{0:T(128)S(1)} %get-tuple-element.150, f32[4096]{0:T(1024)S(1)} %bitcast.74, f32[64]{0:T(128)S(1)} %get-tuple-element.152, f32[64]{0:T(128)S(1)} %get-tuple-element.175), kind=kOutput, calls=%fused_computation.clone.1 | convolution fusion | flops 10747904 | bytes 83456 | tf_op jit(solution)/shard_map/while/body/eval_jaxpr/dot_general | solution.py:80
  40.8 0.9 %convolution_bitcast_fusion.2 = f32[3,4096]{1,0:T(4,128)S(1)} fusion(f32[3,64]{1,0:T(4,128)S(1)} %get-tuple-element.179, f32[4096]{0:T(1024)S(1)} %bitcast.73, f32[64]{0:T(128)S(1)} %get-tuple-element.150, f32[4096]{0:T(1024)S(1)} %bitcast.74, f32[64]{0:T(128)S(1)} %get-tuple-element.152, f32[64]{0:T(128)S(1)} %get-tuple-element.175), kind=kOutput, calls=%fused_computation.clone.1 | convolution fusion | flops 10747904 | bytes 83456 | tf_op jit(solution)/shard_map/while/body/eval_jaxpr/dot_general | solution.py:80
  41.9 0.9 %convolution_bitcast_fusion.2 = f32[3,4096]{1,0:T(4,128)S(1)} fusion(f32[3,64]{1,0:T(4,128)S(1)} %get-tuple-element.179, f32[4096]{0:T(1024)S(1)} %bitcast.73, f32[64]{0:T(128)S(1)} %get-tuple-element.150, f32[4096]{0:T(1024)S(1)} %bitcast.74, f32[64]{0:T(128)S(1)} %get-tuple-element.152, f32[64]{0:T(128)S(1)} %get-tuple-element.175), kind=kOutput, calls=%fused_computation.clone.1 | convolution fusion | flops 10747904 | bytes 83456 | tf_op jit(solution)/shard_map/while/body/eval_jaxpr/dot_general | solution.py:80
  43.0 0.9 %convolution_bitcast_fusion.2 = f32[3,4096]{1,0:T(4,128)S(1)} fusion(f32[3,64]{1,0:T(4,128)S(1)} %get-tuple-element.179, f32[4096]{0:T(1024)S(1)} %bitcast.73, f32[64]{0:T(128)S(1)} %get-tuple-element.150, f32[4096]{0:T(1024)S(1)} %bitcast.74, f32[64]{0:T(128)S(1)} %get-tuple-element.152, f32[64]{0:T(128)S(1)} %get-tuple-element.175), kind=kOutput, calls=%fused_computation.clone.1 | convolution fusion | flops 10747904 | bytes 83456 | tf_op jit(solution)/shard_map/while/body/eval_jaxpr/dot_general | solution.py:80
  44.1 0.9 %convolution_bitcast_fusion.2 = f32[3,4096]{1,0:T(4,128)S(1)} fusion(f32[3,64]{1,0:T(4,128)S(1)} %get-tuple-element.179, f32[4096]{0:T(1024)S(1)} %bitcast.73, f32[64]{0:T(128)S(1)} %get-tuple-element.150, f32[4096]{0:T(1024)S(1)} %bitcast.74, f32[64]{0:T(128)S(1)} %get-tuple-element.152, f32[64]{0:T(128)S(1)} %get-tuple-element.175), kind=kOutput, calls=%fused_computation.clone.1 | convolution fusion | flops 10747904 | bytes 83456 | tf_op jit(solution)/shard_map/while/body/eval_jaxpr/dot_general | solution.py:80
  45.2 0.9 %convolution_bitcast_fusion.2 = f32[3,4096]{1,0:T(4,128)S(1)} fusion(f32[3,64]{1,0:T(4,128)S(1)} %get-tuple-element.179, f32[4096]{0:T(1024)S(1)} %bitcast.73, f32[64]{0:T(128)S(1)} %get-tuple-element.150, f32[4096]{0:T(1024)S(1)} %bitcast.74, f32[64]{0:T(128)S(1)} %get-tuple-element.152, f32[64]{0:T(128)S(1)} %get-tuple-element.175), kind=kOutput, calls=%fused_computation.clone.1 | convolution fusion | flops 10747904 | bytes 83456 | tf_op jit(solution)/shard_map/while/body/eval_jaxpr/dot_general | solution.py:80
  46.3 0.9 %convolution_bitcast_fusion.2 = f32[3,4096]{1,0:T(4,128)S(1)} fusion(f32[3,64]{1,0:T(4,128)S(1)} %get-tuple-element.179, f32[4096]{0:T(1024)S(1)} %bitcast.73, f32[64]{0:T(128)S(1)} %get-tuple-element.150, f32[4096]{0:T(1024)S(1)} %bitcast.74, f32[64]{0:T(128)S(1)} %get-tuple-element.152, f32[64]{0:T(128)S(1)} %get-tuple-element.175), kind=kOutput, calls=%fused_computation.clone.1 | convolution fusion | flops 10747904 | bytes 83456 | tf_op jit(solution)/shard_map/while/body/eval_jaxpr/dot_general | solution.py:80
  47.5 2.1 %collective-permute-start.2 = (bf16[16,8,64]{2,1,0:T(8,128)(2,1)S(1)}, bf16[16,8,64]{2,1,0:T(8,128)(2,1)S(1)}, u32[]{:S(2)}, u32[]{:S(2)}) collective-permute-start(bf16[16,8,64]{2,1,0:T(8,128)(2,1)S(1)} %get-tuple-element.80), channel_id=1, source_target_pairs={{0,1},{2,3},{4,5},{6,7},{8,9},{10,11},{12,13},{14,15},{16,17},{18,... | collective-permute-start | bytes 49160 | tf_op jit(solution)/shard_map/ppermute | solution.py:18
  49.6 1.3 %collective-permute-start.3 = (bf16[16,8,64]{2,1,0:T(8,128)(2,1)S(1)}, bf16[16,8,64]{2,1,0:T(8,128)(2,1)S(1)}, u32[]{:S(2)}, u32[]{:S(2)}) collective-permute-start(bf16[16,8,64]{2,1,0:T(8,128)(2,1)S(1)} %get-tuple-element.81), channel_id=1, source_target_pairs={{1,0},{3,2},{5,4},{7,6},{9,8},{11,10},{13,12},{15,14},{17,16},{19,... | collective-permute-start | bytes 49160 | tf_op jit(solution)/shard_map/ppermute | solution.py:19
  52.9 0.8 %maximum_convert_fusion.1.src_ref = f32[16,8,640]{2,1,0:T(8,128)} fusion(bf16[16,8,64]{2,1,0:T(8,128)(2,1)S(1)} %collective-permute-done.3, bf16[16,8,512]{2,1,0:T(8,128)(2,1)S(1)} %reshape.70, bf16[16,8,64]{2,1,0:T(8,128)(2,1)S(1)} %collective-permute-done.2), kind=kLoop, calls=%fused_computation.24 | loop fusion | flops 491520 | bytes 491520 | tf_op jit(solution)/shard_map/convert_element_type | solution.py:257
  53.7 5.5 %shard_map.65 = f32[16,8,512]{2,1,0:T(8,128)} custom-call(s32[16,16]{1,0:T(8,128)} %add_select_fusion.1.rot_ref, s32[16,16]{1,0:T(8,128)} %copy-done.2, f32[16,16]{1,0:T(8,128)} %copy.67.wa_ref, f32[16,16]{1,0:T(8,128)} %copy.68.wb_ref, f32[16,8,640]{2,1,0:T(8,128)} %maximum_convert_fusion.1.src_ref), custom_call_target="tpu_custom_call" | custom-call | tf_op jit(solution)/shard_map/pallas_call | solution.py:182
  59.3 1.1 %reshape.71 = f32[4,4,4,2,512]{4,3,2,1,0:T(2,128)S(1)} reshape(f32[16,8,512]{2,1,0:T(8,128)} %shard_map.65) | data formatting | bytes 524288 | tf_op jit(solution)/shard_map/reshape | solution.py:261
  60.4 1.5 %collective-permute-start.4 = (f32[1,4,4,2,512]{4,3,2,1,0:T(2,128)S(1)}, f32[1,4,4,2,512]{4,3,2,1,0:T(2,128)S(1)}, u32[]{:S(2)}, u32[]{:S(2)}) collective-permute-start(f32[1,4,4,2,512]{4,3,2,1,0:T(2,128)S(1)} %constant_dynamic-slice_fusion.4), channel_id=1, source_target_pairs={{0,2},{2,4},{4,6},{6,0},{1,3},{3,5},{5,7},{7,1},{8,10},{10,12},{12... | collective-permute-start | bytes 196616 | tf_op jit(solution)/shard_map/ppermute | solution.py:31
  61.9 5.2 %collective-permute-done.4 = f32[1,4,4,2,512]{4,3,2,1,0:T(2,128)S(1)} collective-permute-done((f32[1,4,4,2,512]{4,3,2,1,0:T(2,128)S(1)}, f32[1,4,4,2,512]{4,3,2,1,0:T(2,128)S(1)}, u32[]{:S(2)}, u32[]{:S(2)}) %collective-permute-start.4) | collective-permute-done | bytes 65568 | tf_op jit(solution)/shard_map/ppermute | solution.py:31
  67.2 1.9 %collective-permute-start.6 = (f32[1,4,4,2,512]{4,3,2,1,0:T(2,128)S(1)}, f32[1,4,4,2,512]{4,3,2,1,0:T(2,128)S(1)}, u32[]{:S(2)}, u32[]{:S(2)}) collective-permute-start(f32[1,4,4,2,512]{4,3,2,1,0:T(2,128)S(1)} %get-tuple-element.77), channel_id=1, source_target_pairs={{0,6},{2,0},{4,2},{6,4},{1,7},{3,1},{5,3},{7,5},{8,14},{10,8},{12,... | collective-permute-start | bytes 196616 | tf_op jit(solution)/shard_map/ppermute | solution.py:31
  69.2 3.9 %collective-permute-done.5 = f32[1,4,4,2,512]{4,3,2,1,0:T(2,128)S(1)} collective-permute-done((f32[1,4,4,2,512]{4,3,2,1,0:T(2,128)S(1)}, f32[1,4,4,2,512]{4,3,2,1,0:T(2,128)S(1)}, u32[]{:S(2)}, u32[]{:S(2)}) %collective-permute-start.5) | collective-permute-done | bytes 65568 | tf_op jit(solution)/shard_map/ppermute | solution.py:31
  73.1 0.9 %copy.69 = f32[4,4,2,4,512]{4,3,2,1,0:T(4,128)} copy(f32[4,4,2,4,512]{4,2,1,3,0:T(2,128)S(1)} %bitcast.67) | data formatting | bytes 524288 | tf_op jit(solution)/shard_map/transpose | solution.py:263
  (98 shorter events, 10.1 us)
Async XLA Ops:
  0.0 1.5 %copy-start = (f32[4,64,512]{2,1,0:T(8,128)S(1)}, f32[4,64,512]{2,1,0:T(8,128)}, u32[]{:S(2)}) copy-start(f32[4,64,512]{2,1,0:T(8,128)} %param.9) | copy-start | bytes 1572868
  0.0 0.7 %copy-start.7 = (s32[4,4]{1,0:T(4,128)S(1)}, s32[4,4]{1,0:T(4,128)}, u32[]{:S(2)}) copy-start(s32[4,4]{1,0:T(4,128)} %param.10) | copy-start | bytes 196
  0.7 0.7 copy-start.6
  2.4 10.4 %all-to-all-start = ((f32[4,17,512]{2,1,0:T(8,128)}), f32[4,17,512]{2,1,0:T(8,128)S(1)}, u32[]{:S(2)}, u32[]{:S(2)}) async-start(f32[4,17,512]{2,1,0:T(8,128)} %pad_maximum_fusion), calls=%async_computation | async-start | bytes 393216 | tf_op jit(solution)/shard_map/all_to_all | solution.py:228
  13.8 10.9 %all-to-all-start.1 = ((bf16[4,33,512]{2,1,0:T(8,128)(2,1)}), bf16[4,33,512]{2,1,0:T(8,128)(2,1)S(1)}, u32[]{:S(2)}, u32[]{:S(2)}) async-start(bf16[4,33,512]{2,1,0:T(8,128)(2,1)} %copy.61), calls=%async_computation.1 | async-start | bytes 327680 | tf_op jit(solution)/shard_map/all_to_all | solution.py:241
  18.7 0.7 copy-start.8
  20.6 0.7 copy-start.5
  25.6 2.7 %copy-start.1 = (s32[1,16,4,4]{1,3,2,0:T(4,128)}, s32[1,16,4,4]{1,3,2,0:T(4,128)S(1)}, u32[]{:S(2)}) copy-start(s32[1,16,4,4]{1,3,2,0:T(4,128)S(1)} %get-tuple-element.84) | copy-start | bytes 3076
  25.7 3.3 %collective-permute-start = (bf16[16,8,64]{2,1,0:T(8,128)(2,1)S(1)}, bf16[16,8,64]{2,1,0:T(8,128)(2,1)S(1)}, u32[]{:S(2)}, u32[]{:S(2)}) collective-permute-start(bf16[16,8,64]{2,1,0:T(8,128)(2,1)S(1)} %get-tuple-element.82), channel_id=1, source_target_pairs={{0,1},{2,3},{4,5},{6,7},{8,9},{10,11},{12,13},{14,15},{16,17},{18,... | collective-permute-start | bytes 49160 | tf_op jit(solution)/shard_map/ppermute | solution.py:18
  27.0 3.1 %collective-permute-start.1 = (bf16[16,8,64]{2,1,0:T(8,128)(2,1)S(1)}, bf16[16,8,64]{2,1,0:T(8,128)(2,1)S(1)}, u32[]{:S(2)}, u32[]{:S(2)}) collective-permute-start(bf16[16,8,64]{2,1,0:T(8,128)(2,1)S(1)} %get-tuple-element.83), channel_id=1, source_target_pairs={{1,0},{3,2},{5,4},{7,6},{9,8},{11,10},{13,12},{15,14},{17,16},{19,... | collective-permute-start | bytes 49160 | tf_op jit(solution)/shard_map/ppermute | solution.py:19
  29.0 21.9 %copy-start.2 = (s32[16,16]{1,0:T(8,128)}, s32[16,16]{1,0:T(8,128)S(1)}, u32[]{:S(2)}) copy-start(s32[16,16]{1,0:T(8,128)S(1)} %copy.63.thr_ref) | copy-start | bytes 3076
  47.5 5.4 %collective-permute-start.2 = (bf16[16,8,64]{2,1,0:T(8,128)(2,1)S(1)}, bf16[16,8,64]{2,1,0:T(8,128)(2,1)S(1)}, u32[]{:S(2)}, u32[]{:S(2)}) collective-permute-start(bf16[16,8,64]{2,1,0:T(8,128)(2,1)S(1)} %get-tuple-element.80), channel_id=1, source_target_pairs={{0,1},{2,3},{4,5},{6,7},{8,9},{10,11},{12,13},{14,15},{16,17},{18,... | collective-permute-start | bytes 49160 | tf_op jit(solution)/shard_map/ppermute | solution.py:18
  49.6 1.9 %copy-start.4 = (f32[1,16,4,4]{1,3,2,0:T(4,128)S(1)}, f32[1,16,4,4]{1,3,2,0:T(4,128)}, u32[]{:S(2)}) copy-start(f32[1,16,4,4]{1,3,2,0:T(4,128)} %get-tuple-element.87) | copy-start | bytes 3076
  49.6 3.3 %collective-permute-start.3 = (bf16[16,8,64]{2,1,0:T(8,128)(2,1)S(1)}, bf16[16,8,64]{2,1,0:T(8,128)(2,1)S(1)}, u32[]{:S(2)}, u32[]{:S(2)}) collective-permute-start(bf16[16,8,64]{2,1,0:T(8,128)(2,1)S(1)} %get-tuple-element.81), channel_id=1, source_target_pairs={{1,0},{3,2},{5,4},{7,6},{9,8},{11,10},{13,12},{15,14},{17,16},{19,... | collective-permute-start | bytes 49160 | tf_op jit(solution)/shard_map/ppermute | solution.py:19
  51.5 0.7 copy-start.3
  60.4 6.7 %collective-permute-start.4 = (f32[1,4,4,2,512]{4,3,2,1,0:T(2,128)S(1)}, f32[1,4,4,2,512]{4,3,2,1,0:T(2,128)S(1)}, u32[]{:S(2)}, u32[]{:S(2)}) collective-permute-start(f32[1,4,4,2,512]{4,3,2,1,0:T(2,128)S(1)} %constant_dynamic-slice_fusion.4), channel_id=1, source_target_pairs={{0,2},{2,4},{4,6},{6,0},{1,3},{3,5},{5,7},{7,1},{8,10},{10,12},{12... | collective-permute-start | bytes 196616 | tf_op jit(solution)/shard_map/ppermute | solution.py:31
  67.1 6.0 %collective-permute-start.5 = (f32[1,4,4,2,512]{4,3,2,1,0:T(2,128)S(1)}, f32[1,4,4,2,512]{4,3,2,1,0:T(2,128)S(1)}, u32[]{:S(2)}, u32[]{:S(2)}) collective-permute-start(f32[1,4,4,2,512]{4,3,2,1,0:T(2,128)S(1)} %get-tuple-element.78), channel_id=1, source_target_pairs={{0,4},{2,6},{4,0},{6,2},{1,5},{3,7},{5,1},{7,3},{8,12},{10,14},{12... | collective-permute-start | bytes 196616 | tf_op jit(solution)/shard_map/ppermute | solution.py:31
  67.2 5.9 %collective-permute-start.6 = (f32[1,4,4,2,512]{4,3,2,1,0:T(2,128)S(1)}, f32[1,4,4,2,512]{4,3,2,1,0:T(2,128)S(1)}, u32[]{:S(2)}, u32[]{:S(2)}) collective-permute-start(f32[1,4,4,2,512]{4,3,2,1,0:T(2,128)S(1)} %get-tuple-element.77), channel_id=1, source_target_pairs={{0,6},{2,0},{4,2},{6,4},{1,7},{3,1},{5,3},{7,5},{8,14},{10,8},{12,... | collective-permute-start | bytes 196616 | tf_op jit(solution)/shard_map/ppermute | solution.py:31

commit v4 on v3

--- a/solution.py
+++ b/solution.py
@@ -263,7 +263,108 @@
     return jnp.transpose(layers, (0, 2, 3, 1, 4)).reshape(rows_group, materials, depth_here, tile_width)
 
 
+def rows_fit_wide(density, measured):
+    rows = density.shape[0]
+    groups = lax.axis_size("views")
+    parts = lax.axis_size("depth") * lax.axis_size("lat")
+    tile_width = density.shape[3]
+    return (
+        rows % groups == 0
+        and (rows // groups) % parts == 0
+        and tile_width % LANES == 0
+        and 2 * HALO <= LANES
+        and tile_width >= HALO
+        and tile_width >= 3 * measured.shape[0] * density.shape[2] * groups
+    )
+
+
+def stack_halves(values, halves, tile_width):
+    count, rows, materials, _ = values.shape
+    padded = jnp.pad(values, ((0, 0), (0, 0), (0, 0), (HALO, HALO)))
+    parts = [
+        padded[..., h * tile_width : h * tile_width + tile_width + 2 * HALO] for h in range(halves)
+    ]
+    return jnp.stack(parts, axis=1).reshape(count, halves * rows * materials, tile_width + 2 * HALO)
+
+
+def join_halves(values, halves, rows, materials):
+    count, _, tile_width = values.shape
+    values = values.reshape(count, halves, rows, materials, tile_width)
+    return jnp.transpose(values, (0, 2, 3, 1, 4)).reshape(count, rows, materials, halves * tile_width)
+
+
+def per_device_wide(density, measured, shear_shift, shear_frac, spectrum, attenuation):
+    row_total, materials, depth_here, tile_width = density.shape
+    groups = lax.axis_size("views")
+    depth_count = lax.axis_size("depth")
+    halves = lax.axis_size("lat")
+    parts = depth_count * halves
+    views_here = measured.shape[0]
+    views_all = views_here * groups
+    depth_all = depth_here * depth_count
+    rows_group = row_total // groups
+    rows_here = rows_group // parts
+    group = lax.axis_index("views")
+    slab = lax.axis_index("depth")
+    half = lax.axis_index("lat")
+
+    lower_weight = (1.0 - shear_frac).astype(jnp.bfloat16).astype(jnp.float32)
+    upper_weight = shear_frac.astype(jnp.bfloat16).astype(jnp.float32)
+    table = jnp.stack([shear_shift.astype(jnp.float32), lower_weight, upper_weight])
+    entries = table.size
+    observed = measured.reshape(views_here, groups, depth_count, halves, rows_here, tile_width)
+    observed = lax.dynamic_index_in_dim(observed, slab, 2, keepdims=False)
+    observed = jnp.transpose(observed, (1, 2, 0, 3, 4)).reshape(
+        groups * halves, views_here * rows_here, tile_width
+    )
+    extra = jnp.pad(table.reshape(1, entries), ((0, 0), (0, tile_width - entries)))
+    extra = jnp.broadcast_to(extra[None], (groups * halves, 1, tile_width))
+    observed = jnp.concatenate([observed, extra], axis=1)
+    observed = lax.all_to_all(observed, ("views", "lat"), 0, 0, tiled=True)
+    observed = observed.reshape(groups, halves, views_here * rows_here + 1, tile_width)
+    table = observed[:, 0, views_here * rows_here, :entries].reshape(groups, 3, views_here, depth_here)
+    table = jnp.transpose(table, (1, 0, 2, 3)).reshape(3, views_all, depth_here)
+    observed = observed[:, :, : views_here * rows_here].reshape(groups, halves, views_here, rows_here, tile_width)
+    observed = jnp.transpose(observed, (0, 2, 3, 1, 4)).reshape(views_all, rows_here, halves * tile_width)
+
+    mine = lax.dynamic_slice_in_dim(density, group * rows_group, rows_group, 0)
+    mine = mine.reshape(parts, rows_here * materials * depth_here, tile_width)
+    wide = table.size
+    extra = jnp.pad(table.reshape(1, wide), ((0, 0), (0, tile_width - wide))).astype(jnp.bfloat16)
+    extra = jnp.broadcast_to(extra[None], (parts, 1, tile_width))
+    mine = jnp.concatenate([mine, extra], axis=1)
+    mine = lax.all_to_all(mine, ("depth", "lat"), 0, 0, tiled=True)
+    mine = mine.reshape(depth_count, halves, rows_here * materials * depth_here + 1, tile_width)
+    table = mine[:, 0, rows_here * materials * depth_here, :wide].astype(jnp.float32)
+    table = table.reshape(depth_count, 3, views_all, depth_here)
+    table = jnp.transpose(table, (1, 2, 0, 3)).reshape(3, views_all, depth_all)
+    shift_all = table[0].astype(jnp.int32)
+    lower_all = table[1]
+    upper_all = table[2]
+    mine = mine[:, :, : rows_here * materials * depth_here]
+    mine = mine.reshape(depth_count, halves, rows_here, materials, depth_here, tile_width)
+    mine = jnp.transpose(mine, (0, 4, 2, 3, 1, 5)).reshape(
+        depth_all, rows_here, materials, halves * tile_width
+    )
+    stacked = stack_halves(mine.astype(jnp.float32), halves, tile_width)
+
+    sums = shear_apply((shift_all + HALO).T, lower_all.T, upper_all.T, stacked, tile_width)
+    sums = join_halves(sums, halves, rows_here, materials) / depth_all
+    grads = spectral(sums, observed, spectrum, attenuation, views_all)
+    stacked_grads = stack_halves(grads.astype(jnp.float32), halves, tile_width)
+    layers = shear_apply(HALO - 1 - shift_all, upper_all, lower_all, stacked_grads, tile_width)
+    layers = join_halves(layers, halves, rows_here, materials)
+    layers = layers.reshape(depth_count, depth_here, rows_here, materials, halves, tile_width)
+    layers = jnp.transpose(layers, (0, 4, 2, 3, 1, 5)).reshape(
+        parts, rows_here, materials, depth_here, tile_width
+    )
+    layers = lax.all_to_all(layers, ("depth", "lat"), 0, 0, tiled=True)
+    return layers.reshape(rows_group, materials, depth_here, tile_width)
+
+
 def per_device_any(density, measured, shear_shift, shear_frac, spectrum, attenuation):
+    if rows_fit_wide(density, measured):
+        return per_device_wide(density, measured, shear_shift, shear_frac, spectrum, attenuation)
     if rows_fit(density, measured):
         return per_device_rows(density, measured, shear_shift, shear_frac, spectrum, attenuation)
     return per_device(density, measured, shear_shift, shear_frac, spectrum, attenuation)

time: 74.7 us -> 72.3 us (0.968)
  blocking collectives: 0 us -> 12.1 us
  starting transfers between devices: 19.5 us -> 10.1 us
  waiting for transfers between devices: 17.7 us -> 12.9 us
    all_to_all x0 -> x1, blocking collectives: none -> 12.1 us  [per_device_wide(): layers = lax.all_to_all(layers, ('depth', 'lat'), 0, 0, tiled=True)]
    ppermute x7 -> x0, waiting for transfers between devices: 10.2 us -> none  [the longest x3 9.07 us: exchange(): part = lax.ppermute(part, axis, pairs)]
    ppermute x7 -> x0, starting transfers between devices: 9.43 us -> none  [the longest x3 3.51 us: exchange(): part = lax.ppermute(part, axis, pairs)]
    all_to_all x2, waiting for transfers between devices: 7.54 us -> 12.9 us  [the longest x1 6.8 us: per_device_wide(): observed = lax.all_to_all(observed, ('views', 'lat'), 0, 0, tiled=True)]
    reshape x5 -> x7, local copies, waits for them, and re-layouts: 1.44 us -> 4.45 us  [the longest x2 1.79 us: stack_halves(): jnp.stack(parts, axis=1)]
    convert_element_type x2 -> x0, other arithmetic: 1.69 us -> none  [the longest x1 0.85 us: per_device_rows(): padded_grads = with_halo(grads, (('lat', 2),), HALO).astype(jnp.float32)]
    dynamic_slice x3 -> x1, local copies, waits for them, and re-layouts: 1.02 us -> 0.05 us  [per_device_wide(): mine = lax.dynamic_slice_in_dim(density, group * rows_group, rows_group, 0)]
    unnamed x18 -> x20, local copies, waits for them, and re-layouts: 2.79 us -> 2.92 us
  transfers between devices with their start and end apart: 9 -> 2, of which waited for: 5 -> 2; matrix products, arithmetic and copies ran while one was open for 6% -> 1% of each run, Pallas kernels for 0% -> 0%
where the time goes in v4:
time: 72.3 us; the launch traced here: 71.7 us
  waiting for transfers between devices  12.9 us (18%)
  blocking collectives  12.1 us (17%)
  local copies, waits for them, and re-layouts  11.3 us (16%)
  Pallas kernels  11.1 us (15%)
  starting transfers between devices  10.1 us (14%)
  matrix products  7.39 us (10%)
  other arithmetic  5.57 us (8%)
  between operations  1.01 us (1%)
    all_to_all x1, blocking collectives, per_device_wide(): layers = lax.all_to_all(layers, ('depth', 'lat'), 0, 0, tiled=True)  12.1 us
    pallas_call x2, Pallas kernels, shear_apply(): pl.pallas_call(shear_kernel, out_shape=jax.ShapeDtypeStruct((inner_count,...  11.1 us
    dot_general x8, matrix products, one_block(): moments = jnp.dot(coefficients, counts, precision=lax.Precision.HIGHEST)  7.39 us
    all_to_all x1, waiting for transfers between devices, per_device_wide(): observed = lax.all_to_all(observed, ('views', 'lat'), 0, 0, tiled=True)  6.8 us
    all_to_all x1, waiting for transfers between devices, per_device_wide(): mine = lax.all_to_all(mine, ('depth', 'lat'), 0, 0, tiled=True)  6.08 us
    all_to_all x1, starting transfers between devices, per_device_wide(): observed = lax.all_to_all(observed, ('views', 'lat'), 0, 0, tiled=True)  5.2 us
    all_to_all x1, starting transfers between devices, per_device_wide(): mine = lax.all_to_all(mine, ('depth', 'lat'), 0, 0, tiled=True)  4.88 us
    unnamed x20, local copies, waits for them, and re-layouts  2.92 us
  transfers between devices with their start and end apart: 2, of which 2 were waited for; matrix products, arithmetic and copies ran while one was open for 1% of the time, Pallas kernels for 0%

profile of v4, /device:TPU:0, one launch (start us, length us, event | category | flops | bytes accessed | tf_op | source)
XLA Modules:
  0.0 71.7 jit_solution(12699691602557184548)
XLA Ops:
  0.0 0.7 %copy-done.7 = s32[4,4]{1,0:T(4,128)S(1)} copy-done((s32[4,4]{1,0:T(4,128)S(1)}, s32[4,4]{1,0:T(4,128)}, u32[]{:S(2)}) %copy-start.7) | copy-done | bytes 88
  0.7 0.7 copy-done.6
  1.5 1.4 %reshape.81 = f32[4,4,4,2,2,512]{5,4,3,2,1,0:T(2,128)S(1)} reshape(f32[4,64,512]{2,1,0:T(8,128)} %param.9) | data formatting | bytes 1048576 | tf_op jit(solution)/shard_map/reshape | solution.py:315
  3.0 0.7 %pad_maximum_fusion.2 = f32[8,9,512]{2,1,0:T(8,128)} fusion(f32[8,1,512]{2,1,0:T(1,128)S(1)} %broadcast_in_dim.14, f32[8,8,512]{2,1,0:T(8,128)S(1)} %reshape.82), kind=kLoop, calls=%fused_computation.24 | loop fusion | flops 36864 | bytes 294912 | tf_op jit(solution)/shard_map/concatenate | solution.py:322
  3.8 5.2 %all-to-all-start = ((f32[8,9,512]{2,1,0:T(8,128)}), f32[8,9,512]{2,1,0:T(8,128)S(1)}, u32[]{:S(2)}, u32[]{:S(2)}) async-start(f32[8,9,512]{2,1,0:T(8,128)} %pad_maximum_fusion.2), calls=%async_computation | async-start | bytes 524288 | tf_op jit(solution)/shard_map/all_to_all | solution.py:323
  9.1 6.8 %all-to-all-done = f32[8,9,512]{2,1,0:T(8,128)S(1)} async-done(((f32[8,9,512]{2,1,0:T(8,128)}), f32[8,9,512]{2,1,0:T(8,128)S(1)}, u32[]{:S(2)}, u32[]{:S(2)}) %all-to-all-start) | async-done | bytes 147488 | tf_op jit(solution)/shard_map/all_to_all | solution.py:323
  16.2 0.7 pad_maximum_fusion.3
  16.9 4.9 %all-to-all-start.1 = ((bf16[8,17,512]{2,1,0:T(8,128)(2,1)}), bf16[8,17,512]{2,1,0:T(8,128)(2,1)S(1)}, u32[]{:S(2)}, u32[]{:S(2)}) async-start(bf16[8,17,512]{2,1,0:T(8,128)(2,1)} %pad_maximum_fusion.3), calls=%async_computation.1 | async-start | bytes 393216 | tf_op jit(solution)/shard_map/all_to_all | solution.py:336
  21.8 0.6 copy-done.8
  22.4 0.6 reduce_sum.9
  24.0 6.1 %all-to-all-done.1 = bf16[8,17,512]{2,1,0:T(8,128)(2,1)S(1)} async-done(((bf16[8,17,512]{2,1,0:T(8,128)(2,1)}), bf16[8,17,512]{2,1,0:T(8,128)(2,1)S(1)}, u32[]{:S(2)}, u32[]{:S(2)}) %all-to-all-start.1) | async-done | bytes 139296 | tf_op jit(solution)/shard_map/all_to_all | solution.py:336
  30.8 0.6 add_select_fusion.1.rot_ref
  31.4 0.6 add_select_fusion.rot_ref
  32.0 0.7 copy.93.wa_ref
  32.7 0.7 copy.94.wb_ref
  33.5 0.8 %copy.99.src_ref = f32[16,8,640]{2,1,0:T(8,128)} copy(f32[16,8,640]{2,0,1:T(8,128)S(1)} %bitcast.105) | data formatting | bytes 655360 | tf_op jit(solution)/shard_map/reshape | solution.py:287
  34.3 5.5 %shard_map.64 = f32[16,8,512]{2,1,0:T(8,128)} custom-call(s32[16,16]{1,0:T(8,128)} %add_select_fusion.rot_ref, s32[16,16]{1,0:T(8,128)} %bitcast.122, f32[16,16]{1,0:T(8,128)} %bitcast.124, f32[16,16]{1,0:T(8,128)} %bitcast.126, f32[16,8,640]{2,1,0:T(8,128)} %copy.99.src_ref), custom_call_target="tpu_custom_call" | custom-call | tf_op jit(solution)/shard_map/pallas_call | solution.py:182
  39.9 1.0 %broadcast_multiply_fusion = f32[16,8,512]{2,1,0:T(8,128)S(1)} fusion(f32[16,8,512]{2,1,0:T(8,128)} %shard_map.64), kind=kLoop, calls=%fused_computation.34 | loop fusion | flops 65536 | bytes 524288 | tf_op jit(solution)/shard_map/div | solution.py:352
  41.9 8.8 %while.10 = (s32[]{:T(128)}, bf16[8,2,4096]{2,1,0:T(2,128)(2,1)S(1)}, f32[64]{0:T(128)S(1)}, f32[2,64]{1,0:T(2,128)S(1)}, f32[8,4096]{1,0:T(8,128)S(1)}, /*index...) while((s32[]{:T(128)}, ...), condition=%wide.region_2.3_spmd, body=%wide.region_1.2_spmd.sunk | while | flops 10780674 | bytes 264829 | solution.py:86
  41.9 0.9 %convolution_bitcast_fusion.2 = f32[3,4096]{1,0:T(4,128)S(1)} fusion(f32[3,64]{1,0:T(4,128)S(1)} %get-tuple-element.176, f32[4096]{0:T(1024)S(1)} %bitcast.116, f32[64]{0:T(128)S(1)} %get-tuple-element.147, f32[4096]{0:T(1024)S(1)} %bitcast.117, f32[64]{0:T(128)S(1)} %get-tuple-element.149, f32[64]{0:T(128)S(1)} %get-tuple-element.172), kind=kOutput, calls=%fused_computation.clone.1 | convolution fusion | flops 10747904 | bytes 83456 | tf_op jit(solution)/shard_map/while/body/eval_jaxpr/dot_general | solution.py:80
  43.0 0.9 %convolution_bitcast_fusion.2 = f32[3,4096]{1,0:T(4,128)S(1)} fusion(f32[3,64]{1,0:T(4,128)S(1)} %get-tuple-element.176, f32[4096]{0:T(1024)S(1)} %bitcast.116, f32[64]{0:T(128)S(1)} %get-tuple-element.147, f32[4096]{0:T(1024)S(1)} %bitcast.117, f32[64]{0:T(128)S(1)} %get-tuple-element.149, f32[64]{0:T(128)S(1)} %get-tuple-element.172), kind=kOutput, calls=%fused_computation.clone.1 | convolution fusion | flops 10747904 | bytes 83456 | tf_op jit(solution)/shard_map/while/body/eval_jaxpr/dot_general | solution.py:80
  44.1 0.9 %convolution_bitcast_fusion.2 = f32[3,4096]{1,0:T(4,128)S(1)} fusion(f32[3,64]{1,0:T(4,128)S(1)} %get-tuple-element.176, f32[4096]{0:T(1024)S(1)} %bitcast.116, f32[64]{0:T(128)S(1)} %get-tuple-element.147, f32[4096]{0:T(1024)S(1)} %bitcast.117, f32[64]{0:T(128)S(1)} %get-tuple-element.149, f32[64]{0:T(128)S(1)} %get-tuple-element.172), kind=kOutput, calls=%fused_computation.clone.1 | convolution fusion | flops 10747904 | bytes 83456 | tf_op jit(solution)/shard_map/while/body/eval_jaxpr/dot_general | solution.py:80
  45.2 0.9 %convolution_bitcast_fusion.2 = f32[3,4096]{1,0:T(4,128)S(1)} fusion(f32[3,64]{1,0:T(4,128)S(1)} %get-tuple-element.176, f32[4096]{0:T(1024)S(1)} %bitcast.116, f32[64]{0:T(128)S(1)} %get-tuple-element.147, f32[4096]{0:T(1024)S(1)} %bitcast.117, f32[64]{0:T(128)S(1)} %get-tuple-element.149, f32[64]{0:T(128)S(1)} %get-tuple-element.172), kind=kOutput, calls=%fused_computation.clone.1 | convolution fusion | flops 10747904 | bytes 83456 | tf_op jit(solution)/shard_map/while/body/eval_jaxpr/dot_general | solution.py:80
  46.3 0.9 %convolution_bitcast_fusion.2 = f32[3,4096]{1,0:T(4,128)S(1)} fusion(f32[3,64]{1,0:T(4,128)S(1)} %get-tuple-element.176, f32[4096]{0:T(1024)S(1)} %bitcast.116, f32[64]{0:T(128)S(1)} %get-tuple-element.147, f32[4096]{0:T(1024)S(1)} %bitcast.117, f32[64]{0:T(128)S(1)} %get-tuple-element.149, f32[64]{0:T(128)S(1)} %get-tuple-element.172), kind=kOutput, calls=%fused_computation.clone.1 | convolution fusion | flops 10747904 | bytes 83456 | tf_op jit(solution)/shard_map/while/body/eval_jaxpr/dot_general | solution.py:80
  47.5 0.9 %convolution_bitcast_fusion.2 = f32[3,4096]{1,0:T(4,128)S(1)} fusion(f32[3,64]{1,0:T(4,128)S(1)} %get-tuple-element.176, f32[4096]{0:T(1024)S(1)} %bitcast.116, f32[64]{0:T(128)S(1)} %get-tuple-element.147, f32[4096]{0:T(1024)S(1)} %bitcast.117, f32[64]{0:T(128)S(1)} %get-tuple-element.149, f32[64]{0:T(128)S(1)} %get-tuple-element.172), kind=kOutput, calls=%fused_computation.clone.1 | convolution fusion | flops 10747904 | bytes 83456 | tf_op jit(solution)/shard_map/while/body/eval_jaxpr/dot_general | solution.py:80
  48.6 0.9 %convolution_bitcast_fusion.2 = f32[3,4096]{1,0:T(4,128)S(1)} fusion(f32[3,64]{1,0:T(4,128)S(1)} %get-tuple-element.176, f32[4096]{0:T(1024)S(1)} %bitcast.116, f32[64]{0:T(128)S(1)} %get-tuple-element.147, f32[4096]{0:T(1024)S(1)} %bitcast.117, f32[64]{0:T(128)S(1)} %get-tuple-element.149, f32[64]{0:T(128)S(1)} %get-tuple-element.172), kind=kOutput, calls=%fused_computation.clone.1 | convolution fusion | flops 10747904 | bytes 83456 | tf_op jit(solution)/shard_map/while/body/eval_jaxpr/dot_general | solution.py:80
  49.7 0.9 %convolution_bitcast_fusion.2 = f32[3,4096]{1,0:T(4,128)S(1)} fusion(f32[3,64]{1,0:T(4,128)S(1)} %get-tuple-element.176, f32[4096]{0:T(1024)S(1)} %bitcast.116, f32[64]{0:T(128)S(1)} %get-tuple-element.147, f32[4096]{0:T(1024)S(1)} %bitcast.117, f32[64]{0:T(128)S(1)} %get-tuple-element.149, f32[64]{0:T(128)S(1)} %get-tuple-element.172), kind=kOutput, calls=%fused_computation.clone.1 | convolution fusion | flops 10747904 | bytes 83456 | tf_op jit(solution)/shard_map/while/body/eval_jaxpr/dot_general | solution.py:80
  51.1 1.0 %reshape.88.src_ref = f32[16,8,640]{2,1,0:T(8,128)} reshape(f32[16,2,2,2,640]{4,3,2,1,0:T(2,128)S(1)} %pad_maximum_fusion.1) | data formatting | bytes 655360 | tf_op jit(solution)/shard_map/reshape | solution.py:287
  52.1 5.5 %shard_map.65 = f32[16,8,512]{2,1,0:T(8,128)} custom-call(s32[16,16]{1,0:T(8,128)} %add_select_fusion.1.rot_ref, s32[16,16]{1,0:T(8,128)} %copy-done.2, f32[16,16]{1,0:T(8,128)} %copy.93.wa_ref, f32[16,16]{1,0:T(8,128)} %copy.94.wb_ref, f32[16,8,640]{2,1,0:T(8,128)} %reshape.88.src_ref), custom_call_target="tpu_custom_call" | custom-call | tf_op jit(solution)/shard_map/pallas_call | solution.py:182
  57.6 1.1 %reshape.89 = f32[16,2,2,2,512]{4,3,2,1,0:T(2,128)S(1)} reshape(f32[16,8,512]{2,1,0:T(8,128)} %shard_map.65) | data formatting | bytes 524288 | tf_op jit(solution)/shard_map/reshape | solution.py:292
  58.9 12.1 %all_to_all.15 = f32[8,2,2,4,512]{4,3,2,1,0:T(4,128)S(1)} all-to-all(f32[8,2,2,4,512]{4,3,2,1,0:T(4,128)S(1)} %bitcast.108), channel_id=1, replica_groups=mesh['views'=4,'depth'=4,'lat'=2] {'depth','lat'}, dimensions={0} | all-to-all | bytes 524288 | tf_op jit(solution)/shard_map/all_to_all | solution.py:361
  71.0 0.7 copy.121
  (94 shorter events, 4.3 us)
Async XLA Ops:
  0.0 9.0 %copy-start = (bf16[64,2,4,512]{3,2,1,0:T(4,128)(2,1)S(1)}, bf16[64,2,4,512]{3,2,1,0:T(4,128)(2,1)}, u32[]{:S(2)}) copy-start(bf16[64,2,4,512]{3,2,1,0:T(4,128)(2,1)} %param.8) | copy-start | bytes 1572868
  0.0 0.7 %copy-start.7 = (s32[4,4]{1,0:T(4,128)S(1)}, s32[4,4]{1,0:T(4,128)}, u32[]{:S(2)}) copy-start(s32[4,4]{1,0:T(4,128)} %param.10) | copy-start | bytes 196
  0.7 0.7 copy-start.6
  3.8 12.1 %all-to-all-start = ((f32[8,9,512]{2,1,0:T(8,128)}), f32[8,9,512]{2,1,0:T(8,128)S(1)}, u32[]{:S(2)}, u32[]{:S(2)}) async-start(f32[8,9,512]{2,1,0:T(8,128)} %pad_maximum_fusion.2), calls=%async_computation | async-start | bytes 524288 | tf_op jit(solution)/shard_map/all_to_all | solution.py:323
  16.9 13.2 %all-to-all-start.1 = ((bf16[8,17,512]{2,1,0:T(8,128)(2,1)}), bf16[8,17,512]{2,1,0:T(8,128)(2,1)S(1)}, u32[]{:S(2)}, u32[]{:S(2)}) async-start(bf16[8,17,512]{2,1,0:T(8,128)(2,1)} %pad_maximum_fusion.3), calls=%async_computation.1 | async-start | bytes 393216 | tf_op jit(solution)/shard_map/all_to_all | solution.py:336
  21.8 0.7 copy-start.8
  23.0 0.7 copy-start.5
  30.3 1.6 %copy-start.4 = (f32[1,16,4,4]{1,3,2,0:T(4,128)}, f32[1,16,4,4]{1,3,2,0:T(4,128)S(1)}, u32[]{:S(2)}) copy-start(f32[1,16,4,4]{1,3,2,0:T(4,128)S(1)} %get-tuple-element.84) | copy-start | bytes 3076
  30.4 2.3 %copy-start.3 = (f32[1,16,4,4]{1,3,2,0:T(4,128)}, f32[1,16,4,4]{1,3,2,0:T(4,128)S(1)}, u32[]{:S(2)}) copy-start(f32[1,16,4,4]{1,3,2,0:T(4,128)S(1)} %get-tuple-element.83) | copy-start | bytes 3076
  30.4 1.0 %copy-start.1 = (s32[1,16,4,4]{1,3,2,0:T(4,128)}, s32[1,16,4,4]{1,3,2,0:T(4,128)S(1)}, u32[]{:S(2)}) copy-start(s32[1,16,4,4]{1,3,2,0:T(4,128)S(1)} %get-tuple-element.81) | copy-start | bytes 3076
  30.8 0.6 copy-start.2

commit v5 on v4

--- a/solution.py
+++ b/solution.py
@@ -1,3 +1,4 @@
+import functools
 import jax
 import jax.numpy as jnp
 from jax import lax
@@ -172,6 +173,58 @@
     lax.fori_loop(0, outer_count, outer, 0)
 
 
+def shear_table_kernel(forward, tab_ref, src_ref, out_ref):
+    outer_count, channels, width = src_ref.shape
+    inner_count, _, out_width = out_ref.shape
+    pieces = width // LANES
+    out_pieces = out_width // LANES
+    out_ref[...] = jnp.zeros(out_ref.shape, jnp.float32)
+    lane = lax.broadcasted_iota(jnp.int32, (channels, LANES), 1)
+
+    def outer(o, carry):
+        cols = [src_ref[o, :, k * LANES : (k + 1) * LANES] for k in range(pieces)]
+        turned = [pltpu.roll(c, LANES - 1, 1) for c in cols]
+        nexts = [
+            jnp.where(lane < LANES - 1, turned[k], turned[k + 1]) for k in range(pieces - 1)
+        ] + [turned[pieces - 1]]
+        for i in range(inner_count):
+            if forward:
+                shift = tab_ref[0, i, o].astype(jnp.int32)
+                wa = tab_ref[1, i, o]
+                wb = tab_ref[2, i, o]
+                offset = shift + HALO
+            else:
+                shift = tab_ref[0, o, i].astype(jnp.int32)
+                wa = tab_ref[2, o, i]
+                wb = tab_ref[1, o, i]
+                offset = HALO - 1 - shift
+            limit = LANES - offset
+            amount = jnp.where(limit == LANES, 0, limit)
+            mixed = [wa * cols[k] + wb * nexts[k] for k in range(pieces)]
+            rolled = [pltpu.roll(m, amount, 1) for m in mixed]
+            keep = lane < limit
+            for j in range(out_pieces):
+                out_ref[i, :, j * LANES : (j + 1) * LANES] += jnp.where(
+                    keep, rolled[j], rolled[j + 1]
+                )
+        return carry
+
+    lax.fori_loop(0, outer_count, outer, 0)
+
+
+def shear_table(forward, table, src, inner_count, out_width):
+    _, channels, _ = src.shape
+    smem = pl.BlockSpec(memory_space=pltpu.SMEM)
+    vmem = pl.BlockSpec(memory_space=pltpu.VMEM)
+    return pl.pallas_call(
+        functools.partial(shear_table_kernel, forward),
+        out_shape=jax.ShapeDtypeStruct((inner_count, channels, out_width), jnp.float32),
+        in_specs=[smem, vmem],
+        out_specs=vmem,
+        interpret=INTERPRET,
+    )(table, src)
+
+
 def shear_apply(offset, wa, wb, src, out_width):
     outer_count, channels, width = src.shape
     inner_count = offset.shape[1]
@@ -310,49 +363,33 @@
 
     lower_weight = (1.0 - shear_frac).astype(jnp.bfloat16).astype(jnp.float32)
     upper_weight = shear_frac.astype(jnp.bfloat16).astype(jnp.float32)
-    table = jnp.stack([shear_shift.astype(jnp.float32), lower_weight, upper_weight])
-    entries = table.size
+    block = jnp.stack([shear_shift.astype(jnp.float32), lower_weight, upper_weight])
+    table = jnp.zeros((3, views_all, depth_all), jnp.float32)
+    table = lax.dynamic_update_slice(table, block, (0, group * views_here, slab * depth_here))
+    table = lax.psum(table, ("views", "depth"))
     observed = measured.reshape(views_here, groups, depth_count, halves, rows_here, tile_width)
     observed = lax.dynamic_index_in_dim(observed, slab, 2, keepdims=False)
     observed = jnp.transpose(observed, (1, 2, 0, 3, 4)).reshape(
         groups * halves, views_here * rows_here, tile_width
     )
-    extra = jnp.pad(table.reshape(1, entries), ((0, 0), (0, tile_width - entries)))
-    extra = jnp.broadcast_to(extra[None], (groups * halves, 1, tile_width))
-    observed = jnp.concatenate([observed, extra], axis=1)
     observed = lax.all_to_all(observed, ("views", "lat"), 0, 0, tiled=True)
-    observed = observed.reshape(groups, halves, views_here * rows_here + 1, tile_width)
-    table = observed[:, 0, views_here * rows_here, :entries].reshape(groups, 3, views_here, depth_here)
-    table = jnp.transpose(table, (1, 0, 2, 3)).reshape(3, views_all, depth_here)
-    observed = observed[:, :, : views_here * rows_here].reshape(groups, halves, views_here, rows_here, tile_width)
+    observed = observed.reshape(groups, halves, views_here, rows_here, tile_width)
     observed = jnp.transpose(observed, (0, 2, 3, 1, 4)).reshape(views_all, rows_here, halves * tile_width)
 
     mine = lax.dynamic_slice_in_dim(density, group * rows_group, rows_group, 0)
     mine = mine.reshape(parts, rows_here * materials * depth_here, tile_width)
-    wide = table.size
-    extra = jnp.pad(table.reshape(1, wide), ((0, 0), (0, tile_width - wide))).astype(jnp.bfloat16)
-    extra = jnp.broadcast_to(extra[None], (parts, 1, tile_width))
-    mine = jnp.concatenate([mine, extra], axis=1)
     mine = lax.all_to_all(mine, ("depth", "lat"), 0, 0, tiled=True)
-    mine = mine.reshape(depth_count, halves, rows_here * materials * depth_here + 1, tile_width)
-    table = mine[:, 0, rows_here * materials * depth_here, :wide].astype(jnp.float32)
-    table = table.reshape(depth_count, 3, views_all, depth_here)
-    table = jnp.transpose(table, (1, 2, 0, 3)).reshape(3, views_all, depth_all)
-    shift_all = table[0].astype(jnp.int32)
-    lower_all = table[1]
-    upper_all = table[2]
-    mine = mine[:, :, : rows_here * materials * depth_here]
     mine = mine.reshape(depth_count, halves, rows_here, materials, depth_here, tile_width)
     mine = jnp.transpose(mine, (0, 4, 2, 3, 1, 5)).reshape(
         depth_all, rows_here, materials, halves * tile_width
     )
     stacked = stack_halves(mine.astype(jnp.float32), halves, tile_width)
 
-    sums = shear_apply((shift_all + HALO).T, lower_all.T, upper_all.T, stacked, tile_width)
+    sums = shear_table(True, table, stacked, views_all, tile_width)
     sums = join_halves(sums, halves, rows_here, materials) / depth_all
     grads = spectral(sums, observed, spectrum, attenuation, views_all)
     stacked_grads = stack_halves(grads.astype(jnp.float32), halves, tile_width)
-    layers = shear_apply(HALO - 1 - shift_all, upper_all, lower_all, stacked_grads, tile_width)
+    layers = shear_table(False, table, stacked_grads, depth_all, tile_width)
     layers = join_halves(layers, halves, rows_here, materials)
     layers = layers.reshape(depth_count, depth_here, rows_here, materials, halves, tile_width)
     layers = jnp.transpose(layers, (0, 4, 2, 3, 1, 5)).reshape(

time: 72.3 us -> 134 us (1.85)
  blocking collectives: 12.1 us -> 89 us
  waiting for transfers between devices: 12.9 us -> 2 us
  other arithmetic: 5.57 us -> 2.96 us
    psum x0 -> x1, blocking collectives: none -> 76.9 us  [per_device_wide(): table = lax.psum(table, ('views', 'depth'))]
    all_to_all x1, waiting for transfers between devices: 6.08 us -> 0.01 us  [per_device_wide(): mine = lax.all_to_all(mine, ('depth', 'lat'), 0, 0, tiled=True)]
    all_to_all x1, waiting for transfers between devices: 6.8 us -> 2 us  [per_device_wide(): observed = lax.all_to_all(observed, ('views', 'lat'), 0, 0, tiled=True)]
    concatenate x2 -> x0, other arithmetic: 1.44 us -> none  [the longest x1 0.73 us: per_device_wide(): observed = jnp.concatenate([observed, extra], axis=1)]
    unnamed x20 -> x11, local copies, waits for them, and re-layouts: 2.92 us -> 2.06 us
  transfers between devices with their start and end apart: 2 -> 2, of which waited for: 2 -> 1; matrix products, arithmetic and copies ran while one was open for 1% -> 2% of each run, Pallas kernels for 0% -> 0%
where the time goes in v5:
time: 134 us
  blocking collectives  89 us (66%)
  Pallas kernels  10.8 us (8%)
  local copies, waits for them, and re-layouts  10.3 us (8%)
  starting transfers between devices  10.1 us (8%)
  matrix products  7.39 us (6%)
  other arithmetic  2.96 us (2%)
  waiting for transfers between devices  2 us (1%)
    psum x1, blocking collectives, per_device_wide(): table = lax.psum(table, ('views', 'depth'))  76.9 us
    all_to_all x1, blocking collectives, per_device_wide(): layers = lax.all_to_all(layers, ('depth', 'lat'), 0, 0, tiled=True)  12.1 us
    pallas_call x2, Pallas kernels, shear_table(): pl.pallas_call(functools.partial(shear_table_kernel, forward), out_shape=...  10.8 us
    dot_general x8, matrix products, one_block(): moments = jnp.dot(coefficients, counts, precision=lax.Precision.HIGHEST)  7.39 us
    all_to_all x1, starting transfers between devices, per_device_wide(): observed = lax.all_to_all(observed, ('views', 'lat'), 0, 0, tiled=True)  5.2 us
    all_to_all x1, starting transfers between devices, per_device_wide(): mine = lax.all_to_all(mine, ('depth', 'lat'), 0, 0, tiled=True)  4.88 us
  transfers between devices with their start and end apart: 2, of which 1 were waited for; matrix products, arithmetic and copies ran while one was open for 2% of the time, Pallas kernels for 0%

profile of v5, /device:TPU:0, one launch (start us, length us, event | category | flops | bytes accessed | tf_op | source)
XLA Modules:
  0.0 133.8 jit_solution(16466047831780475778)
XLA Ops:
  0.0 1.4 %reshape.47 = f32[4,4,4,2,2,512]{5,4,3,2,1,0:T(2,128)S(1)} reshape(f32[4,64,512]{2,1,0:T(8,128)} %param.9) | data formatting | bytes 1048576 | tf_op jit(solution)/shard_map/reshape | solution.py:370
  1.4 0.7 reshape.48
  2.2 5.2 %all-to-all-start.1 = ((f32[8,8,512]{2,1,0:T(8,128)}), f32[8,8,512]{2,1,0:T(8,128)S(1)}, u32[]{:S(2)}, u32[]{:S(2)}) async-start(f32[8,8,512]{2,1,0:T(8,128)} %reshape.48), calls=%async_computation.1 | async-start | bytes 262144 | tf_op jit(solution)/shard_map/all_to_all | solution.py:375
  7.5 0.7 reshape.45
  8.1 0.7 reduce_sum.9
  9.5 0.7 copy-done.1
  10.2 0.7 copy-done.2
  10.9 2.0 %all-to-all-done.1 = f32[8,8,512]{2,1,0:T(8,128)S(1)} async-done(((f32[8,8,512]{2,1,0:T(8,128)}), f32[8,8,512]{2,1,0:T(8,128)S(1)}, u32[]{:S(2)}, u32[]{:S(2)}) %all-to-all-start.1) | async-done | bytes 131104 | tf_op jit(solution)/shard_map/all_to_all | solution.py:375
  12.9 4.9 %all-to-all-start = ((bf16[8,16,512]{2,1,0:T(8,128)(2,1)}), bf16[8,16,512]{2,1,0:T(8,128)(2,1)S(1)}, u32[]{:S(2)}, u32[]{:S(2)}) async-start(bf16[8,16,512]{2,1,0:T(8,128)(2,1)} %reshape.45), calls=%async_computation | async-start | bytes 262144 | tf_op jit(solution)/shard_map/all_to_all | solution.py:381
  17.8 0.4 dynamic_update_slice.7
  18.2 76.9 %psum.7.tab_ref = f32[3,16,16]{2,1,0:T(8,128)} all-reduce(f32[3,16,16]{2,1,0:T(8,128)S(1)} %dynamic_update_slice.7), channel_id=1, replica_groups=mesh['views'=4,'depth'=4,'lat'=2] {'views','depth'}, use_global_device_ids=true, to_apply=%region_0.0 | all-reduce | flops 768 | bytes 6144 | tf_op jit(solution)/shard_map/psum | solution.py:369
  95.9 0.8 copy.24.src_ref
  96.7 5.4 %shard_map.64 = f32[16,8,512]{2,1,0:T(8,128)} custom-call(f32[3,16,16]{2,1,0:T(8,128)} %psum.7.tab_ref, f32[16,8,640]{2,1,0:T(8,128)} %copy.24.src_ref), custom_call_target="tpu_custom_call" | custom-call | tf_op jit(solution)/shard_map/pallas_call | solution.py:219
  102.1 1.0 broadcast_multiply_fusion
  103.1 0.1 div.21
  103.4 0.2 div.23
  104.1 8.8 %while.10 = (s32[]{:T(128)}, bf16[8,2,4096]{2,1,0:T(2,128)(2,1)S(1)}, f32[64]{0:T(128)S(1)}, f32[2,64]{1,0:T(2,128)S(1)}, f32[8,4096]{1,0:T(8,128)S(1)}, /*index...) while((s32[]{:T(128)}, ...), condition=%wide.region_3.4_spmd, body=%wide.region_2.3_spmd.sunk | while | flops 10780674 | bytes 264821 | solution.py:87
  104.2 0.9 convolution_bitcast_fusion.2
  105.3 0.9 convolution_bitcast_fusion.2
  106.4 0.9 convolution_bitcast_fusion.2
  107.5 0.9 convolution_bitcast_fusion.2
  108.6 0.9 convolution_bitcast_fusion.2
  109.7 0.9 convolution_bitcast_fusion.2
  110.8 0.9 convolution_bitcast_fusion.2
  111.9 0.9 convolution_bitcast_fusion.2
  112.9 0.2 pad_convert_fusion
  113.4 1.0 reshape.50.src_ref
  114.3 5.4 %shard_map.65 = f32[16,8,512]{2,1,0:T(8,128)} custom-call(f32[3,16,16]{2,1,0:T(8,128)} %psum.7.tab_ref, f32[16,8,640]{2,1,0:T(8,128)} %reshape.50.src_ref), custom_call_target="tpu_custom_call" | custom-call | tf_op jit(solution)/shard_map/pallas_call | solution.py:219
  119.7 1.1 reshape.51
  120.8 0.2 copy.23
  121.0 12.1 %all_to_all.15 = f32[8,2,2,4,512]{4,3,2,1,0:T(4,128)S(1)} all-to-all(f32[8,2,2,4,512]{4,3,2,1,0:T(4,128)S(1)} %bitcast.82), channel_id=1, replica_groups=mesh['views'=4,'depth'=4,'lat'=2] {'depth','lat'}, dimensions={0} | all-to-all | bytes 524288 | tf_op jit(solution)/shard_map/all_to_all | solution.py:398
  133.1 0.7 copy.39
  (66 shorter events, 2.7 us)
Async XLA Ops:
  0.0 7.4 %copy-start = (bf16[64,2,4,512]{3,2,1,0:T(4,128)(2,1)S(1)}, bf16[64,2,4,512]{3,2,1,0:T(4,128)(2,1)}, u32[]{:S(2)}) copy-start(bf16[64,2,4,512]{3,2,1,0:T(4,128)(2,1)} %param.8) | copy-start | bytes 1572868
  2.2 10.7 %all-to-all-start.1 = ((f32[8,8,512]{2,1,0:T(8,128)}), f32[8,8,512]{2,1,0:T(8,128)S(1)}, u32[]{:S(2)}, u32[]{:S(2)}) async-start(f32[8,8,512]{2,1,0:T(8,128)} %reshape.48), calls=%async_computation.1 | async-start | bytes 262144 | tf_op jit(solution)/shard_map/all_to_all | solution.py:375
  7.4 0.7 copy-start.4
  9.5 0.7 copy-start.1
  10.2 0.7 copy-start.2
  10.9 6.9 %copy-start.3 = (s32[4,4]{1,0:T(4,128)S(1)}, s32[4,4]{1,0:T(4,128)}, u32[]{:S(2)}) copy-start(s32[4,4]{1,0:T(4,128)} %param.10) | copy-start | bytes 196
  12.9 82.6 %all-to-all-start = ((bf16[8,16,512]{2,1,0:T(8,128)(2,1)}), bf16[8,16,512]{2,1,0:T(8,128)(2,1)S(1)}, u32[]{:S(2)}, u32[]{:S(2)}) async-start(bf16[8,16,512]{2,1,0:T(8,128)(2,1)} %reshape.45), calls=%async_computation | async-start | bytes 262144 | tf_op jit(solution)/shard_map/all_to_all | solution.py:381

commit v6 on v5

--- a/solution.py
+++ b/solution.py
@@ -327,7 +327,8 @@
         and tile_width % LANES == 0
         and 2 * HALO <= LANES
         and tile_width >= HALO
-        and tile_width >= 3 * measured.shape[0] * density.shape[2] * groups
+        and tile_width >= 3 * measured.shape[0] * density.shape[2]
+        and ((rows // groups // parts) * density.shape[1] * density.shape[2]) % groups == 0
     )
 
 
@@ -364,9 +365,7 @@
     lower_weight = (1.0 - shear_frac).astype(jnp.bfloat16).astype(jnp.float32)
     upper_weight = shear_frac.astype(jnp.bfloat16).astype(jnp.float32)
     block = jnp.stack([shear_shift.astype(jnp.float32), lower_weight, upper_weight])
-    table = jnp.zeros((3, views_all, depth_all), jnp.float32)
-    table = lax.dynamic_update_slice(table, block, (0, group * views_here, slab * depth_here))
-    table = lax.psum(table, ("views", "depth"))
+    entries = block.size
     observed = measured.reshape(views_here, groups, depth_count, halves, rows_here, tile_width)
     observed = lax.dynamic_index_in_dim(observed, slab, 2, keepdims=False)
     observed = jnp.transpose(observed, (1, 2, 0, 3, 4)).reshape(
@@ -376,10 +375,23 @@
     observed = observed.reshape(groups, halves, views_here, rows_here, tile_width)
     observed = jnp.transpose(observed, (0, 2, 3, 1, 4)).reshape(views_all, rows_here, halves * tile_width)
 
-    mine = lax.dynamic_slice_in_dim(density, group * rows_group, rows_group, 0)
-    mine = mine.reshape(parts, rows_here * materials * depth_here, tile_width)
-    mine = lax.all_to_all(mine, ("depth", "lat"), 0, 0, tiled=True)
-    mine = mine.reshape(depth_count, halves, rows_here, materials, depth_here, tile_width)
+    chunk = rows_here * materials * depth_here * tile_width
+    piece = chunk // groups
+    mine = density.reshape(groups * parts, groups, piece)
+    mine = lax.dynamic_index_in_dim(mine, group, 1, keepdims=False)
+    mine = mine.reshape(groups * parts, piece // tile_width, tile_width)
+    extra = jnp.pad(block.reshape(1, entries), ((0, 0), (0, tile_width - entries))).astype(jnp.bfloat16)
+    extra = jnp.broadcast_to(extra[None], (groups * parts, 1, tile_width))
+    mine = jnp.concatenate([mine, extra], axis=1)
+    mine = lax.all_to_all(mine, ("views", "depth", "lat"), 0, 0, tiled=True)
+    mine = mine.reshape(groups, depth_count, halves, piece // tile_width + 1, tile_width)
+    table = mine[:, :, 0, piece // tile_width, :entries].astype(jnp.float32)
+    table = table.reshape(groups, depth_count, 3, views_here, depth_here)
+    table = jnp.transpose(table, (2, 0, 3, 1, 4)).reshape(3, views_all, depth_all)
+    mine = mine[:, :, :, : piece // tile_width].reshape(groups, depth_count, halves, piece)
+    mine = jnp.transpose(mine, (1, 2, 0, 3)).reshape(
+        depth_count, halves, rows_here, materials, depth_here, tile_width
+    )
     mine = jnp.transpose(mine, (0, 4, 2, 3, 1, 5)).reshape(
         depth_all, rows_here, materials, halves * tile_width
     )

time: 134 us -> 67.5 us (0.50)
  blocking collectives: 89 us -> 12.4 us
  waiting for transfers between devices: 2 us -> 9.7 us
  local copies, waits for them, and re-layouts: 10.3 us -> 12.1 us
    psum x1 -> x0, blocking collectives: 76.9 us -> none  [per_device_wide(): table = lax.psum(table, ('views', 'depth'))]
    all_to_all x1, waiting for transfers between devices: 0.01 us -> 7.7 us  [per_device_wide(): mine = lax.all_to_all(mine, ('views', 'depth', 'lat'), 0, 0, tiled=True)]
  transfers between devices with their start and end apart: 2 -> 2, of which waited for: 1 -> 2; matrix products, arithmetic and copies ran while one was open for 2% -> 5% of each run, Pallas kernels for 0% -> 0%
where the time goes in v6:
time: 67.5 us; the launch traced here: 67 us
  blocking collectives  12.4 us (18%)
  local copies, waits for them, and re-layouts  12.1 us (18%)
  Pallas kernels  10.8 us (16%)
  waiting for transfers between devices  9.7 us (14%)
  starting transfers between devices  9.52 us (14%)
  matrix products  7.39 us (11%)
  other arithmetic  3.77 us (6%)
  between operations  0.98 us (1%)
    all_to_all x1, blocking collectives, per_device_wide(): layers = lax.all_to_all(layers, ('depth', 'lat'), 0, 0, tiled=True)  12.4 us
    pallas_call x2, Pallas kernels, shear_table(): pl.pallas_call(functools.partial(shear_table_kernel, forward), out_shape=...  10.8 us
    all_to_all x1, waiting for transfers between devices, per_device_wide(): mine = lax.all_to_all(mine, ('views', 'depth', 'lat'), 0, 0, tiled=True)  7.7 us
    dot_general x8, matrix products, one_block(): moments = jnp.dot(coefficients, counts, precision=lax.Precision.HIGHEST)  7.39 us
    all_to_all x1, starting transfers between devices, per_device_wide(): observed = lax.all_to_all(observed, ('views', 'lat'), 0, 0, tiled=True)  5.2 us
    all_to_all x1, starting transfers between devices, per_device_wide(): mine = lax.all_to_all(mine, ('views', 'depth', 'lat'), 0, 0, tiled=True)  4.32 us
    unnamed x11, local copies, waits for them, and re-layouts  2.63 us
    all_to_all x1, waiting for transfers between devices, per_device_wide(): observed = lax.all_to_all(observed, ('views', 'lat'), 0, 0, tiled=True)  2 us
  transfers between devices with their start and end apart: 2, of which 2 were waited for; matrix products, arithmetic and copies ran while one was open for 5% of the time, Pallas kernels for 0%

profile of v6, /device:TPU:0, one launch (start us, length us, event | category | flops | bytes accessed | tf_op | source)
XLA Modules:
  0.0 67.0 jit_solution(17848679796994698884)
XLA Ops:
  0.0 1.3 %reshape.79 = f32[4,4,4,2,2,512]{5,4,3,2,1,0:T(2,128)S(1)} reshape(f32[4,64,512]{2,1,0:T(8,128)} %param.9) | data formatting | bytes 1048576 | tf_op jit(solution)/shard_map/reshape | solution.py:369
  1.4 0.7 %reshape.80 = f32[8,8,512]{2,1,0:T(8,128)} reshape(f32[4,2,4,2,512]{4,3,2,1,0:T(2,128)S(1)} %copy_bitcast_fusion.2) | data formatting | bytes 262144 | tf_op jit(solution)/shard_map/reshape | solution.py:371
  2.1 5.2 %all-to-all-start.1 = ((f32[8,8,512]{2,1,0:T(8,128)}), f32[8,8,512]{2,1,0:T(8,128)S(1)}, u32[]{:S(2)}, u32[]{:S(2)}) async-start(f32[8,8,512]{2,1,0:T(8,128)} %reshape.80), calls=%async_computation.1 | async-start | bytes 262144 | tf_op jit(solution)/shard_map/all_to_all | solution.py:374
  7.3 0.3 reshape.71
  7.7 0.8 %dynamic-slice_reduce_fusion = bf16[32,2048]{1,0:T(8,128)(2,1)S(1)} fusion(bf16[32,4,2048]{2,1,0:T(4,128)(2,1)S(1)} %reshape.71, s32[]{:T(128)S(6)} %select_n.8), kind=kLoop, calls=%fused_computation.26 | loop fusion | bytes 262148 | tf_op jit(solution)/shard_map/jit(dynamic_index_in_dim)/dynamic_slice | solution.py:381
  8.5 0.6 copy-done.3
  9.1 0.7 %copy-done.2 = s32[4,4]{1,0:T(4,128)S(1)} copy-done((s32[4,4]{1,0:T(4,128)S(1)}, s32[4,4]{1,0:T(4,128)}, u32[]{:S(2)}) %copy-start.2) | copy-done | bytes 88
  10.0 0.8 %pad_maximum_fusion.2 = bf16[32,5,512]{2,1,0:T(8,128)(2,1)} fusion(bf16[32,1,512]{2,1,0:T(2,128)(2,1)S(1)} %broadcast_in_dim.10, bf16[32,4,512]{2,1,0:T(4,128)(2,1)S(1)} %reshape.72), kind=kLoop, calls=%fused_computation.24 | loop fusion | flops 327680 | bytes 327680 | tf_op jit(solution)/shard_map/concatenate | solution.py:385
  10.8 2.0 %all-to-all-done.1 = f32[8,8,512]{2,1,0:T(8,128)S(1)} async-done(((f32[8,8,512]{2,1,0:T(8,128)}), f32[8,8,512]{2,1,0:T(8,128)S(1)}, u32[]{:S(2)}, u32[]{:S(2)}) %all-to-all-start.1) | async-done | bytes 131104 | tf_op jit(solution)/shard_map/all_to_all | solution.py:374
  12.8 4.3 %all-to-all-start = ((bf16[32,5,512]{2,1,0:T(8,128)(2,1)}), bf16[32,5,512]{2,1,0:T(8,128)(2,1)S(1)}, u32[]{:S(2)}, u32[]{:S(2)}) async-start(bf16[32,5,512]{2,1,0:T(8,128)(2,1)} %pad_maximum_fusion.2), calls=%async_computation | async-start | bytes 524288 | tf_op jit(solution)/shard_map/all_to_all | solution.py:386
  17.2 0.6 copy-done.4
  17.8 0.6 reduce_sum.9
  19.5 7.7 %all-to-all-done = bf16[32,5,512]{2,1,0:T(8,128)(2,1)S(1)} async-done(((bf16[32,5,512]{2,1,0:T(8,128)(2,1)}), bf16[32,5,512]{2,1,0:T(8,128)(2,1)S(1)}, u32[]{:S(2)}, u32[]{:S(2)}) %all-to-all-start) | async-done | bytes 163872 | tf_op jit(solution)/shard_map/all_to_all | solution.py:386
  27.9 0.8 %copy.33.src_ref = f32[16,8,640]{2,1,0:T(8,128)} copy(f32[16,8,640]{2,0,1:T(8,128)S(1)} %bitcast.82) | data formatting | bytes 655360 | tf_op jit(solution)/shard_map/reshape | solution.py:341
  28.9 0.7 %reshape.87.tab_ref = f32[3,16,16]{2,1,0:T(8,128)} reshape(f32[3,4,4,4,4]{4,3,2,1,0:T(4,128)S(1)} %copy.21) | data formatting | bytes 6144 | tf_op jit(solution)/shard_map/reshape | solution.py:390
  29.6 5.4 %shard_map.64 = f32[16,8,512]{2,1,0:T(8,128)} custom-call(f32[3,16,16]{2,1,0:T(8,128)} %reshape.87.tab_ref, f32[16,8,640]{2,1,0:T(8,128)} %copy.33.src_ref), custom_call_target="tpu_custom_call" | custom-call | tf_op jit(solution)/shard_map/pallas_call | solution.py:219
  35.0 1.0 %broadcast_multiply_fusion = f32[16,8,512]{2,1,0:T(8,128)S(1)} fusion(f32[16,8,512]{2,1,0:T(8,128)} %shard_map.64), kind=kLoop, calls=%fused_computation.35 | loop fusion | flops 65536 | bytes 524288 | tf_op jit(solution)/shard_map/div | solution.py:401
  36.3 0.2 div.23
  37.0 8.8 %while.10 = (s32[]{:T(128)}, bf16[8,2,4096]{2,1,0:T(2,128)(2,1)S(1)}, f32[64]{0:T(128)S(1)}, f32[2,64]{1,0:T(2,128)S(1)}, f32[8,4096]{1,0:T(8,128)S(1)}, /*index...) while((s32[]{:T(128)}, ...), condition=%wide.region_2.3_spmd, body=%wide.region_1.2_spmd.sunk | while | flops 10780674 | bytes 264821 | solution.py:87
  37.1 0.9 %convolution_bitcast_fusion.2 = f32[3,4096]{1,0:T(4,128)S(1)} fusion(f32[3,64]{1,0:T(4,128)S(1)} %get-tuple-element.172, f32[4096]{0:T(1024)S(1)} %bitcast.92, f32[64]{0:T(128)S(1)} %get-tuple-element.143, f32[4096]{0:T(1024)S(1)} %bitcast.93, f32[64]{0:T(128)S(1)} %get-tuple-element.145, f32[64]{0:T(128)S(1)} %get-tuple-element.168), kind=kOutput, calls=%fused_computation.clone.1 | convolution fusion | flops 10747904 | bytes 83456 | tf_op jit(solution)/shard_map/while/body/eval_jaxpr/dot_general | solution.py:81
  38.2 0.9 %convolution_bitcast_fusion.2 = f32[3,4096]{1,0:T(4,128)S(1)} fusion(f32[3,64]{1,0:T(4,128)S(1)} %get-tuple-element.172, f32[4096]{0:T(1024)S(1)} %bitcast.92, f32[64]{0:T(128)S(1)} %get-tuple-element.143, f32[4096]{0:T(1024)S(1)} %bitcast.93, f32[64]{0:T(128)S(1)} %get-tuple-element.145, f32[64]{0:T(128)S(1)} %get-tuple-element.168), kind=kOutput, calls=%fused_computation.clone.1 | convolution fusion | flops 10747904 | bytes 83456 | tf_op jit(solution)/shard_map/while/body/eval_jaxpr/dot_general | solution.py:81
  39.3 0.9 %convolution_bitcast_fusion.2 = f32[3,4096]{1,0:T(4,128)S(1)} fusion(f32[3,64]{1,0:T(4,128)S(1)} %get-tuple-element.172, f32[4096]{0:T(1024)S(1)} %bitcast.92, f32[64]{0:T(128)S(1)} %get-tuple-element.143, f32[4096]{0:T(1024)S(1)} %bitcast.93, f32[64]{0:T(128)S(1)} %get-tuple-element.145, f32[64]{0:T(128)S(1)} %get-tuple-element.168), kind=kOutput, calls=%fused_computation.clone.1 | convolution fusion | flops 10747904 | bytes 83456 | tf_op jit(solution)/shard_map/while/body/eval_jaxpr/dot_general | solution.py:81
  40.4 0.9 %convolution_bitcast_fusion.2 = f32[3,4096]{1,0:T(4,128)S(1)} fusion(f32[3,64]{1,0:T(4,128)S(1)} %get-tuple-element.172, f32[4096]{0:T(1024)S(1)} %bitcast.92, f32[64]{0:T(128)S(1)} %get-tuple-element.143, f32[4096]{0:T(1024)S(1)} %bitcast.93, f32[64]{0:T(128)S(1)} %get-tuple-element.145, f32[64]{0:T(128)S(1)} %get-tuple-element.168), kind=kOutput, calls=%fused_computation.clone.1 | convolution fusion | flops 10747904 | bytes 83456 | tf_op jit(solution)/shard_map/while/body/eval_jaxpr/dot_general | solution.py:81
  41.5 0.9 %convolution_bitcast_fusion.2 = f32[3,4096]{1,0:T(4,128)S(1)} fusion(f32[3,64]{1,0:T(4,128)S(1)} %get-tuple-element.172, f32[4096]{0:T(1024)S(1)} %bitcast.92, f32[64]{0:T(128)S(1)} %get-tuple-element.143, f32[4096]{0:T(1024)S(1)} %bitcast.93, f32[64]{0:T(128)S(1)} %get-tuple-element.145, f32[64]{0:T(128)S(1)} %get-tuple-element.168), kind=kOutput, calls=%fused_computation.clone.1 | convolution fusion | flops 10747904 | bytes 83456 | tf_op jit(solution)/shard_map/while/body/eval_jaxpr/dot_general | solution.py:81
  42.6 0.9 %convolution_bitcast_fusion.2 = f32[3,4096]{1,0:T(4,128)S(1)} fusion(f32[3,64]{1,0:T(4,128)S(1)} %get-tuple-element.172, f32[4096]{0:T(1024)S(1)} %bitcast.92, f32[64]{0:T(128)S(1)} %get-tuple-element.143, f32[4096]{0:T(1024)S(1)} %bitcast.93, f32[64]{0:T(128)S(1)} %get-tuple-element.145, f32[64]{0:T(128)S(1)} %get-tuple-element.168), kind=kOutput, calls=%fused_computation.clone.1 | convolution fusion | flops 10747904 | bytes 83456 | tf_op jit(solution)/shard_map/while/body/eval_jaxpr/dot_general | solution.py:81
  43.7 0.9 %convolution_bitcast_fusion.2 = f32[3,4096]{1,0:T(4,128)S(1)} fusion(f32[3,64]{1,0:T(4,128)S(1)} %get-tuple-element.172, f32[4096]{0:T(1024)S(1)} %bitcast.92, f32[64]{0:T(128)S(1)} %get-tuple-element.143, f32[4096]{0:T(1024)S(1)} %bitcast.93, f32[64]{0:T(128)S(1)} %get-tuple-element.145, f32[64]{0:T(128)S(1)} %get-tuple-element.168), kind=kOutput, calls=%fused_computation.clone.1 | convolution fusion | flops 10747904 | bytes 83456 | tf_op jit(solution)/shard_map/while/body/eval_jaxpr/dot_general | solution.py:81
  44.8 0.9 %convolution_bitcast_fusion.2 = f32[3,4096]{1,0:T(4,128)S(1)} fusion(f32[3,64]{1,0:T(4,128)S(1)} %get-tuple-element.172, f32[4096]{0:T(1024)S(1)} %bitcast.92, f32[64]{0:T(128)S(1)} %get-tuple-element.143, f32[4096]{0:T(1024)S(1)} %bitcast.93, f32[64]{0:T(128)S(1)} %get-tuple-element.145, f32[64]{0:T(128)S(1)} %get-tuple-element.168), kind=kOutput, calls=%fused_computation.clone.1 | convolution fusion | flops 10747904 | bytes 83456 | tf_op jit(solution)/shard_map/while/body/eval_jaxpr/dot_general | solution.py:81
  46.2 1.0 %reshape.82.src_ref = f32[16,8,640]{2,1,0:T(8,128)} reshape(f32[16,2,2,2,640]{4,3,2,1,0:T(2,128)S(1)} %pad_maximum_fusion.1) | data formatting | bytes 655360 | tf_op jit(solution)/shard_map/reshape | solution.py:341
  47.2 5.4 %shard_map.65 = f32[16,8,512]{2,1,0:T(8,128)} custom-call(f32[3,16,16]{2,1,0:T(8,128)} %reshape.87.tab_ref, f32[16,8,640]{2,1,0:T(8,128)} %reshape.82.src_ref), custom_call_target="tpu_custom_call" | custom-call | tf_op jit(solution)/shard_map/pallas_call | solution.py:219
  52.6 1.1 %reshape.83 = f32[16,2,2,2,512]{4,3,2,1,0:T(2,128)S(1)} reshape(f32[16,8,512]{2,1,0:T(8,128)} %shard_map.65) | data formatting | bytes 524288 | tf_op jit(solution)/shard_map/reshape | solution.py:346
  53.9 12.4 %all_to_all.15 = f32[8,2,2,4,512]{4,3,2,1,0:T(4,128)S(1)} all-to-all(f32[8,2,2,4,512]{4,3,2,1,0:T(4,128)S(1)} %bitcast.85), channel_id=1, replica_groups=mesh['views'=4,'depth'=4,'lat'=2] {'depth','lat'}, dimensions={0} | all-to-all | bytes 524288 | tf_op jit(solution)/shard_map/all_to_all | solution.py:410
  66.3 0.7 %copy.52 = f32[16,2,4,512]{3,2,1,0:T(4,128)} copy(f32[16,2,4,512]{3,2,1,0:T(4,128)S(1)} %bitcast.86) | data formatting | bytes 524288
  (76 shorter events, 3.8 us)
Async XLA Ops:
  1.3 6.0 %copy-start = (bf16[64,2,4,512]{3,2,1,0:T(4,128)(2,1)S(1)}, bf16[64,2,4,512]{3,2,1,0:T(4,128)(2,1)}, u32[]{:S(2)}) copy-start(bf16[64,2,4,512]{3,2,1,0:T(4,128)(2,1)} %param.8) | copy-start | bytes 1572868
  2.1 10.7 %all-to-all-start.1 = ((f32[8,8,512]{2,1,0:T(8,128)}), f32[8,8,512]{2,1,0:T(8,128)S(1)}, u32[]{:S(2)}, u32[]{:S(2)}) async-start(f32[8,8,512]{2,1,0:T(8,128)} %reshape.80), calls=%async_computation.1 | async-start | bytes 262144 | tf_op jit(solution)/shard_map/all_to_all | solution.py:374
  8.4 0.7 %copy-start.3 = (f32[4,4]{1,0:T(4,128)S(1)}, f32[4,4]{1,0:T(4,128)}, u32[]{:S(2)}) copy-start(f32[4,4]{1,0:T(4,128)} %param.11) | copy-start | bytes 196
  9.1 0.7 %copy-start.2 = (s32[4,4]{1,0:T(4,128)S(1)}, s32[4,4]{1,0:T(4,128)}, u32[]{:S(2)}) copy-start(s32[4,4]{1,0:T(4,128)} %param.10) | copy-start | bytes 196
  12.8 14.3 %all-to-all-start = ((bf16[32,5,512]{2,1,0:T(8,128)(2,1)}), bf16[32,5,512]{2,1,0:T(8,128)(2,1)S(1)}, u32[]{:S(2)}, u32[]{:S(2)}) async-start(bf16[32,5,512]{2,1,0:T(8,128)(2,1)} %pad_maximum_fusion.2), calls=%async_computation | async-start | bytes 524288 | tf_op jit(solution)/shard_map/all_to_all | solution.py:386
  17.2 0.7 copy-start.4
  18.5 0.7 %copy-start.1 = (f32[2,64]{1,0:T(2,128)S(1)}, f32[2,64]{1,0:T(2,128)}, u32[]{:S(2)}) copy-start(f32[2,64]{1,0:T(2,128)} %param.13) | copy-start | bytes 1540

commit v7 on v6

--- a/solution.py
+++ b/solution.py
@@ -329,6 +329,7 @@
         and tile_width >= HALO
         and tile_width >= 3 * measured.shape[0] * density.shape[2]
         and ((rows // groups // parts) * density.shape[1] * density.shape[2]) % groups == 0
+        and (measured.shape[0] * (rows // groups // parts)) % lax.axis_size("depth") == 0
     )
 
 
@@ -366,36 +367,39 @@
     upper_weight = shear_frac.astype(jnp.bfloat16).astype(jnp.float32)
     block = jnp.stack([shear_shift.astype(jnp.float32), lower_weight, upper_weight])
     entries = block.size
-    observed = measured.reshape(views_here, groups, depth_count, halves, rows_here, tile_width)
-    observed = lax.dynamic_index_in_dim(observed, slab, 2, keepdims=False)
-    observed = jnp.transpose(observed, (1, 2, 0, 3, 4)).reshape(
-        groups * halves, views_here * rows_here, tile_width
-    )
-    observed = lax.all_to_all(observed, ("views", "lat"), 0, 0, tiled=True)
-    observed = observed.reshape(groups, halves, views_here, rows_here, tile_width)
-    observed = jnp.transpose(observed, (0, 2, 3, 1, 4)).reshape(views_all, rows_here, halves * tile_width)
-
+    parts_all = groups * parts
     chunk = rows_here * materials * depth_here * tile_width
     piece = chunk // groups
-    mine = density.reshape(groups * parts, groups, piece)
+    dens_rows = piece // tile_width
+    mine = density.reshape(parts_all, groups, piece)
     mine = lax.dynamic_index_in_dim(mine, group, 1, keepdims=False)
-    mine = mine.reshape(groups * parts, piece // tile_width, tile_width)
-    extra = jnp.pad(block.reshape(1, entries), ((0, 0), (0, tile_width - entries))).astype(jnp.bfloat16)
-    extra = jnp.broadcast_to(extra[None], (groups * parts, 1, tile_width))
-    mine = jnp.concatenate([mine, extra], axis=1)
-    mine = lax.all_to_all(mine, ("views", "depth", "lat"), 0, 0, tiled=True)
-    mine = mine.reshape(groups, depth_count, halves, piece // tile_width + 1, tile_width)
-    table = mine[:, :, 0, piece // tile_width, :entries].astype(jnp.float32)
+    mine = mine.reshape(parts_all, dens_rows, tile_width).astype(jnp.float32)
+    meas_rows = views_here * rows_here // depth_count
+    observed = measured.reshape(views_here, parts_all, rows_here, tile_width)
+    observed = jnp.transpose(observed, (1, 0, 2, 3)).reshape(parts_all, depth_count, meas_rows * tile_width)
+    observed = lax.dynamic_index_in_dim(observed, slab, 1, keepdims=False)
+    observed = observed.reshape(parts_all, meas_rows, tile_width)
+    extra = jnp.pad(block.reshape(1, entries), ((0, 0), (0, tile_width - entries)))
+    extra = jnp.broadcast_to(extra[None], (parts_all, 1, tile_width))
+    packed = jnp.concatenate([mine, observed, extra], axis=1)
+    packed = lax.all_to_all(packed, ("views", "depth", "lat"), 0, 0, tiled=True)
+    packed = packed.reshape(groups, depth_count, halves, dens_rows + meas_rows + 1, tile_width)
+    table = packed[:, :, 0, dens_rows + meas_rows, :entries]
     table = table.reshape(groups, depth_count, 3, views_here, depth_here)
     table = jnp.transpose(table, (2, 0, 3, 1, 4)).reshape(3, views_all, depth_all)
-    mine = mine[:, :, :, : piece // tile_width].reshape(groups, depth_count, halves, piece)
+    observed = packed[:, :, :, dens_rows : dens_rows + meas_rows]
+    observed = jnp.transpose(observed, (0, 2, 1, 3, 4)).reshape(
+        groups, halves, views_here, rows_here, tile_width
+    )
+    observed = jnp.transpose(observed, (0, 2, 3, 1, 4)).reshape(views_all, rows_here, halves * tile_width)
+    mine = packed[:, :, :, :dens_rows].reshape(groups, depth_count, halves, piece)
     mine = jnp.transpose(mine, (1, 2, 0, 3)).reshape(
         depth_count, halves, rows_here, materials, depth_here, tile_width
     )
     mine = jnp.transpose(mine, (0, 4, 2, 3, 1, 5)).reshape(
         depth_all, rows_here, materials, halves * tile_width
     )
-    stacked = stack_halves(mine.astype(jnp.float32), halves, tile_width)
+    stacked = stack_halves(mine, halves, tile_width)
 
     sums = shear_table(True, table, stacked, views_all, tile_width)
     sums = join_halves(sums, halves, rows_here, materials) / depth_all

time: 67.5 us -> 70.4 us (1.043)
  waiting for transfers between devices: 9.7 us -> 14.2 us
  starting transfers between devices: 9.52 us -> 7.33 us
    all_to_all x2 -> x1, waiting for transfers between devices: 9.7 us -> 14.2 us  [per_device_wide(): packed = lax.all_to_all(packed, ('views', 'depth', 'lat'), 0, 0, tiled=True)]
    all_to_all x2 -> x1, starting transfers between devices: 9.52 us -> 7.33 us  [per_device_wide(): packed = lax.all_to_all(packed, ('views', 'depth', 'lat'), 0, 0, tiled=True)]
    unnamed x11 -> x12, local copies, waits for them, and re-layouts: 2.63 us -> 3.46 us
  transfers between devices with their start and end apart: 2 -> 1, of which waited for: 2 -> 1; matrix products, arithmetic and copies ran while one was open for 5% -> 1% of each run, Pallas kernels for 0% -> 0%
where the time goes in v7:
time: 70.4 us; the launch traced here: 69.9 us
  waiting for transfers between devices  14.2 us (20%)
  local copies, waits for them, and re-layouts  12.8 us (18%)
  blocking collectives  12.1 us (17%)
  Pallas kernels  10.8 us (15%)
  matrix products  7.39 us (10%)
  starting transfers between devices  7.33 us (10%)
  other arithmetic  3.85 us (5%)
  between operations  1.03 us (1%)
    all_to_all x1, waiting for transfers between devices, per_device_wide(): packed = lax.all_to_all(packed, ('views', 'depth', 'lat'), 0, 0, tiled=True)  14.2 us
    all_to_all x1, blocking collectives, per_device_wide(): layers = lax.all_to_all(layers, ('depth', 'lat'), 0, 0, tiled=True)  12.1 us
    pallas_call x2, Pallas kernels, shear_table(): pl.pallas_call(functools.partial(shear_table_kernel, forward), out_shape=...  10.8 us
    dot_general x8, matrix products, one_block(): moments = jnp.dot(coefficients, counts, precision=lax.Precision.HIGHEST)  7.39 us
    all_to_all x1, starting transfers between devices, per_device_wide(): packed = lax.all_to_all(packed, ('views', 'depth', 'lat'), 0, 0, tiled=True)  7.33 us
    unnamed x12, local copies, waits for them, and re-layouts  3.46 us
    reshape x2, local copies, waits for them, and re-layouts, stack_halves(): jnp.stack(parts, axis=1)  1.77 us
  transfers between devices with their start and end apart: 1, of which 1 were waited for; matrix products, arithmetic and copies ran while one was open for 1% of the time, Pallas kernels for 0%

profile of v7, /device:TPU:0, one launch (start us, length us, event | category | flops | bytes accessed | tf_op | source)
XLA Modules:
  0.0 69.9 jit_solution(1742026988796396814)
XLA Ops:
  0.0 1.3 %reshape.66 = f32[4,32,2,512]{3,2,1,0:T(2,128)S(1)} reshape(f32[4,64,512]{2,1,0:T(8,128)} %param.9) | data formatting | bytes 1048576 | tf_op jit(solution)/shard_map/reshape | solution.py:378
  1.3 0.5 reshape.67
  2.0 0.9 %copy-done = bf16[64,2,4,512]{3,2,1,0:T(4,128)(2,1)S(1)} copy-done((bf16[64,2,4,512]{3,2,1,0:T(4,128)(2,1)S(1)}, bf16[64,2,4,512]{3,2,1,0:T(4,128)(2,1)}, u32[]{:S(2)}) %copy-start) | copy-done | bytes 524312
  2.9 0.3 reshape.65
  3.2 0.3 constant_dynamic-slice_fusion.3
  3.8 0.5 copy-done.2
  4.3 0.7 copy-done.3
  5.1 1.0 %pad_maximum_fusion = f32[32,7,512]{2,1,0:T(8,128)} fusion(f32[32,1,512]{2,1,0:T(1,128)S(1)} %broadcast_in_dim.10, f32[32,2,512]{2,1,0:T(2,128)S(1)} %reshape.68, f32[32,4,512]{2,1,0:T(4,128)S(1)} %reshape.80), kind=kLoop, calls=%fused_computation.22 | loop fusion | flops 229376 | bytes 917504 | tf_op jit(solution)/shard_map/concatenate | solution.py:384
  6.1 7.3 %all-to-all-start = ((f32[32,7,512]{2,1,0:T(8,128)}), f32[32,7,512]{2,1,0:T(8,128)S(1)}, u32[]{:S(2)}, u32[]{:S(2)}) async-start(f32[32,7,512]{2,1,0:T(8,128)} %pad_maximum_fusion), calls=%async_computation | async-start | bytes 1048576 | tf_op jit(solution)/shard_map/all_to_all | solution.py:385
  13.4 0.6 copy-done.4
  14.1 0.6 reduce_sum.9
  15.4 14.2 %all-to-all-done = f32[32,7,512]{2,1,0:T(8,128)S(1)} async-done(((f32[32,7,512]{2,1,0:T(8,128)}), f32[32,7,512]{2,1,0:T(8,128)S(1)}, u32[]{:S(2)}, u32[]{:S(2)}) %all-to-all-start) | async-done | bytes 458784 | tf_op jit(solution)/shard_map/all_to_all | solution.py:385
  29.8 0.3 reshape.72
  30.1 0.3 reshape.83
  30.9 0.8 %copy.31.src_ref = f32[16,8,640]{2,1,0:T(8,128)} copy(f32[16,8,640]{2,0,1:T(8,128)S(1)} %bitcast.99) | data formatting | bytes 655360 | tf_op jit(solution)/shard_map/reshape | solution.py:342
  31.9 0.7 %reshape.71.tab_ref = f32[3,16,16]{2,1,0:T(8,128)} reshape(f32[3,4,4,4,4]{4,3,2,1,0:T(4,128)S(1)} %copy.17) | data formatting | bytes 6144 | tf_op jit(solution)/shard_map/reshape | solution.py:389
  32.6 5.4 %shard_map.64 = f32[16,8,512]{2,1,0:T(8,128)} custom-call(f32[3,16,16]{2,1,0:T(8,128)} %reshape.71.tab_ref, f32[16,8,640]{2,1,0:T(8,128)} %copy.31.src_ref), custom_call_target="tpu_custom_call" | custom-call | tf_op jit(solution)/shard_map/pallas_call | solution.py:219
  38.0 1.0 %broadcast_multiply_fusion = f32[16,8,512]{2,1,0:T(8,128)S(1)} fusion(f32[16,8,512]{2,1,0:T(8,128)} %shard_map.64), kind=kLoop, calls=%fused_computation.35 | loop fusion | flops 65536 | bytes 524288 | tf_op jit(solution)/shard_map/div | solution.py:405
  40.2 8.8 %while.10 = (s32[]{:T(128)}, bf16[8,2,4096]{2,1,0:T(2,128)(2,1)S(1)}, f32[64]{0:T(128)S(1)}, f32[2,64]{1,0:T(2,128)S(1)}, f32[8,4096]{1,0:T(8,128)S(1)}, /*index...) while((s32[]{:T(128)}, ...), condition=%wide.region_2.3_spmd, body=%wide.region_1.2_spmd.sunk | while | flops 10780674 | bytes 264821 | solution.py:87
  40.3 0.9 %convolution_bitcast_fusion.2 = f32[3,4096]{1,0:T(4,128)S(1)} fusion(f32[3,64]{1,0:T(4,128)S(1)} %get-tuple-element.172, f32[4096]{0:T(1024)S(1)} %bitcast.106, f32[64]{0:T(128)S(1)} %get-tuple-element.143, f32[4096]{0:T(1024)S(1)} %bitcast.107, f32[64]{0:T(128)S(1)} %get-tuple-element.145, f32[64]{0:T(128)S(1)} %get-tuple-element.168), kind=kOutput, calls=%fused_computation.clone.1 | convolution fusion | flops 10747904 | bytes 83456 | tf_op jit(solution)/shard_map/while/body/eval_jaxpr/dot_general | solution.py:81
  41.4 0.9 %convolution_bitcast_fusion.2 = f32[3,4096]{1,0:T(4,128)S(1)} fusion(f32[3,64]{1,0:T(4,128)S(1)} %get-tuple-element.172, f32[4096]{0:T(1024)S(1)} %bitcast.106, f32[64]{0:T(128)S(1)} %get-tuple-element.143, f32[4096]{0:T(1024)S(1)} %bitcast.107, f32[64]{0:T(128)S(1)} %get-tuple-element.145, f32[64]{0:T(128)S(1)} %get-tuple-element.168), kind=kOutput, calls=%fused_computation.clone.1 | convolution fusion | flops 10747904 | bytes 83456 | tf_op jit(solution)/shard_map/while/body/eval_jaxpr/dot_general | solution.py:81
  42.5 0.9 %convolution_bitcast_fusion.2 = f32[3,4096]{1,0:T(4,128)S(1)} fusion(f32[3,64]{1,0:T(4,128)S(1)} %get-tuple-element.172, f32[4096]{0:T(1024)S(1)} %bitcast.106, f32[64]{0:T(128)S(1)} %get-tuple-element.143, f32[4096]{0:T(1024)S(1)} %bitcast.107, f32[64]{0:T(128)S(1)} %get-tuple-element.145, f32[64]{0:T(128)S(1)} %get-tuple-element.168), kind=kOutput, calls=%fused_computation.clone.1 | convolution fusion | flops 10747904 | bytes 83456 | tf_op jit(solution)/shard_map/while/body/eval_jaxpr/dot_general | solution.py:81
  43.6 0.9 %convolution_bitcast_fusion.2 = f32[3,4096]{1,0:T(4,128)S(1)} fusion(f32[3,64]{1,0:T(4,128)S(1)} %get-tuple-element.172, f32[4096]{0:T(1024)S(1)} %bitcast.106, f32[64]{0:T(128)S(1)} %get-tuple-element.143, f32[4096]{0:T(1024)S(1)} %bitcast.107, f32[64]{0:T(128)S(1)} %get-tuple-element.145, f32[64]{0:T(128)S(1)} %get-tuple-element.168), kind=kOutput, calls=%fused_computation.clone.1 | convolution fusion | flops 10747904 | bytes 83456 | tf_op jit(solution)/shard_map/while/body/eval_jaxpr/dot_general | solution.py:81
  44.7 0.9 %convolution_bitcast_fusion.2 = f32[3,4096]{1,0:T(4,128)S(1)} fusion(f32[3,64]{1,0:T(4,128)S(1)} %get-tuple-element.172, f32[4096]{0:T(1024)S(1)} %bitcast.106, f32[64]{0:T(128)S(1)} %get-tuple-element.143, f32[4096]{0:T(1024)S(1)} %bitcast.107, f32[64]{0:T(128)S(1)} %get-tuple-element.145, f32[64]{0:T(128)S(1)} %get-tuple-element.168), kind=kOutput, calls=%fused_computation.clone.1 | convolution fusion | flops 10747904 | bytes 83456 | tf_op jit(solution)/shard_map/while/body/eval_jaxpr/dot_general | solution.py:81
  45.8 0.9 %convolution_bitcast_fusion.2 = f32[3,4096]{1,0:T(4,128)S(1)} fusion(f32[3,64]{1,0:T(4,128)S(1)} %get-tuple-element.172, f32[4096]{0:T(1024)S(1)} %bitcast.106, f32[64]{0:T(128)S(1)} %get-tuple-element.143, f32[4096]{0:T(1024)S(1)} %bitcast.107, f32[64]{0:T(128)S(1)} %get-tuple-element.145, f32[64]{0:T(128)S(1)} %get-tuple-element.168), kind=kOutput, calls=%fused_computation.clone.1 | convolution fusion | flops 10747904 | bytes 83456 | tf_op jit(solution)/shard_map/while/body/eval_jaxpr/dot_general | solution.py:81
  46.9 0.9 %convolution_bitcast_fusion.2 = f32[3,4096]{1,0:T(4,128)S(1)} fusion(f32[3,64]{1,0:T(4,128)S(1)} %get-tuple-element.172, f32[4096]{0:T(1024)S(1)} %bitcast.106, f32[64]{0:T(128)S(1)} %get-tuple-element.143, f32[4096]{0:T(1024)S(1)} %bitcast.107, f32[64]{0:T(128)S(1)} %get-tuple-element.145, f32[64]{0:T(128)S(1)} %get-tuple-element.168), kind=kOutput, calls=%fused_computation.clone.1 | convolution fusion | flops 10747904 | bytes 83456 | tf_op jit(solution)/shard_map/while/body/eval_jaxpr/dot_general | solution.py:81
  48.0 0.9 %convolution_bitcast_fusion.2 = f32[3,4096]{1,0:T(4,128)S(1)} fusion(f32[3,64]{1,0:T(4,128)S(1)} %get-tuple-element.172, f32[4096]{0:T(1024)S(1)} %bitcast.106, f32[64]{0:T(128)S(1)} %get-tuple-element.143, f32[4096]{0:T(1024)S(1)} %bitcast.107, f32[64]{0:T(128)S(1)} %get-tuple-element.145, f32[64]{0:T(128)S(1)} %get-tuple-element.168), kind=kOutput, calls=%fused_computation.clone.1 | convolution fusion | flops 10747904 | bytes 83456 | tf_op jit(solution)/shard_map/while/body/eval_jaxpr/dot_general | solution.py:81
  49.5 0.9 %reshape.76.src_ref = f32[16,8,640]{2,1,0:T(8,128)} reshape(f32[16,2,2,2,640]{4,3,2,1,0:T(2,128)S(1)} %pad_maximum_fusion.2) | data formatting | bytes 655360 | tf_op jit(solution)/shard_map/reshape | solution.py:342
  50.4 5.4 %shard_map.65 = f32[16,8,512]{2,1,0:T(8,128)} custom-call(f32[3,16,16]{2,1,0:T(8,128)} %reshape.71.tab_ref, f32[16,8,640]{2,1,0:T(8,128)} %reshape.76.src_ref), custom_call_target="tpu_custom_call" | custom-call | tf_op jit(solution)/shard_map/pallas_call | solution.py:219
  55.8 1.1 %reshape.77 = f32[16,2,2,2,512]{4,3,2,1,0:T(2,128)S(1)} reshape(f32[16,8,512]{2,1,0:T(8,128)} %shard_map.65) | data formatting | bytes 524288 | tf_op jit(solution)/shard_map/reshape | solution.py:347
  57.1 12.1 %all_to_all.10 = f32[8,2,2,4,512]{4,3,2,1,0:T(4,128)S(1)} all-to-all(f32[8,2,2,4,512]{4,3,2,1,0:T(4,128)S(1)} %bitcast.104), channel_id=1, replica_groups=mesh['views'=4,'depth'=4,'lat'=2] {'depth','lat'}, dimensions={0} | all-to-all | bytes 524288 | tf_op jit(solution)/shard_map/all_to_all | solution.py:414
  69.2 0.7 %copy.50 = f32[16,2,4,512]{3,2,1,0:T(4,128)} copy(f32[16,2,4,512]{3,2,1,0:T(4,128)S(1)} %bitcast.105) | data formatting | bytes 524288
  (73 shorter events, 4.2 us)
Async XLA Ops:
  1.8 1.0 %copy-start = (bf16[64,2,4,512]{3,2,1,0:T(4,128)(2,1)S(1)}, bf16[64,2,4,512]{3,2,1,0:T(4,128)(2,1)}, u32[]{:S(2)}) copy-start(bf16[64,2,4,512]{3,2,1,0:T(4,128)(2,1)} %param.8) | copy-start | bytes 1572868
  3.6 0.7 copy-start.2
  4.3 0.7 copy-start.3
  6.1 23.6 %all-to-all-start = ((f32[32,7,512]{2,1,0:T(8,128)}), f32[32,7,512]{2,1,0:T(8,128)S(1)}, u32[]{:S(2)}, u32[]{:S(2)}) async-start(f32[32,7,512]{2,1,0:T(8,128)} %pad_maximum_fusion), calls=%async_computation | async-start | bytes 1048576 | tf_op jit(solution)/shard_map/all_to_all | solution.py:385
  13.4 0.7 copy-start.4
  14.7 0.7 %copy-start.1 = (f32[2,64]{1,0:T(2,128)S(1)}, f32[2,64]{1,0:T(2,128)}, u32[]{:S(2)}) copy-start(f32[2,64]{1,0:T(2,128)} %param.13) | copy-start | bytes 1540

commit v8 on v6

--- a/solution.py
+++ b/solution.py
@@ -87,6 +87,58 @@
     stacked = lax.map(one_block, (path_water, path_bone, target_flat))
     gradients = jnp.swapaxes(stacked, 0, 1).reshape(materials, view_count, row_count, tile_width)
     return jnp.transpose(gradients, (1, 2, 0, 3))
+
+
+def spectral_kernel(views_all, emitted_ref, spectrum_ref, attenuation_ref, water_ref, bone_ref, target_ref, out0_ref, out1_ref):
+    rows, width = water_ref.shape
+    energies = spectrum_ref.shape[0]
+    block = 8
+
+    def one_block(b, carry):
+        lo = pl.multiple_of(b * block, block)
+        water = water_ref[pl.ds(lo, block), :]
+        bone = bone_ref[pl.ds(lo, block), :]
+
+        def one_energy(e, sums):
+            intensity, first, second = sums
+            a0 = attenuation_ref[0, e]
+            a1 = attenuation_ref[1, e]
+            counts = spectrum_ref[e] * jnp.exp(-(a0 * water + a1 * bone))
+            return (intensity + counts, first + a0 * counts, second + a1 * counts)
+
+        zero = jnp.zeros((block, width), jnp.float32)
+        intensity, first, second = lax.fori_loop(0, energies, one_energy, (zero, zero, zero), unroll=8)
+        residual = emitted_ref[0] - jnp.log(intensity) - target_ref[pl.ds(lo, block), :]
+        factor = residual / intensity / views_all
+        out0_ref[pl.ds(lo, block), :] = (first * factor).astype(out0_ref.dtype)
+        out1_ref[pl.ds(lo, block), :] = (second * factor).astype(out1_ref.dtype)
+        return carry
+
+    lax.fori_loop(0, rows // block, one_block, 0)
+
+
+def spectral_pallas(path_sums, observed, spectrum, attenuation, views_all):
+    view_count, row_count, materials, width_all = path_sums.shape
+    pixels = view_count * row_count * width_all
+    rows = pixels // LANES // 4
+    water = path_sums[:, :, 0, :].reshape(rows, 4 * LANES)
+    bone = path_sums[:, :, 1, :].reshape(rows, 4 * LANES)
+    target = observed.reshape(rows, 4 * LANES)
+    emitted = jnp.log(jnp.sum(spectrum)).reshape(1)
+    smem = pl.BlockSpec(memory_space=pltpu.SMEM)
+    vmem = pl.BlockSpec(memory_space=pltpu.VMEM)
+    first, second = pl.pallas_call(
+        functools.partial(spectral_kernel, views_all),
+        out_shape=(
+            jax.ShapeDtypeStruct((rows, 4 * LANES), jnp.bfloat16),
+            jax.ShapeDtypeStruct((rows, 4 * LANES), jnp.bfloat16),
+        ),
+        in_specs=[smem, smem, smem, vmem, vmem, vmem],
+        out_specs=(vmem, vmem),
+        interpret=INTERPRET,
+    )(emitted, spectrum, attenuation, water, bone, target)
+    shape = (view_count, row_count, width_all)
+    return jnp.stack([first.reshape(shape), second.reshape(shape)], axis=2)
 
 
 def per_device(density, measured, shear_shift, shear_frac, spectrum, attenuation):
@@ -399,7 +451,7 @@
 
     sums = shear_table(True, table, stacked, views_all, tile_width)
     sums = join_halves(sums, halves, rows_here, materials) / depth_all
-    grads = spectral(sums, observed, spectrum, attenuation, views_all)
+    grads = spectral_pallas(sums, observed, spectrum, attenuation, views_all)
     stacked_grads = stack_halves(grads.astype(jnp.float32), halves, tile_width)
     layers = shear_table(False, table, stacked_grads, depth_all, tile_width)
     layers = join_halves(layers, halves, rows_here, materials)

time: 67.5 us -> 67.1 us (level)
  matrix products: 7.39 us -> 0 us
  Pallas kernels: 10.8 us -> 16.6 us
  local copies, waits for them, and re-layouts: 12.1 us -> 13.9 us
    dot_general x8 -> x0, matrix products: 7.39 us -> none  [one_block(): moments = jnp.dot(coefficients, counts, precision=lax.Precision.HIGHEST)]
    pallas_call x0 -> x1, Pallas kernels: none -> 5.82 us  [spectral_pallas(): pl.pallas_call(functools.partial(spectral_kernel, views_all), out_shape=(...]
    another operation x3 -> x5, local copies, waits for them, and re-layouts: 0.34 us -> 3.18 us  [the longest x2 0.94 us: spectral_pallas(): return jnp.stack([first.reshape(shape), second.reshape(shape)], axis=2)]
  transfers between devices with their start and end apart: 2 -> 2, of which waited for: 2 -> 2; matrix products, arithmetic and copies ran while one was open for 5% -> 6% of each run, Pallas kernels for 0% -> 0%
where the time goes in v8:
time: 67.1 us; the launch traced here: 66.5 us
  Pallas kernels  16.6 us (25%)
  local copies, waits for them, and re-layouts  13.9 us (21%)
  blocking collectives  12.4 us (18%)
  waiting for transfers between devices  9.87 us (15%)
  starting transfers between devices  9.52 us (14%)
  other arithmetic  3.38 us (5%)
  between operations  0.87 us (1%)
    all_to_all x1, blocking collectives, per_device_wide(): layers = lax.all_to_all(layers, ('depth', 'lat'), 0, 0, tiled=True)  12.4 us
    pallas_call x2, Pallas kernels, shear_table(): pl.pallas_call(functools.partial(shear_table_kernel, forward), out_shape=...  10.8 us
    all_to_all x1, waiting for transfers between devices, per_device_wide(): mine = lax.all_to_all(mine, ('views', 'depth', 'lat'), 0, 0, tiled=True)  7.87 us
    pallas_call x1, Pallas kernels, spectral_pallas(): pl.pallas_call(functools.partial(spectral_kernel, views_all), out_shape=(...  5.82 us
    all_to_all x1, starting transfers between devices, per_device_wide(): observed = lax.all_to_all(observed, ('views', 'lat'), 0, 0, tiled=True)  5.2 us
    all_to_all x1, starting transfers between devices, per_device_wide(): mine = lax.all_to_all(mine, ('views', 'depth', 'lat'), 0, 0, tiled=True)  4.32 us
    all_to_all x1, waiting for transfers between devices, per_device_wide(): observed = lax.all_to_all(observed, ('views', 'lat'), 0, 0, tiled=True)  2 us
    unnamed x11, local copies, waits for them, and re-layouts  1.99 us
  transfers between devices with their start and end apart: 2, of which 2 were waited for; matrix products, arithmetic and copies ran while one was open for 6% of the time, Pallas kernels for 0%

profile of v8, /device:TPU:0, one launch (start us, length us, event | category | flops | bytes accessed | tf_op | source)
XLA Modules:
  0.0 66.5 jit_solution(2702135452040707641)
XLA Ops:
  0.0 1.3 %reshape.77 = f32[4,4,4,2,2,512]{5,4,3,2,1,0:T(2,128)S(1)} reshape(f32[4,64,512]{2,1,0:T(8,128)} %param.7) | data formatting | bytes 1048576 | tf_op jit(solution)/shard_map/reshape | solution.py:421
  1.4 0.7 %reshape.78 = f32[8,8,512]{2,1,0:T(8,128)} reshape(f32[4,2,4,2,512]{4,3,2,1,0:T(2,128)S(1)} %copy_bitcast_fusion.1) | data formatting | bytes 262144 | tf_op jit(solution)/shard_map/reshape | solution.py:423
  2.1 5.2 %all-to-all-start.1 = ((f32[8,8,512]{2,1,0:T(8,128)}), f32[8,8,512]{2,1,0:T(8,128)S(1)}, u32[]{:S(2)}, u32[]{:S(2)}) async-start(f32[8,8,512]{2,1,0:T(8,128)} %reshape.78), calls=%async_computation.1 | async-start | bytes 262144 | tf_op jit(solution)/shard_map/all_to_all | solution.py:426
  7.3 0.3 reshape.68
  7.7 0.8 %dynamic-slice_reduce_fusion = bf16[32,2048]{1,0:T(8,128)(2,1)S(1)} fusion(bf16[32,4,2048]{2,1,0:T(4,128)(2,1)S(1)} %reshape.68, s32[]{:T(128)S(6)} %select_n.8), kind=kLoop, calls=%fused_computation.4 | loop fusion | bytes 262148 | tf_op jit(solution)/shard_map/jit(dynamic_index_in_dim)/dynamic_slice | solution.py:433
  8.5 0.6 copy-done.3
  9.1 0.7 %copy-done.2 = s32[4,4]{1,0:T(4,128)S(1)} copy-done((s32[4,4]{1,0:T(4,128)S(1)}, s32[4,4]{1,0:T(4,128)}, u32[]{:S(2)}) %copy-start.2) | copy-done | bytes 88
  10.0 0.8 %pad_maximum_fusion.2 = bf16[32,5,512]{2,1,0:T(8,128)(2,1)} fusion(bf16[32,1,512]{2,1,0:T(2,128)(2,1)S(1)} %broadcast_in_dim.9, bf16[32,4,512]{2,1,0:T(4,128)(2,1)S(1)} %reshape.69), kind=kLoop, calls=%fused_computation.3 | loop fusion | flops 327680 | bytes 327680 | tf_op jit(solution)/shard_map/concatenate | solution.py:437
  10.8 2.0 %all-to-all-done.1 = f32[8,8,512]{2,1,0:T(8,128)S(1)} async-done(((f32[8,8,512]{2,1,0:T(8,128)}), f32[8,8,512]{2,1,0:T(8,128)S(1)}, u32[]{:S(2)}, u32[]{:S(2)}) %all-to-all-start.1) | async-done | bytes 131104 | tf_op jit(solution)/shard_map/all_to_all | solution.py:426
  12.8 4.3 %all-to-all-start = ((bf16[32,5,512]{2,1,0:T(8,128)(2,1)}), bf16[32,5,512]{2,1,0:T(8,128)(2,1)S(1)}, u32[]{:S(2)}, u32[]{:S(2)}) async-start(bf16[32,5,512]{2,1,0:T(8,128)(2,1)} %pad_maximum_fusion.2), calls=%async_computation | async-start | bytes 524288 | tf_op jit(solution)/shard_map/all_to_all | solution.py:438
  17.2 0.6 reduce_sum.9
  18.6 0.7 %reshape_reshape.6.target_ref = f32[64,512]{1,0:T(8,128)} reshape(f32[4,4,2,2,512]{4,3,2,1,0:T(2,128)S(1)} %copy.33) | data formatting | bytes 262144 | tf_op jit(solution)/shard_map/reshape;reshape | solution.py:126
  19.3 7.9 %all-to-all-done = bf16[32,5,512]{2,1,0:T(8,128)(2,1)S(1)} async-done(((bf16[32,5,512]{2,1,0:T(8,128)(2,1)}), bf16[32,5,512]{2,1,0:T(8,128)(2,1)S(1)}, u32[]{:S(2)}, u32[]{:S(2)}) %all-to-all-start) | async-done | bytes 163872 | tf_op jit(solution)/shard_map/all_to_all | solution.py:438
  27.5 0.1 copy.29
  27.9 0.8 %copy.39.src_ref = f32[16,8,640]{2,1,0:T(8,128)} copy(f32[16,8,640]{2,0,1:T(8,128)S(1)} %bitcast.47) | data formatting | bytes 655360 | tf_op jit(solution)/shard_map/reshape | solution.py:393
  28.9 0.7 %reshape.85.tab_ref = f32[3,16,16]{2,1,0:T(8,128)} reshape(f32[3,4,4,4,4]{4,3,2,1,0:T(4,128)S(1)} %copy.27) | data formatting | bytes 6144 | tf_op jit(solution)/shard_map/reshape | solution.py:442
  29.6 5.4 %shard_map.64 = f32[16,8,512]{2,1,0:T(8,128)} custom-call(f32[3,16,16]{2,1,0:T(8,128)} %reshape.85.tab_ref, f32[16,8,640]{2,1,0:T(8,128)} %copy.39.src_ref), custom_call_target="tpu_custom_call" | custom-call | tf_op jit(solution)/shard_map/pallas_call | solution.py:271
  35.0 1.0 %broadcast_multiply_fusion = f32[16,8,512]{2,1,0:T(8,128)S(1)} fusion(f32[16,8,512]{2,1,0:T(8,128)} %shard_map.64), kind=kLoop, calls=%fused_computation.14 | loop fusion | flops 65536 | bytes 524288 | tf_op jit(solution)/shard_map/div | solution.py:453
  36.0 0.1 div.14
  36.3 0.3 div.16
  36.6 0.8 %reshape_squeeze.6.water_ref = f32[64,512]{1,0:T(8,128)} reshape(f32[16,2,1,1024]{3,1,0,2:T(2,128)S(1)} %get-tuple-element.14) | data formatting | bytes 262144 | tf_op jit(solution)/shard_map/reshape;squeeze | solution.py:124
  37.4 0.7 %reshape_squeeze.7.bone_ref = f32[64,512]{1,0:T(8,128)} reshape(f32[16,2,1,1024]{3,1,0,2:T(2,128)S(1)} %get-tuple-element.13) | data formatting | bytes 262144 | tf_op jit(solution)/shard_map/reshape;squeeze | solution.py:125
  38.1 5.8 %shard_map.65 = (bf16[64,512]{1,0:T(8,128)(2,1)}, bf16[64,512]{1,0:T(8,128)(2,1)}) custom-call(f32[1]{0:T(128)} %bitcast.5.emitted_ref, f32[64]{0:T(128)} %spectrum_ref.1, f32[2,64]{1,0:T(2,128)} %attenuation_ref.1, f32[64,512]{1,0:T(8,128)} %reshape_squeeze.6.water_ref, f32[64,512]{1,0:T(8,128)} %reshape_squeeze.7.bone_ref, f32[64,512]{1,0:T(8,128)} %reshape_reshape.6.target_ref), custom_call_target="tpu_custom_call" | custom-call | tf_op jit(solution)/shard_map/pallas_call | solution.py:130
  44.0 0.9 %stack_reshape.8 = bf16[16,2,1,1024]{3,2,1,0:T(2,128)(2,1)S(1)} reshape(bf16[64,512]{1,0:T(8,128)(2,1)} %get-tuple-element.7) | data formatting | bytes 131072 | tf_op jit(solution)/shard_map/stack;reshape | solution.py:141
  44.9 0.7 %fusion = f32[16,2,2,1152]{3,2,1,0:T(2,128)S(1)} fusion(bf16[16,2,1,1024]{3,2,1,0:T(2,128)(2,1)S(1)} %stack_reshape.9, bf16[16,2,1,1024]{3,2,1,0:T(2,128)(2,1)S(1)} %stack_reshape.8), kind=kLoop, calls=%fused_computation.10 | loop fusion | flops 663552 | bytes 425984 | tf_op jit(solution)/shard_map/jit(_pad)/pad | solution.py:389
  45.6 0.1 pad_maximum_fusion.1
  45.8 0.9 %reshape.80.src_ref = f32[16,8,640]{2,1,0:T(8,128)} reshape(f32[16,2,2,2,640]{4,3,2,1,0:T(2,128)S(1)} %pad_maximum_fusion.1) | data formatting | bytes 655360 | tf_op jit(solution)/shard_map/reshape | solution.py:393
  46.7 5.4 %shard_map.66 = f32[16,8,512]{2,1,0:T(8,128)} custom-call(f32[3,16,16]{2,1,0:T(8,128)} %reshape.85.tab_ref, f32[16,8,640]{2,1,0:T(8,128)} %reshape.80.src_ref), custom_call_target="tpu_custom_call" | custom-call | tf_op jit(solution)/shard_map/pallas_call | solution.py:271
  52.2 1.1 %reshape.81 = f32[16,2,2,2,512]{4,3,2,1,0:T(2,128)S(1)} reshape(f32[16,8,512]{2,1,0:T(8,128)} %shard_map.66) | data formatting | bytes 524288 | tf_op jit(solution)/shard_map/reshape | solution.py:398
  53.3 0.2 copy.37
  53.4 12.4 %all_to_all.15 = f32[8,2,2,4,512]{4,3,2,1,0:T(4,128)S(1)} all-to-all(f32[8,2,2,4,512]{4,3,2,1,0:T(4,128)S(1)} %bitcast.50), channel_id=1, replica_groups=mesh['views'=4,'depth'=4,'lat'=2] {'depth','lat'}, dimensions={0} | all-to-all | bytes 524288 | tf_op jit(solution)/shard_map/all_to_all | solution.py:462
  65.8 0.7 %copy.47 = f32[16,2,4,512]{3,2,1,0:T(4,128)} copy(f32[16,2,4,512]{3,2,1,0:T(4,128)S(1)} %bitcast.51) | data formatting | bytes 524288
  (34 shorter events, 1.4 us)
Async XLA Ops:
  1.3 6.0 %copy-start = (bf16[64,2,4,512]{3,2,1,0:T(4,128)(2,1)S(1)}, bf16[64,2,4,512]{3,2,1,0:T(4,128)(2,1)}, u32[]{:S(2)}) copy-start(bf16[64,2,4,512]{3,2,1,0:T(4,128)(2,1)} %param.6) | copy-start | bytes 1572868
  2.1 10.7 %all-to-all-start.1 = ((f32[8,8,512]{2,1,0:T(8,128)}), f32[8,8,512]{2,1,0:T(8,128)S(1)}, u32[]{:S(2)}, u32[]{:S(2)}) async-start(f32[8,8,512]{2,1,0:T(8,128)} %reshape.78), calls=%async_computation.1 | async-start | bytes 262144 | tf_op jit(solution)/shard_map/all_to_all | solution.py:426
  8.4 0.7 %copy-start.3 = (f32[4,4]{1,0:T(4,128)S(1)}, f32[4,4]{1,0:T(4,128)}, u32[]{:S(2)}) copy-start(f32[4,4]{1,0:T(4,128)} %param.9) | copy-start | bytes 196
  9.1 0.7 %copy-start.2 = (s32[4,4]{1,0:T(4,128)S(1)}, s32[4,4]{1,0:T(4,128)}, u32[]{:S(2)}) copy-start(s32[4,4]{1,0:T(4,128)} %param.8) | copy-start | bytes 196
  10.8 6.3 %copy-start.4 = (f32[64]{0:T(128)S(1)}, f32[64]{0:T(128)}, u32[]{:S(2)}) copy-start(f32[64]{0:T(128)} %spectrum_ref.1) | copy-start | bytes 772
  12.8 14.3 %all-to-all-start = ((bf16[32,5,512]{2,1,0:T(8,128)(2,1)}), bf16[32,5,512]{2,1,0:T(8,128)(2,1)S(1)}, u32[]{:S(2)}, u32[]{:S(2)}) async-start(bf16[32,5,512]{2,1,0:T(8,128)(2,1)} %pad_maximum_fusion.2), calls=%async_computation | async-start | bytes 524288 | tf_op jit(solution)/shard_map/all_to_all | solution.py:438
  43.9 0.9 %copy-start.1 = (bf16[64,512]{1,0:T(8,128)(2,1)S(1)}, bf16[64,512]{1,0:T(8,128)(2,1)}, u32[]{:S(2)}) copy-start(bf16[64,512]{1,0:T(8,128)(2,1)} %get-tuple-element.8) | copy-start | bytes 196612

commit v9 on v8

--- a/solution.py
+++ b/solution.py
@@ -277,6 +277,94 @@
     )(table, src)
 
 
+def halo_columns(ys, lane, half_of, rows_here, halves, channels):
+    count = len(ys)
+    turned = [pltpu.roll(y, HALO, 1) for y in ys]
+    zero = jnp.zeros_like(ys[0])
+    left = jnp.where(half_of >= 1, pltpu.roll(turned[count - 1], rows_here, 0), zero)
+    right = jnp.where(half_of <= halves - 2, pltpu.roll(turned[0], channels - rows_here, 0), zero)
+    edge = lane < HALO
+    cols = [jnp.where(edge, left, turned[0])]
+    cols += [jnp.where(edge, turned[k - 1], turned[k]) for k in range(1, count)]
+    cols += [jnp.where(edge, turned[count - 1], right)]
+    return cols
+
+
+def shear_pass(forward, rows_here, halves, tab_ref, src_ref, acc_ref):
+    outer_count, channels, width = src_ref.shape
+    inner_count = acc_ref.shape[0]
+    pieces = width // LANES
+    lane = lax.broadcasted_iota(jnp.int32, (channels, LANES), 1)
+    half_of = (lax.broadcasted_iota(jnp.int32, (channels, LANES), 0) // rows_here) % halves
+    acc_ref[...] = jnp.zeros(acc_ref.shape, jnp.float32)
+
+    def outer(o, carry):
+        ys = [src_ref[o, :, k * LANES : (k + 1) * LANES] for k in range(pieces)]
+        cols = halo_columns(ys, lane, half_of, rows_here, halves, channels)
+        turned = [pltpu.roll(c, LANES - 1, 1) for c in cols]
+        nexts = [jnp.where(lane < LANES - 1, turned[k], turned[k + 1]) for k in range(pieces)]
+        nexts.append(turned[pieces])
+        for i in range(inner_count):
+            if forward:
+                shift = tab_ref[0, i, o].astype(jnp.int32)
+                wa = tab_ref[1, i, o]
+                wb = tab_ref[2, i, o]
+                offset = shift + HALO
+            else:
+                shift = tab_ref[0, o, i].astype(jnp.int32)
+                wa = tab_ref[2, o, i]
+                wb = tab_ref[1, o, i]
+                offset = HALO - 1 - shift
+            limit = LANES - offset
+            amount = jnp.where(limit == LANES, 0, limit)
+            mixed = [wa * cols[k] + wb * nexts[k] for k in range(pieces + 1)]
+            rolled = [pltpu.roll(m, amount, 1) for m in mixed]
+            keep = lane < limit
+            for j in range(pieces):
+                acc_ref[i, :, j * LANES : (j + 1) * LANES] += jnp.where(keep, rolled[j], rolled[j + 1])
+        return carry
+
+    lax.fori_loop(0, outer_count, outer, 0)
+
+
+def forward_kernel(rows_here, halves, depth_all, views_all, tab_ref, emitted_ref, spectrum_ref,
+                   attenuation_ref, src_ref, target_ref, out_ref, sums_ref):
+    shear_pass(True, rows_here, halves, tab_ref, src_ref, sums_ref)
+    _, channels, width = sums_ref.shape
+    energies = spectrum_ref.shape[0]
+    split = channels // 2
+    low = lax.broadcasted_iota(jnp.int32, (channels, width), 0) < split
+
+    def one_pair(p, carry):
+        first_view = sums_ref[2 * p] / depth_all
+        second_view = sums_ref[2 * p + 1] / depth_all
+        water = jnp.where(low, first_view, pltpu.roll(second_view, split, 0))
+        bone = jnp.where(low, pltpu.roll(first_view, split, 0), second_view)
+
+        def one_energy(e, sums):
+            intensity, first, second = sums
+            a0 = attenuation_ref[0, e]
+            a1 = attenuation_ref[1, e]
+            counts = spectrum_ref[e] * jnp.exp(-(a0 * water + a1 * bone))
+            return (intensity + counts, first + a0 * counts, second + a1 * counts)
+
+        zero = jnp.zeros((channels, width), jnp.float32)
+        intensity, first, second = lax.fori_loop(0, energies, one_energy, (zero, zero, zero), unroll=8)
+        residual = emitted_ref[0] - jnp.log(intensity) - target_ref[p]
+        factor = residual / intensity / views_all
+        first = (first * factor).astype(jnp.bfloat16).astype(jnp.float32)
+        second = (second * factor).astype(jnp.bfloat16).astype(jnp.float32)
+        out_ref[2 * p] = jnp.where(low, first, pltpu.roll(second, split, 0))
+        out_ref[2 * p + 1] = jnp.where(low, pltpu.roll(first, split, 0), second)
+        return carry
+
+    lax.fori_loop(0, out_ref.shape[0] // 2, one_pair, 0)
+
+
+def backward_kernel(rows_here, halves, tab_ref, src_ref, out_ref):
+    shear_pass(False, rows_here, halves, tab_ref, src_ref, out_ref)
+
+
 def shear_apply(offset, wa, wb, src, out_width):
     outer_count, channels, width = src.shape
     inner_count = offset.shape[1]
@@ -302,8 +390,9 @@
         rows % groups == 0
         and (rows // groups) % depth == 0
         and tile_width % LANES == 0
-        and 2 * HALO <= LANES
-        and tile_width >= HALO
+        and 2 * HALO == LANES
+        and density.shape[1] == 2
+        and measured.shape[0] * groups % 2 == 0
         and tile_width >= 3 * measured.shape[0] * density.shape[2] * groups
     )
 
@@ -377,8 +466,9 @@
         rows % groups == 0
         and (rows // groups) % parts == 0
         and tile_width % LANES == 0
-        and 2 * HALO <= LANES
-        and tile_width >= HALO
+        and 2 * HALO == LANES
+        and density.shape[1] == 2
+        and measured.shape[0] * groups % 2 == 0
         and tile_width >= 3 * measured.shape[0] * density.shape[2]
         and ((rows // groups // parts) * density.shape[1] * density.shape[2]) % groups == 0
     )
@@ -444,19 +534,31 @@
     mine = jnp.transpose(mine, (1, 2, 0, 3)).reshape(
         depth_count, halves, rows_here, materials, depth_here, tile_width
     )
-    mine = jnp.transpose(mine, (0, 4, 2, 3, 1, 5)).reshape(
-        depth_all, rows_here, materials, halves * tile_width
-    )
-    stacked = stack_halves(mine.astype(jnp.float32), halves, tile_width)
-
-    sums = shear_table(True, table, stacked, views_all, tile_width)
-    sums = join_halves(sums, halves, rows_here, materials) / depth_all
-    grads = spectral_pallas(sums, observed, spectrum, attenuation, views_all)
-    stacked_grads = stack_halves(grads.astype(jnp.float32), halves, tile_width)
-    layers = shear_table(False, table, stacked_grads, depth_all, tile_width)
-    layers = join_halves(layers, halves, rows_here, materials)
-    layers = layers.reshape(depth_count, depth_here, rows_here, materials, halves, tile_width)
-    layers = jnp.transpose(layers, (0, 4, 2, 3, 1, 5)).reshape(
+    channels = materials * halves * rows_here
+    mine = jnp.transpose(mine, (0, 4, 3, 1, 2, 5)).reshape(depth_all, channels, tile_width)
+    mine = mine.astype(jnp.float32)
+    target = observed.reshape(views_all // 2, 2, rows_here, halves, tile_width)
+    target = jnp.transpose(target, (0, 1, 3, 2, 4)).reshape(views_all // 2, 2 * halves * rows_here, tile_width)
+    emitted = jnp.log(jnp.sum(spectrum)).reshape(1)
+    smem = pl.BlockSpec(memory_space=pltpu.SMEM)
+    vmem = pl.BlockSpec(memory_space=pltpu.VMEM)
+    grads = pl.pallas_call(
+        functools.partial(forward_kernel, rows_here, halves, depth_all, views_all),
+        out_shape=jax.ShapeDtypeStruct((views_all, channels, tile_width), jnp.float32),
+        in_specs=[smem, smem, smem, smem, vmem, vmem],
+        out_specs=vmem,
+        scratch_shapes=[pltpu.VMEM((views_all, channels, tile_width), jnp.float32)],
+        interpret=INTERPRET,
+    )(table, emitted, spectrum, attenuation, mine, target)
+    layers = pl.pallas_call(
+        functools.partial(backward_kernel, rows_here, halves),
+        out_shape=jax.ShapeDtypeStruct((depth_all, channels, tile_width), jnp.float32),
+        in_specs=[smem, vmem],
+        out_specs=vmem,
+        interpret=INTERPRET,
+    )(table, grads)
+    layers = layers.reshape(depth_count, depth_here, materials, halves, rows_here, tile_width)
+    layers = jnp.transpose(layers, (0, 3, 4, 2, 1, 5)).reshape(
         parts, rows_here, materials, depth_here, tile_width
     )
     layers = lax.all_to_all(layers, ("depth", "lat"), 0, 0, tiled=True)

time: 67.1 us -> 61.9 us (0.923)
  local copies, waits for them, and re-layouts: 13.9 us -> 10.3 us
  other arithmetic: 3.38 us -> 1.51 us
    another operation x7 -> x0, local copies, waits for them, and re-layouts: 3.24 us -> none  [the longest x2 0.94 us: spectral_pallas(): return jnp.stack([first.reshape(shape), second.reshape(shape)], axis=2)]
    convert_element_type x3 -> x5, local copies, waits for them, and re-layouts: 0.3 us -> 1.74 us  [per_device_wide(): mine = mine.astype(jnp.float32)]
    reshape x5 -> x3, local copies, waits for them, and re-layouts: 3.03 us -> 2.02 us  [the longest x2 1.27 us: per_device_wide(): layers.reshape(depth_count, depth_here, materials, halves, rows_here, til...]
    div x1 -> x0, other arithmetic: 0.97 us -> none  [per_device_wide(): sums = join_halves(sums, halves, rows_here, materials) / depth_all]
    pad x2 -> x0, other arithmetic: 0.79 us -> none  [stack_halves(): padded = jnp.pad(values, ((0, 0), (0, 0), (0, 0), (HALO, HALO)))]
    pallas_call x3 -> x2, Pallas kernels: 16.6 us -> 17.1 us  [the longest x1 10.7 us: per_device_wide(): pl.pallas_call(functools.partial(forward_kernel, rows_here, halves, depth...]
    unnamed x11 -> x9, local copies, waits for them, and re-layouts: 1.99 us -> 1.98 us
where the time goes in v9:
time: 61.9 us; the launch traced here: 61.4 us
  Pallas kernels  17.1 us (28%)
  blocking collectives  12.4 us (20%)
  local copies, waits for them, and re-layouts  10.3 us (17%)
  waiting for transfers between devices  9.75 us (16%)
  starting transfers between devices  9.52 us (15%)
  other arithmetic  1.51 us (2%)
  between operations  0.79 us (1%)
    all_to_all x1, blocking collectives, per_device_wide(): layers = lax.all_to_all(layers, ('depth', 'lat'), 0, 0, tiled=True)  12.4 us
    pallas_call x1, Pallas kernels, per_device_wide(): pl.pallas_call(functools.partial(forward_kernel, rows_here, halves, depth...  10.7 us
    all_to_all x1, waiting for transfers between devices, per_device_wide(): mine = lax.all_to_all(mine, ('views', 'depth', 'lat'), 0, 0, tiled=True)  7.75 us
    pallas_call x1, Pallas kernels, per_device_wide(): pl.pallas_call(functools.partial(backward_kernel, rows_here, halves), out...  6.47 us
    all_to_all x1, starting transfers between devices, per_device_wide(): observed = lax.all_to_all(observed, ('views', 'lat'), 0, 0, tiled=True)  5.2 us
    all_to_all x1, starting transfers between devices, per_device_wide(): mine = lax.all_to_all(mine, ('views', 'depth', 'lat'), 0, 0, tiled=True)  4.32 us
    all_to_all x1, waiting for transfers between devices, per_device_wide(): observed = lax.all_to_all(observed, ('views', 'lat'), 0, 0, tiled=True)  2 us
    unnamed x9, local copies, waits for them, and re-layouts  1.98 us
  transfers between devices with their start and end apart: 2, of which 2 were waited for; matrix products, arithmetic and copies ran while one was open for 6% of the time, Pallas kernels for 0%

profile of v9, /device:TPU:0, one launch (start us, length us, event | category | flops | bytes accessed | tf_op | source)
XLA Modules:
  0.0 61.4 jit_solution(6747256711587401827)
XLA Ops:
  0.0 1.3 %reshape.67 = f32[4,4,4,2,2,512]{5,4,3,2,1,0:T(2,128)S(1)} reshape(f32[4,64,512]{2,1,0:T(8,128)} %param.7) | data formatting | bytes 1048576 | tf_op jit(solution)/shard_map/reshape | solution.py:511
  1.4 0.7 %reshape.68 = f32[8,8,512]{2,1,0:T(8,128)} reshape(f32[4,2,4,2,512]{4,3,2,1,0:T(2,128)S(1)} %copy_bitcast_fusion.1) | data formatting | bytes 262144 | tf_op jit(solution)/shard_map/reshape | solution.py:513
  2.1 5.2 %all-to-all-start.1 = ((f32[8,8,512]{2,1,0:T(8,128)}), f32[8,8,512]{2,1,0:T(8,128)S(1)}, u32[]{:S(2)}, u32[]{:S(2)}) async-start(f32[8,8,512]{2,1,0:T(8,128)} %reshape.68), calls=%async_computation.1 | async-start | bytes 262144 | tf_op jit(solution)/shard_map/all_to_all | solution.py:516
  7.3 0.3 reshape.59
  7.7 0.8 %dynamic-slice_reduce_fusion = bf16[32,2048]{1,0:T(8,128)(2,1)S(1)} fusion(bf16[32,4,2048]{2,1,0:T(4,128)(2,1)S(1)} %reshape.59, s32[]{:T(128)S(6)} %select_n.8), kind=kLoop, calls=%fused_computation.2 | loop fusion | bytes 262148 | tf_op jit(solution)/shard_map/jit(dynamic_index_in_dim)/dynamic_slice | solution.py:523
  8.5 0.1 reshape.60
  8.5 0.6 copy-done.2
  9.1 0.7 %copy-done.1 = s32[4,4]{1,0:T(4,128)S(1)} copy-done((s32[4,4]{1,0:T(4,128)S(1)}, s32[4,4]{1,0:T(4,128)}, u32[]{:S(2)}) %copy-start.1) | copy-done | bytes 88
  9.8 0.1 reshape.61
  10.0 0.8 %pad_maximum_fusion = bf16[32,5,512]{2,1,0:T(8,128)(2,1)} fusion(bf16[32,1,512]{2,1,0:T(2,128)(2,1)S(1)} %broadcast_in_dim.9, bf16[32,4,512]{2,1,0:T(4,128)(2,1)S(1)} %reshape.60), kind=kLoop, calls=%fused_computation | loop fusion | flops 327680 | bytes 327680 | tf_op jit(solution)/shard_map/concatenate | solution.py:527
  10.8 2.0 %all-to-all-done.1 = f32[8,8,512]{2,1,0:T(8,128)S(1)} async-done(((f32[8,8,512]{2,1,0:T(8,128)}), f32[8,8,512]{2,1,0:T(8,128)S(1)}, u32[]{:S(2)}, u32[]{:S(2)}) %all-to-all-start.1) | async-done | bytes 131104 | tf_op jit(solution)/shard_map/all_to_all | solution.py:516
  12.8 4.3 %all-to-all-start = ((bf16[32,5,512]{2,1,0:T(8,128)(2,1)}), bf16[32,5,512]{2,1,0:T(8,128)(2,1)S(1)}, u32[]{:S(2)}, u32[]{:S(2)}) async-start(bf16[32,5,512]{2,1,0:T(8,128)(2,1)} %pad_maximum_fusion), calls=%async_computation | async-start | bytes 524288 | tf_op jit(solution)/shard_map/all_to_all | solution.py:528
  17.2 0.6 reduce_sum.9
  18.4 0.1 reshape.69
  18.5 0.1 copy.20
  18.6 0.1 copy.21
  18.7 0.7 %reshape.70.target_ref = f32[8,8,512]{2,1,0:T(8,128)} reshape(f32[8,2,2,2,512]{4,3,2,1,0:T(2,128)S(1)} %copy.21) | data formatting | bytes 262144 | tf_op jit(solution)/shard_map/reshape | solution.py:541
  19.4 7.8 %all-to-all-done = bf16[32,5,512]{2,1,0:T(8,128)(2,1)S(1)} async-done(((bf16[32,5,512]{2,1,0:T(8,128)(2,1)}), bf16[32,5,512]{2,1,0:T(8,128)(2,1)S(1)}, u32[]{:S(2)}, u32[]{:S(2)}) %all-to-all-start) | async-done | bytes 163872 | tf_op jit(solution)/shard_map/all_to_all | solution.py:528
  27.2 0.1 slice_convert_fusion
  27.3 0.1 reshape.79
  27.4 0.7 %reshape.75.tab_ref = f32[3,16,16]{2,1,0:T(8,128)} reshape(f32[3,4,4,4,4]{4,3,2,1,0:T(4,128)S(1)} %copy.16) | data formatting | bytes 6144 | tf_op jit(solution)/shard_map/reshape | solution.py:532
  28.1 0.3 reshape.82
  28.4 0.2 copy.29
  28.6 0.2 reshape.80
  28.8 0.2 copy.18
  29.0 0.9 %reshape.76.src_ref = f32[16,8,512]{2,1,0:T(8,128)} reshape(f32[4,4,2,2,2,512]{5,4,3,2,1,0:T(2,128)S(1)} %copy.18) | data formatting | bytes 524288 | tf_op jit(solution)/shard_map/convert_element_type | solution.py:539
  29.9 10.7 %shard_map.64.src_ref = f32[16,8,512]{2,1,0:T(8,128)} custom-call(f32[3,16,16]{2,1,0:T(8,128)} %reshape.75.tab_ref, f32[1]{0:T(128)} %bitcast.5.emitted_ref, f32[64]{0:T(128)} %spectrum_ref.1, f32[2,64]{1,0:T(2,128)} %attenuation_ref.1, f32[16,8,512]{2,1,0:T(8,128)} %reshape.76.src_ref, f32[8,8,512]{2,1,0:T(8,128)} %reshape.70.target_ref), custom_call_target="tpu_custom_call" | custom-call | tf_op jit(solution)/shard_map/pallas_call | solution.py:545
  40.6 6.5 %shard_map.65 = f32[16,8,512]{2,1,0:T(8,128)} custom-call(f32[3,16,16]{2,1,0:T(8,128)} %reshape.75.tab_ref, f32[16,8,512]{2,1,0:T(8,128)} %shard_map.64.src_ref), custom_call_target="tpu_custom_call" | custom-call | tf_op jit(solution)/shard_map/pallas_call | solution.py:553
  47.0 1.1 %reshape.71 = f32[4,4,2,2,2,512]{5,4,3,2,1,0:T(2,128)S(1)} reshape(f32[16,8,512]{2,1,0:T(8,128)} %shard_map.65) | data formatting | bytes 524288 | tf_op jit(solution)/shard_map/reshape | solution.py:560
  48.1 0.2 copy.22
  48.3 12.4 %all_to_all.15 = f32[8,2,2,4,512]{4,3,2,1,0:T(4,128)S(1)} all-to-all(f32[8,2,2,4,512]{4,3,2,1,0:T(4,128)S(1)} %bitcast.29), channel_id=1, replica_groups=mesh['views'=4,'depth'=4,'lat'=2] {'depth','lat'}, dimensions={0} | all-to-all | bytes 524288 | tf_op jit(solution)/shard_map/all_to_all | solution.py:564
  60.7 0.7 %copy.31 = f32[16,2,4,512]{3,2,1,0:T(4,128)} copy(f32[16,2,4,512]{3,2,1,0:T(4,128)S(1)} %bitcast.30) | data formatting | bytes 524288
  (15 shorter events, 0.2 us)
Async XLA Ops:
  1.3 6.0 %copy-start = (bf16[64,2,4,512]{3,2,1,0:T(4,128)(2,1)S(1)}, bf16[64,2,4,512]{3,2,1,0:T(4,128)(2,1)}, u32[]{:S(2)}) copy-start(bf16[64,2,4,512]{3,2,1,0:T(4,128)(2,1)} %param.6) | copy-start | bytes 1572868
  2.1 10.7 %all-to-all-start.1 = ((f32[8,8,512]{2,1,0:T(8,128)}), f32[8,8,512]{2,1,0:T(8,128)S(1)}, u32[]{:S(2)}, u32[]{:S(2)}) async-start(f32[8,8,512]{2,1,0:T(8,128)} %reshape.68), calls=%async_computation.1 | async-start | bytes 262144 | tf_op jit(solution)/shard_map/all_to_all | solution.py:516
  8.4 0.7 %copy-start.2 = (f32[4,4]{1,0:T(4,128)S(1)}, f32[4,4]{1,0:T(4,128)}, u32[]{:S(2)}) copy-start(f32[4,4]{1,0:T(4,128)} %param.9) | copy-start | bytes 196
  9.1 0.7 %copy-start.1 = (s32[4,4]{1,0:T(4,128)S(1)}, s32[4,4]{1,0:T(4,128)}, u32[]{:S(2)}) copy-start(s32[4,4]{1,0:T(4,128)} %param.8) | copy-start | bytes 196
  10.8 6.3 %copy-start.3 = (f32[64]{0:T(128)S(1)}, f32[64]{0:T(128)}, u32[]{:S(2)}) copy-start(f32[64]{0:T(128)} %spectrum_ref.1) | copy-start | bytes 772
  12.8 14.3 %all-to-all-start = ((bf16[32,5,512]{2,1,0:T(8,128)(2,1)}), bf16[32,5,512]{2,1,0:T(8,128)(2,1)S(1)}, u32[]{:S(2)}, u32[]{:S(2)}) async-start(bf16[32,5,512]{2,1,0:T(8,128)(2,1)} %pad_maximum_fusion), calls=%async_computation | async-start | bytes 524288 | tf_op jit(solution)/shard_map/all_to_all | solution.py:528

commit v10 on v9

--- a/solution.py
+++ b/solution.py
@@ -290,21 +290,29 @@
     return cols
 
 
-def shear_pass(forward, rows_here, halves, tab_ref, src_ref, acc_ref):
+def shear_pass(forward, rows_here, halves, tab_ref, src_ref, acc_ref, cols_ref, nexts_ref):
     outer_count, channels, width = src_ref.shape
     inner_count = acc_ref.shape[0]
     pieces = width // LANES
     lane = lax.broadcasted_iota(jnp.int32, (channels, LANES), 1)
     half_of = (lax.broadcasted_iota(jnp.int32, (channels, LANES), 0) // rows_here) % halves
-    acc_ref[...] = jnp.zeros(acc_ref.shape, jnp.float32)
-
-    def outer(o, carry):
+
+    def prepare(o, carry):
         ys = [src_ref[o, :, k * LANES : (k + 1) * LANES] for k in range(pieces)]
         cols = halo_columns(ys, lane, half_of, rows_here, halves, channels)
         turned = [pltpu.roll(c, LANES - 1, 1) for c in cols]
         nexts = [jnp.where(lane < LANES - 1, turned[k], turned[k + 1]) for k in range(pieces)]
         nexts.append(turned[pieces])
-        for i in range(inner_count):
+        for k in range(pieces + 1):
+            cols_ref[o, :, k * LANES : (k + 1) * LANES] = cols[k]
+            nexts_ref[o, :, k * LANES : (k + 1) * LANES] = nexts[k]
+        return carry
+
+    lax.fori_loop(0, outer_count, prepare, 0)
+
+    def inner(i, carry):
+        acc = [jnp.zeros((channels, LANES), jnp.float32) for _ in range(pieces)]
+        for o in range(outer_count):
             if forward:
                 shift = tab_ref[0, i, o].astype(jnp.int32)
                 wa = tab_ref[1, i, o]
@@ -317,19 +325,24 @@
                 offset = HALO - 1 - shift
             limit = LANES - offset
             amount = jnp.where(limit == LANES, 0, limit)
-            mixed = [wa * cols[k] + wb * nexts[k] for k in range(pieces + 1)]
+            mixed = [
+                wa * cols_ref[o, :, k * LANES : (k + 1) * LANES]
+                + wb * nexts_ref[o, :, k * LANES : (k + 1) * LANES]
+                for k in range(pieces + 1)
+            ]
             rolled = [pltpu.roll(m, amount, 1) for m in mixed]
             keep = lane < limit
-            for j in range(pieces):
-                acc_ref[i, :, j * LANES : (j + 1) * LANES] += jnp.where(keep, rolled[j], rolled[j + 1])
+            acc = [acc[j] + jnp.where(keep, rolled[j], rolled[j + 1]) for j in range(pieces)]
+        for j in range(pieces):
+            acc_ref[i, :, j * LANES : (j + 1) * LANES] = acc[j]
         return carry
 
-    lax.fori_loop(0, outer_count, outer, 0)
+    lax.fori_loop(0, inner_count, inner, 0)
 
 
 def forward_kernel(rows_here, halves, depth_all, views_all, tab_ref, emitted_ref, spectrum_ref,
-                   attenuation_ref, src_ref, target_ref, out_ref, sums_ref):
-    shear_pass(True, rows_here, halves, tab_ref, src_ref, sums_ref)
+                   attenuation_ref, src_ref, target_ref, out_ref, sums_ref, cols_ref, nexts_ref):
+    shear_pass(True, rows_here, halves, tab_ref, src_ref, sums_ref, cols_ref, nexts_ref)
     _, channels, width = sums_ref.shape
     energies = spectrum_ref.shape[0]
     split = channels // 2
@@ -361,8 +374,8 @@
     lax.fori_loop(0, out_ref.shape[0] // 2, one_pair, 0)
 
 
-def backward_kernel(rows_here, halves, tab_ref, src_ref, out_ref):
-    shear_pass(False, rows_here, halves, tab_ref, src_ref, out_ref)
+def backward_kernel(rows_here, halves, tab_ref, src_ref, out_ref, cols_ref, nexts_ref):
+    shear_pass(False, rows_here, halves, tab_ref, src_ref, out_ref, cols_ref, nexts_ref)
 
 
 def shear_apply(offset, wa, wb, src, out_width):
@@ -547,7 +560,11 @@
         out_shape=jax.ShapeDtypeStruct((views_all, channels, tile_width), jnp.float32),
         in_specs=[smem, smem, smem, smem, vmem, vmem],
         out_specs=vmem,
-        scratch_shapes=[pltpu.VMEM((views_all, channels, tile_width), jnp.float32)],
+        scratch_shapes=[
+            pltpu.VMEM((views_all, channels, tile_width), jnp.float32),
+            pltpu.VMEM((depth_all, channels, tile_width + LANES), jnp.float32),
+            pltpu.VMEM((depth_all, channels, tile_width + LANES), jnp.float32),
+        ],
         interpret=INTERPRET,
     )(table, emitted, spectrum, attenuation, mine, target)
     layers = pl.pallas_call(
@@ -555,6 +572,10 @@
         out_shape=jax.ShapeDtypeStruct((depth_all, channels, tile_width), jnp.float32),
         in_specs=[smem, vmem],
         out_specs=vmem,
+        scratch_shapes=[
+            pltpu.VMEM((views_all, channels, tile_width + LANES), jnp.float32),
+            pltpu.VMEM((views_all, channels, tile_width + LANES), jnp.float32),
+        ],
         interpret=INTERPRET,
     )(table, grads)
     layers = layers.reshape(depth_count, depth_here, materials, halves, rows_here, tile_width)

time: 61.9 us -> 62.2 us (level)
  no operation moved by 1% of the time
where the time goes in v10:
time: 62.2 us; the launch traced here: 61.7 us
  Pallas kernels  17.5 us (28%)
  blocking collectives  12.4 us (20%)
  local copies, waits for them, and re-layouts  10.3 us (17%)
  waiting for transfers between devices  9.75 us (16%)
  starting transfers between devices  9.52 us (15%)
  other arithmetic  1.51 us (2%)
  between operations  0.79 us (1%)
    all_to_all x1, blocking collectives, per_device_wide(): layers = lax.all_to_all(layers, ('depth', 'lat'), 0, 0, tiled=True)  12.4 us
    pallas_call x1, Pallas kernels, per_device_wide(): pl.pallas_call(functools.partial(forward_kernel, rows_here, halves, depth...  10.8 us
    all_to_all x1, waiting for transfers between devices, per_device_wide(): mine = lax.all_to_all(mine, ('views', 'depth', 'lat'), 0, 0, tiled=True)  7.75 us
    pallas_call x1, Pallas kernels, per_device_wide(): pl.pallas_call(functools.partial(backward_kernel, rows_here, halves), out...  6.64 us
    all_to_all x1, starting transfers between devices, per_device_wide(): observed = lax.all_to_all(observed, ('views', 'lat'), 0, 0, tiled=True)  5.2 us
    all_to_all x1, starting transfers between devices, per_device_wide(): mine = lax.all_to_all(mine, ('views', 'depth', 'lat'), 0, 0, tiled=True)  4.32 us
    all_to_all x1, waiting for transfers between devices, per_device_wide(): observed = lax.all_to_all(observed, ('views', 'lat'), 0, 0, tiled=True)  2 us
    unnamed x9, local copies, waits for them, and re-layouts  1.98 us
  transfers between devices with their start and end apart: 2, of which 2 were waited for; matrix products, arithmetic and copies ran while one was open for 6% of the time, Pallas kernels for 0%

profile of v10, /device:TPU:0, one launch (start us, length us, event | category | flops | bytes accessed | tf_op | source)
XLA Modules:
  0.0 61.7 jit_solution(16969903472362932041)
XLA Ops:
  0.0 1.3 %reshape.67 = f32[4,4,4,2,2,512]{5,4,3,2,1,0:T(2,128)S(1)} reshape(f32[4,64,512]{2,1,0:T(8,128)} %param.7) | data formatting | bytes 1048576 | tf_op jit(solution)/shard_map/reshape | solution.py:524
  1.4 0.7 %reshape.68 = f32[8,8,512]{2,1,0:T(8,128)} reshape(f32[4,2,4,2,512]{4,3,2,1,0:T(2,128)S(1)} %copy_bitcast_fusion.1) | data formatting | bytes 262144 | tf_op jit(solution)/shard_map/reshape | solution.py:526
  2.1 5.2 %all-to-all-start.1 = ((f32[8,8,512]{2,1,0:T(8,128)}), f32[8,8,512]{2,1,0:T(8,128)S(1)}, u32[]{:S(2)}, u32[]{:S(2)}) async-start(f32[8,8,512]{2,1,0:T(8,128)} %reshape.68), calls=%async_computation.1 | async-start | bytes 262144 | tf_op jit(solution)/shard_map/all_to_all | solution.py:529
  7.3 0.3 reshape.59
  7.7 0.8 %dynamic-slice_reduce_fusion = bf16[32,2048]{1,0:T(8,128)(2,1)S(1)} fusion(bf16[32,4,2048]{2,1,0:T(4,128)(2,1)S(1)} %reshape.59, s32[]{:T(128)S(6)} %select_n.8), kind=kLoop, calls=%fused_computation.2 | loop fusion | bytes 262148 | tf_op jit(solution)/shard_map/jit(dynamic_index_in_dim)/dynamic_slice | solution.py:536
  8.5 0.1 reshape.60
  8.5 0.6 copy-done.2
  9.1 0.7 %copy-done.1 = s32[4,4]{1,0:T(4,128)S(1)} copy-done((s32[4,4]{1,0:T(4,128)S(1)}, s32[4,4]{1,0:T(4,128)}, u32[]{:S(2)}) %copy-start.1) | copy-done | bytes 88
  9.8 0.1 reshape.61
  10.0 0.8 %pad_maximum_fusion = bf16[32,5,512]{2,1,0:T(8,128)(2,1)} fusion(bf16[32,1,512]{2,1,0:T(2,128)(2,1)S(1)} %broadcast_in_dim.9, bf16[32,4,512]{2,1,0:T(4,128)(2,1)S(1)} %reshape.60), kind=kLoop, calls=%fused_computation | loop fusion | flops 327680 | bytes 327680 | tf_op jit(solution)/shard_map/concatenate | solution.py:540
  10.8 2.0 %all-to-all-done.1 = f32[8,8,512]{2,1,0:T(8,128)S(1)} async-done(((f32[8,8,512]{2,1,0:T(8,128)}), f32[8,8,512]{2,1,0:T(8,128)S(1)}, u32[]{:S(2)}, u32[]{:S(2)}) %all-to-all-start.1) | async-done | bytes 131104 | tf_op jit(solution)/shard_map/all_to_all | solution.py:529
  12.8 4.3 %all-to-all-start = ((bf16[32,5,512]{2,1,0:T(8,128)(2,1)}), bf16[32,5,512]{2,1,0:T(8,128)(2,1)S(1)}, u32[]{:S(2)}, u32[]{:S(2)}) async-start(bf16[32,5,512]{2,1,0:T(8,128)(2,1)} %pad_maximum_fusion), calls=%async_computation | async-start | bytes 524288 | tf_op jit(solution)/shard_map/all_to_all | solution.py:541
  17.2 0.6 reduce_sum.9
  18.4 0.1 reshape.69
  18.5 0.1 copy.20
  18.6 0.1 copy.21
  18.7 0.7 %reshape.70.target_ref = f32[8,8,512]{2,1,0:T(8,128)} reshape(f32[8,2,2,2,512]{4,3,2,1,0:T(2,128)S(1)} %copy.21) | data formatting | bytes 262144 | tf_op jit(solution)/shard_map/reshape | solution.py:554
  19.4 7.8 %all-to-all-done = bf16[32,5,512]{2,1,0:T(8,128)(2,1)S(1)} async-done(((bf16[32,5,512]{2,1,0:T(8,128)(2,1)}), bf16[32,5,512]{2,1,0:T(8,128)(2,1)S(1)}, u32[]{:S(2)}, u32[]{:S(2)}) %all-to-all-start) | async-done | bytes 163872 | tf_op jit(solution)/shard_map/all_to_all | solution.py:541
  27.2 0.1 slice_convert_fusion
  27.3 0.1 reshape.79
  27.4 0.7 %reshape.75.tab_ref = f32[3,16,16]{2,1,0:T(8,128)} reshape(f32[3,4,4,4,4]{4,3,2,1,0:T(4,128)S(1)} %copy.16) | data formatting | bytes 6144 | tf_op jit(solution)/shard_map/reshape | solution.py:545
  28.1 0.3 reshape.82
  28.4 0.2 copy.29
  28.6 0.2 reshape.80
  28.8 0.2 copy.18
  29.0 0.9 %reshape.76.src_ref = f32[16,8,512]{2,1,0:T(8,128)} reshape(f32[4,4,2,2,2,512]{5,4,3,2,1,0:T(2,128)S(1)} %copy.18) | data formatting | bytes 524288 | tf_op jit(solution)/shard_map/convert_element_type | solution.py:552
  29.9 10.8 %shard_map.64.src_ref = f32[16,8,512]{2,1,0:T(8,128)} custom-call(f32[3,16,16]{2,1,0:T(8,128)} %reshape.75.tab_ref, f32[1]{0:T(128)} %bitcast.5.emitted_ref, f32[64]{0:T(128)} %spectrum_ref.1, f32[2,64]{1,0:T(2,128)} %attenuation_ref.1, f32[16,8,512]{2,1,0:T(8,128)} %reshape.76.src_ref, f32[8,8,512]{2,1,0:T(8,128)} %reshape.70.target_ref), custom_call_target="tpu_custom_call" | custom-call | tf_op jit(solution)/shard_map/pallas_call | solution.py:558
  40.7 6.6 %shard_map.65 = f32[16,8,512]{2,1,0:T(8,128)} custom-call(f32[3,16,16]{2,1,0:T(8,128)} %reshape.75.tab_ref, f32[16,8,512]{2,1,0:T(8,128)} %shard_map.64.src_ref), custom_call_target="tpu_custom_call" | custom-call | tf_op jit(solution)/shard_map/pallas_call | solution.py:570
  47.4 1.1 %reshape.71 = f32[4,4,2,2,2,512]{5,4,3,2,1,0:T(2,128)S(1)} reshape(f32[16,8,512]{2,1,0:T(8,128)} %shard_map.65) | data formatting | bytes 524288 | tf_op jit(solution)/shard_map/reshape | solution.py:581
  48.5 0.2 copy.22
  48.7 12.4 %all_to_all.15 = f32[8,2,2,4,512]{4,3,2,1,0:T(4,128)S(1)} all-to-all(f32[8,2,2,4,512]{4,3,2,1,0:T(4,128)S(1)} %bitcast.29), channel_id=1, replica_groups=mesh['views'=4,'depth'=4,'lat'=2] {'depth','lat'}, dimensions={0} | all-to-all | bytes 524288 | tf_op jit(solution)/shard_map/all_to_all | solution.py:585
  61.0 0.7 %copy.31 = f32[16,2,4,512]{3,2,1,0:T(4,128)} copy(f32[16,2,4,512]{3,2,1,0:T(4,128)S(1)} %bitcast.30) | data formatting | bytes 524288
  (15 shorter events, 0.2 us)
Async XLA Ops:
  1.3 6.0 %copy-start = (bf16[64,2,4,512]{3,2,1,0:T(4,128)(2,1)S(1)}, bf16[64,2,4,512]{3,2,1,0:T(4,128)(2,1)}, u32[]{:S(2)}) copy-start(bf16[64,2,4,512]{3,2,1,0:T(4,128)(2,1)} %param.6) | copy-start | bytes 1572868
  2.1 10.7 %all-to-all-start.1 = ((f32[8,8,512]{2,1,0:T(8,128)}), f32[8,8,512]{2,1,0:T(8,128)S(1)}, u32[]{:S(2)}, u32[]{:S(2)}) async-start(f32[8,8,512]{2,1,0:T(8,128)} %reshape.68), calls=%async_computation.1 | async-start | bytes 262144 | tf_op jit(solution)/shard_map/all_to_all | solution.py:529
  8.4 0.7 %copy-start.2 = (f32[4,4]{1,0:T(4,128)S(1)}, f32[4,4]{1,0:T(4,128)}, u32[]{:S(2)}) copy-start(f32[4,4]{1,0:T(4,128)} %param.9) | copy-start | bytes 196
  9.1 0.7 %copy-start.1 = (s32[4,4]{1,0:T(4,128)S(1)}, s32[4,4]{1,0:T(4,128)}, u32[]{:S(2)}) copy-start(s32[4,4]{1,0:T(4,128)} %param.8) | copy-start | bytes 196
  10.8 6.3 %copy-start.3 = (f32[64]{0:T(128)S(1)}, f32[64]{0:T(128)}, u32[]{:S(2)}) copy-start(f32[64]{0:T(128)} %spectrum_ref.1) | copy-start | bytes 772
  12.8 14.3 %all-to-all-start = ((bf16[32,5,512]{2,1,0:T(8,128)(2,1)}), bf16[32,5,512]{2,1,0:T(8,128)(2,1)S(1)}, u32[]{:S(2)}, u32[]{:S(2)}) async-start(bf16[32,5,512]{2,1,0:T(8,128)(2,1)} %pad_maximum_fusion), calls=%async_computation | async-start | bytes 524288 | tf_op jit(solution)/shard_map/all_to_all | solution.py:541

commit v11 on v10

--- a/solution.py
+++ b/solution.py
@@ -340,6 +340,57 @@
     lax.fori_loop(0, inner_count, inner, 0)
 
 
+def scatter_pass(rows_here, halves, tab_ref, src_ref, out_ref, cols_ref, nexts_ref):
+    outer_count, channels, width = src_ref.shape
+    _, depth_here, _ = out_ref.shape
+    materials = channels // (halves * rows_here)
+    pieces = width // LANES
+    lane = lax.broadcasted_iota(jnp.int32, (channels, LANES), 1)
+    half_of = (lax.broadcasted_iota(jnp.int32, (channels, LANES), 0) // rows_here) % halves
+
+    def prepare(o, carry):
+        ys = [src_ref[o, :, k * LANES : (k + 1) * LANES] for k in range(pieces)]
+        cols = halo_columns(ys, lane, half_of, rows_here, halves, channels)
+        turned = [pltpu.roll(c, LANES - 1, 1) for c in cols]
+        nexts = [jnp.where(lane < LANES - 1, turned[k], turned[k + 1]) for k in range(pieces)]
+        nexts.append(turned[pieces])
+        for k in range(pieces + 1):
+            cols_ref[o, :, k * LANES : (k + 1) * LANES] = cols[k]
+            nexts_ref[o, :, k * LANES : (k + 1) * LANES] = nexts[k]
+        return carry
+
+    lax.fori_loop(0, outer_count, prepare, 0)
+    inner_count = tab_ref.shape[2]
+
+    for i in range(inner_count):
+        slab, level = divmod(i, depth_here)
+
+        def one_view(o, acc):
+            shift = tab_ref[0, o, i].astype(jnp.int32)
+            wa = tab_ref[2, o, i]
+            wb = tab_ref[1, o, i]
+            offset = HALO - 1 - shift
+            limit = LANES - offset
+            amount = jnp.where(limit == LANES, 0, limit)
+            mixed = [
+                wa * cols_ref[o, :, k * LANES : (k + 1) * LANES]
+                + wb * nexts_ref[o, :, k * LANES : (k + 1) * LANES]
+                for k in range(pieces + 1)
+            ]
+            rolled = [pltpu.roll(m, amount, 1) for m in mixed]
+            keep = lane < limit
+            return tuple(acc[j] + jnp.where(keep, rolled[j], rolled[j + 1]) for j in range(pieces))
+
+        zero = jnp.zeros((channels, LANES), jnp.float32)
+        acc = lax.fori_loop(0, outer_count, one_view, tuple(zero for _ in range(pieces)), unroll=True)
+        value = jnp.concatenate(acc, axis=1)
+        for c in range(channels):
+            material, rest = divmod(c, halves * rows_here)
+            half, row = divmod(rest, rows_here)
+            target = ((slab * halves + half) * rows_here + row) * materials + material
+            out_ref[target, level : level + 1, :] = value[c : c + 1, :]
+
+
 def forward_kernel(rows_here, halves, depth_all, views_all, tab_ref, emitted_ref, spectrum_ref,
                    attenuation_ref, src_ref, target_ref, out_ref, sums_ref, cols_ref, nexts_ref):
     shear_pass(True, rows_here, halves, tab_ref, src_ref, sums_ref, cols_ref, nexts_ref)
@@ -375,7 +426,7 @@
 
 
 def backward_kernel(rows_here, halves, tab_ref, src_ref, out_ref, cols_ref, nexts_ref):
-    shear_pass(False, rows_here, halves, tab_ref, src_ref, out_ref, cols_ref, nexts_ref)
+    scatter_pass(rows_here, halves, tab_ref, src_ref, out_ref, cols_ref, nexts_ref)
 
 
 def shear_apply(offset, wa, wb, src, out_width):
@@ -569,7 +620,7 @@
     )(table, emitted, spectrum, attenuation, mine, target)
     layers = pl.pallas_call(
         functools.partial(backward_kernel, rows_here, halves),
-        out_shape=jax.ShapeDtypeStruct((depth_all, channels, tile_width), jnp.float32),
+        out_shape=jax.ShapeDtypeStruct((parts * rows_here * materials, depth_here, tile_width), jnp.float32),
         in_specs=[smem, vmem],
         out_specs=vmem,
         scratch_shapes=[
@@ -578,10 +629,7 @@
         ],
         interpret=INTERPRET,
     )(table, grads)
-    layers = layers.reshape(depth_count, depth_here, materials, halves, rows_here, tile_width)
-    layers = jnp.transpose(layers, (0, 3, 4, 2, 1, 5)).reshape(
-        parts, rows_here, materials, depth_here, tile_width
-    )
+    layers = layers.reshape(parts, rows_here, materials, depth_here, tile_width)
     layers = lax.all_to_all(layers, ("depth", "lat"), 0, 0, tiled=True)
     return layers.reshape(rows_group, materials, depth_here, tile_width)
 

time: 62.2 us -> 60.5 us (0.973)
  local copies, waits for them, and re-layouts: 10.3 us -> 9.04 us
  Pallas kernels: 17.5 us -> 16.3 us
    reshape x2 -> x0, local copies, waits for them, and re-layouts: 1.27 us -> none  [per_device_wide(): layers.reshape(depth_count, depth_here, materials, halves, rows_here, til...]
    pallas_call x1, Pallas kernels: 6.64 us -> 5.5 us  [per_device_wide(): pl.pallas_call(functools.partial(backward_kernel, rows_here, halves), out...]
    all_to_all x1, blocking collectives: 12.4 us -> 13 us  [per_device_wide(): layers = lax.all_to_all(layers, ('depth', 'lat'), 0, 0, tiled=True)]
where the time goes in v11:
time: 60.5 us; the launch traced here: 60 us
  Pallas kernels  16.3 us (27%)
  blocking collectives  13 us (21%)
  waiting for transfers between devices  9.75 us (16%)
  starting transfers between devices  9.52 us (16%)
  local copies, waits for them, and re-layouts  9.04 us (15%)
  other arithmetic  1.51 us (2%)
  between operations  0.78 us (1%)
    all_to_all x1, blocking collectives, per_device_wide(): layers = lax.all_to_all(layers, ('depth', 'lat'), 0, 0, tiled=True)  13 us
    pallas_call x1, Pallas kernels, per_device_wide(): pl.pallas_call(functools.partial(forward_kernel, rows_here, halves, depth...  10.8 us
    all_to_all x1, waiting for transfers between devices, per_device_wide(): mine = lax.all_to_all(mine, ('views', 'depth', 'lat'), 0, 0, tiled=True)  7.75 us
    pallas_call x1, Pallas kernels, per_device_wide(): pl.pallas_call(functools.partial(backward_kernel, rows_here, halves), out...  5.5 us
    all_to_all x1, starting transfers between devices, per_device_wide(): observed = lax.all_to_all(observed, ('views', 'lat'), 0, 0, tiled=True)  5.2 us
    all_to_all x1, starting transfers between devices, per_device_wide(): mine = lax.all_to_all(mine, ('views', 'depth', 'lat'), 0, 0, tiled=True)  4.32 us
    all_to_all x1, waiting for transfers between devices, per_device_wide(): observed = lax.all_to_all(observed, ('views', 'lat'), 0, 0, tiled=True)  2 us
    unnamed x9, local copies, waits for them, and re-layouts  1.98 us
  transfers between devices with their start and end apart: 2, of which 2 were waited for; matrix products, arithmetic and copies ran while one was open for 6% of the time, Pallas kernels for 0%

profile of v11, /device:TPU:0, one launch (start us, length us, event | category | flops | bytes accessed | tf_op | source)
XLA Modules:
  0.0 60.0 jit_solution(4374082556585891221)
XLA Ops:
  0.0 1.3 %reshape.64 = f32[4,4,4,2,2,512]{5,4,3,2,1,0:T(2,128)S(1)} reshape(f32[4,64,512]{2,1,0:T(8,128)} %param.7) | data formatting | bytes 1048576 | tf_op jit(solution)/shard_map/reshape | solution.py:575
  1.3 0.0 copy-start
  1.4 0.7 %reshape.65 = f32[8,8,512]{2,1,0:T(8,128)} reshape(f32[4,2,4,2,512]{4,3,2,1,0:T(2,128)S(1)} %copy_bitcast_fusion.1) | data formatting | bytes 262144 | tf_op jit(solution)/shard_map/reshape | solution.py:577
  2.1 5.2 %all-to-all-start.1 = ((f32[8,8,512]{2,1,0:T(8,128)}), f32[8,8,512]{2,1,0:T(8,128)S(1)}, u32[]{:S(2)}, u32[]{:S(2)}) async-start(f32[8,8,512]{2,1,0:T(8,128)} %reshape.65), calls=%async_computation.1 | async-start | bytes 262144 | tf_op jit(solution)/shard_map/all_to_all | solution.py:580
  7.3 0.3 reshape.56
  7.7 0.8 %dynamic-slice_reduce_fusion = bf16[32,2048]{1,0:T(8,128)(2,1)S(1)} fusion(bf16[32,4,2048]{2,1,0:T(4,128)(2,1)S(1)} %reshape.56, s32[]{:T(128)S(6)} %select_n.8), kind=kLoop, calls=%fused_computation.2 | loop fusion | bytes 262148 | tf_op jit(solution)/shard_map/jit(dynamic_index_in_dim)/dynamic_slice | solution.py:587
  8.4 0.0 copy-start.2
  8.5 0.1 reshape.57
  8.5 0.6 copy-done.2
  9.1 0.7 %copy-done.1 = s32[4,4]{1,0:T(4,128)S(1)} copy-done((s32[4,4]{1,0:T(4,128)S(1)}, s32[4,4]{1,0:T(4,128)}, u32[]{:S(2)}) %copy-start.1) | copy-done | bytes 88
  9.8 0.1 reshape.58
  10.0 0.8 %pad_maximum_fusion = bf16[32,5,512]{2,1,0:T(8,128)(2,1)} fusion(bf16[32,1,512]{2,1,0:T(2,128)(2,1)S(1)} %broadcast_in_dim.9, bf16[32,4,512]{2,1,0:T(4,128)(2,1)S(1)} %reshape.57), kind=kLoop, calls=%fused_computation | loop fusion | flops 327680 | bytes 327680 | tf_op jit(solution)/shard_map/concatenate | solution.py:591
  10.8 2.0 %all-to-all-done.1 = f32[8,8,512]{2,1,0:T(8,128)S(1)} async-done(((f32[8,8,512]{2,1,0:T(8,128)}), f32[8,8,512]{2,1,0:T(8,128)S(1)}, u32[]{:S(2)}, u32[]{:S(2)}) %all-to-all-start.1) | async-done | bytes 131104 | tf_op jit(solution)/shard_map/all_to_all | solution.py:580
  12.8 4.3 %all-to-all-start = ((bf16[32,5,512]{2,1,0:T(8,128)(2,1)}), bf16[32,5,512]{2,1,0:T(8,128)(2,1)S(1)}, u32[]{:S(2)}, u32[]{:S(2)}) async-start(bf16[32,5,512]{2,1,0:T(8,128)(2,1)} %pad_maximum_fusion), calls=%async_computation | async-start | bytes 524288 | tf_op jit(solution)/shard_map/all_to_all | solution.py:592
  17.2 0.6 %reduce_sum.9 = f32[]{:T(128)} reduce(f32[64]{0:T(128)S(1)} %copy-done.3, f32[]{:T(128)} %constant.25.clone.1), dimensions={0}, to_apply=%region_0.1 | reduce | flops 63 | bytes 264 | tf_op jit(solution)/shard_map/reduce_sum | solution.py:606
  18.4 0.1 reshape.66
  18.5 0.1 copy.19
  18.6 0.1 copy.20
  18.7 0.7 %reshape.67.target_ref = f32[8,8,512]{2,1,0:T(8,128)} reshape(f32[8,2,2,2,512]{4,3,2,1,0:T(2,128)S(1)} %copy.20) | data formatting | bytes 262144 | tf_op jit(solution)/shard_map/reshape | solution.py:605
  19.4 7.8 %all-to-all-done = bf16[32,5,512]{2,1,0:T(8,128)(2,1)S(1)} async-done(((bf16[32,5,512]{2,1,0:T(8,128)(2,1)}), bf16[32,5,512]{2,1,0:T(8,128)(2,1)S(1)}, u32[]{:S(2)}, u32[]{:S(2)}) %all-to-all-start) | async-done | bytes 163872 | tf_op jit(solution)/shard_map/all_to_all | solution.py:592
  27.2 0.1 slice_convert_fusion
  27.3 0.1 reshape.75
  27.4 0.7 %reshape.71.tab_ref = f32[3,16,16]{2,1,0:T(8,128)} reshape(f32[3,4,4,4,4]{4,3,2,1,0:T(4,128)S(1)} %copy.15) | data formatting | bytes 6144 | tf_op jit(solution)/shard_map/reshape | solution.py:596
  28.1 0.3 reshape.78
  28.4 0.2 copy.27
  28.6 0.2 reshape.76
  28.8 0.2 copy.17
  29.0 0.9 %reshape.72.src_ref = f32[16,8,512]{2,1,0:T(8,128)} reshape(f32[4,4,2,2,2,512]{5,4,3,2,1,0:T(2,128)S(1)} %copy.17) | data formatting | bytes 524288 | tf_op jit(solution)/shard_map/convert_element_type | solution.py:603
  29.9 10.8 %shard_map.64.src_ref = f32[16,8,512]{2,1,0:T(8,128)} custom-call(f32[3,16,16]{2,1,0:T(8,128)} %reshape.71.tab_ref, f32[1]{0:T(128)} %bitcast.5.emitted_ref, f32[64]{0:T(128)} %spectrum_ref.1, f32[2,64]{1,0:T(2,128)} %attenuation_ref.1, f32[16,8,512]{2,1,0:T(8,128)} %reshape.72.src_ref, f32[8,8,512]{2,1,0:T(8,128)} %reshape.67.target_ref), custom_call_target="tpu_custom_call" | custom-call | tf_op jit(solution)/shard_map/pallas_call | solution.py:609
  40.7 5.5 %shard_map.65 = f32[32,4,512]{2,1,0:T(4,128)} custom-call(f32[3,16,16]{2,1,0:T(8,128)} %reshape.71.tab_ref, f32[16,8,512]{2,1,0:T(8,128)} %shard_map.64.src_ref), custom_call_target="tpu_custom_call" | custom-call | tf_op jit(solution)/shard_map/pallas_call | solution.py:621
  46.2 13.0 %all_to_all.15 = f32[8,2,2,4,512]{4,3,2,1,0:T(4,128)S(1)} all-to-all(f32[8,2,2,4,512]{4,3,2,1,0:T(4,128)} %bitcast.25), channel_id=1, replica_groups=mesh['views'=4,'depth'=4,'lat'=2] {'depth','lat'}, dimensions={0} | all-to-all | bytes 524288 | tf_op jit(solution)/shard_map/all_to_all | solution.py:633
  59.3 0.7 %copy.29 = f32[16,2,4,512]{3,2,1,0:T(4,128)} copy(f32[16,2,4,512]{3,2,1,0:T(4,128)S(1)} %bitcast.28) | data formatting | bytes 524288
  (13 shorter events, 0.2 us)
Async XLA Ops:
  1.3 6.0 %copy-start = (bf16[64,2,4,512]{3,2,1,0:T(4,128)(2,1)S(1)}, bf16[64,2,4,512]{3,2,1,0:T(4,128)(2,1)}, u32[]{:S(2)}) copy-start(bf16[64,2,4,512]{3,2,1,0:T(4,128)(2,1)} %param.6) | copy-start | bytes 1572868
  2.1 10.7 %all-to-all-start.1 = ((f32[8,8,512]{2,1,0:T(8,128)}), f32[8,8,512]{2,1,0:T(8,128)S(1)}, u32[]{:S(2)}, u32[]{:S(2)}) async-start(f32[8,8,512]{2,1,0:T(8,128)} %reshape.65), calls=%async_computation.1 | async-start | bytes 262144 | tf_op jit(solution)/shard_map/all_to_all | solution.py:580
  8.4 0.7 %copy-start.2 = (f32[4,4]{1,0:T(4,128)S(1)}, f32[4,4]{1,0:T(4,128)}, u32[]{:S(2)}) copy-start(f32[4,4]{1,0:T(4,128)} %param.9) | copy-start | bytes 196
  9.1 0.7 %copy-start.1 = (s32[4,4]{1,0:T(4,128)S(1)}, s32[4,4]{1,0:T(4,128)}, u32[]{:S(2)}) copy-start(s32[4,4]{1,0:T(4,128)} %param.8) | copy-start | bytes 196
  10.8 6.3 %copy-start.3 = (f32[64]{0:T(128)S(1)}, f32[64]{0:T(128)}, u32[]{:S(2)}) copy-start(f32[64]{0:T(128)} %spectrum_ref.1) | copy-start | bytes 772
  12.8 14.3 %all-to-all-start = ((bf16[32,5,512]{2,1,0:T(8,128)(2,1)}), bf16[32,5,512]{2,1,0:T(8,128)(2,1)S(1)}, u32[]{:S(2)}, u32[]{:S(2)}) async-start(bf16[32,5,512]{2,1,0:T(8,128)(2,1)} %pad_maximum_fusion), calls=%async_computation | async-start | bytes 524288 | tf_op jit(solution)/shard_map/all_to_all | solution.py:592

commit v12 on v11

--- a/solution.py
+++ b/solution.py
@@ -310,9 +310,9 @@
 
     lax.fori_loop(0, outer_count, prepare, 0)
 
-    def inner(i, carry):
-        acc = [jnp.zeros((channels, LANES), jnp.float32) for _ in range(pieces)]
-        for o in range(outer_count):
+    for i in range(inner_count):
+
+        def one_input(o, acc):
             if forward:
                 shift = tab_ref[0, i, o].astype(jnp.int32)
                 wa = tab_ref[1, i, o]
@@ -332,12 +332,12 @@
             ]
             rolled = [pltpu.roll(m, amount, 1) for m in mixed]
             keep = lane < limit
-            acc = [acc[j] + jnp.where(keep, rolled[j], rolled[j + 1]) for j in range(pieces)]
+            return tuple(acc[j] + jnp.where(keep, rolled[j], rolled[j + 1]) for j in range(pieces))
+
+        zero = jnp.zeros((channels, LANES), jnp.float32)
+        acc = lax.fori_loop(0, outer_count, one_input, tuple(zero for _ in range(pieces)), unroll=True)
         for j in range(pieces):
             acc_ref[i, :, j * LANES : (j + 1) * LANES] = acc[j]
-        return carry
-
-    lax.fori_loop(0, inner_count, inner, 0)
 
 
 def scatter_pass(rows_here, halves, tab_ref, src_ref, out_ref, cols_ref, nexts_ref):

time: 60.5 us -> 59.3 us (0.980)
  Pallas kernels: 16.3 us -> 15.2 us
    pallas_call x1, Pallas kernels: 10.8 us -> 9.69 us  [per_device_wide(): pl.pallas_call(functools.partial(forward_kernel, rows_here, halves, depth...]
where the time goes in v12:
time: 59.3 us; the launch traced here: 58.8 us
  Pallas kernels  15.2 us (26%)
  blocking collectives  13 us (22%)
  waiting for transfers between devices  9.75 us (16%)
  starting transfers between devices  9.52 us (16%)
  local copies, waits for them, and re-layouts  9.04 us (15%)
  other arithmetic  1.51 us (3%)
  between operations  0.78 us (1%)
    all_to_all x1, blocking collectives, per_device_wide(): layers = lax.all_to_all(layers, ('depth', 'lat'), 0, 0, tiled=True)  13 us
    pallas_call x1, Pallas kernels, per_device_wide(): pl.pallas_call(functools.partial(forward_kernel, rows_here, halves, depth...  9.69 us
    all_to_all x1, waiting for transfers between devices, per_device_wide(): mine = lax.all_to_all(mine, ('views', 'depth', 'lat'), 0, 0, tiled=True)  7.75 us
    pallas_call x1, Pallas kernels, per_device_wide(): pl.pallas_call(functools.partial(backward_kernel, rows_here, halves), out...  5.5 us
    all_to_all x1, starting transfers between devices, per_device_wide(): observed = lax.all_to_all(observed, ('views', 'lat'), 0, 0, tiled=True)  5.2 us
    all_to_all x1, starting transfers between devices, per_device_wide(): mine = lax.all_to_all(mine, ('views', 'depth', 'lat'), 0, 0, tiled=True)  4.32 us
    all_to_all x1, waiting for transfers between devices, per_device_wide(): observed = lax.all_to_all(observed, ('views', 'lat'), 0, 0, tiled=True)  2 us
    unnamed x9, local copies, waits for them, and re-layouts  1.98 us
  transfers between devices with their start and end apart: 2, of which 2 were waited for; matrix products, arithmetic and copies ran while one was open for 6% of the time, Pallas kernels for 0%

profile of v12, /device:TPU:0, one launch (start us, length us, event | category | flops | bytes accessed | tf_op | source)
XLA Modules:
  0.0 58.8 jit_solution(4235489374131927602)
XLA Ops:
  0.0 1.3 %reshape.64 = f32[4,4,4,2,2,512]{5,4,3,2,1,0:T(2,128)S(1)} reshape(f32[4,64,512]{2,1,0:T(8,128)} %param.7) | data formatting | bytes 1048576 | tf_op jit(solution)/shard_map/reshape | solution.py:575
  1.3 0.0 copy-start
  1.4 0.7 %reshape.65 = f32[8,8,512]{2,1,0:T(8,128)} reshape(f32[4,2,4,2,512]{4,3,2,1,0:T(2,128)S(1)} %copy_bitcast_fusion.1) | data formatting | bytes 262144 | tf_op jit(solution)/shard_map/reshape | solution.py:577
  2.1 5.2 %all-to-all-start.1 = ((f32[8,8,512]{2,1,0:T(8,128)}), f32[8,8,512]{2,1,0:T(8,128)S(1)}, u32[]{:S(2)}, u32[]{:S(2)}) async-start(f32[8,8,512]{2,1,0:T(8,128)} %reshape.65), calls=%async_computation.1 | async-start | bytes 262144 | tf_op jit(solution)/shard_map/all_to_all | solution.py:580
  7.3 0.3 reshape.56
  7.7 0.8 %dynamic-slice_reduce_fusion = bf16[32,2048]{1,0:T(8,128)(2,1)S(1)} fusion(bf16[32,4,2048]{2,1,0:T(4,128)(2,1)S(1)} %reshape.56, s32[]{:T(128)S(6)} %select_n.8), kind=kLoop, calls=%fused_computation.2 | loop fusion | bytes 262148 | tf_op jit(solution)/shard_map/jit(dynamic_index_in_dim)/dynamic_slice | solution.py:587
  8.4 0.0 copy-start.2
  8.5 0.1 reshape.57
  8.5 0.6 %copy-done.2 = f32[4,4]{1,0:T(4,128)S(1)} copy-done((f32[4,4]{1,0:T(4,128)S(1)}, f32[4,4]{1,0:T(4,128)}, u32[]{:S(2)}) %copy-start.2) | copy-done | bytes 88
  9.1 0.7 %copy-done.1 = s32[4,4]{1,0:T(4,128)S(1)} copy-done((s32[4,4]{1,0:T(4,128)S(1)}, s32[4,4]{1,0:T(4,128)}, u32[]{:S(2)}) %copy-start.1) | copy-done | bytes 88
  9.8 0.1 reshape.58
  10.0 0.8 %pad_maximum_fusion = bf16[32,5,512]{2,1,0:T(8,128)(2,1)} fusion(bf16[32,1,512]{2,1,0:T(2,128)(2,1)S(1)} %broadcast_in_dim.9, bf16[32,4,512]{2,1,0:T(4,128)(2,1)S(1)} %reshape.57), kind=kLoop, calls=%fused_computation | loop fusion | flops 327680 | bytes 327680 | tf_op jit(solution)/shard_map/concatenate | solution.py:591
  10.8 2.0 %all-to-all-done.1 = f32[8,8,512]{2,1,0:T(8,128)S(1)} async-done(((f32[8,8,512]{2,1,0:T(8,128)}), f32[8,8,512]{2,1,0:T(8,128)S(1)}, u32[]{:S(2)}, u32[]{:S(2)}) %all-to-all-start.1) | async-done | bytes 131104 | tf_op jit(solution)/shard_map/all_to_all | solution.py:580
  12.8 4.3 %all-to-all-start = ((bf16[32,5,512]{2,1,0:T(8,128)(2,1)}), bf16[32,5,512]{2,1,0:T(8,128)(2,1)S(1)}, u32[]{:S(2)}, u32[]{:S(2)}) async-start(bf16[32,5,512]{2,1,0:T(8,128)(2,1)} %pad_maximum_fusion), calls=%async_computation | async-start | bytes 524288 | tf_op jit(solution)/shard_map/all_to_all | solution.py:592
  17.2 0.6 %reduce_sum.9 = f32[]{:T(128)} reduce(f32[64]{0:T(128)S(1)} %copy-done.3, f32[]{:T(128)} %constant.25.clone.1), dimensions={0}, to_apply=%region_0.1 | reduce | flops 63 | bytes 264 | tf_op jit(solution)/shard_map/reduce_sum | solution.py:606
  18.4 0.1 reshape.66
  18.5 0.1 copy.19
  18.6 0.1 copy.20
  18.7 0.7 %reshape.67.target_ref = f32[8,8,512]{2,1,0:T(8,128)} reshape(f32[8,2,2,2,512]{4,3,2,1,0:T(2,128)S(1)} %copy.20) | data formatting | bytes 262144 | tf_op jit(solution)/shard_map/reshape | solution.py:605
  19.4 7.8 %all-to-all-done = bf16[32,5,512]{2,1,0:T(8,128)(2,1)S(1)} async-done(((bf16[32,5,512]{2,1,0:T(8,128)(2,1)}), bf16[32,5,512]{2,1,0:T(8,128)(2,1)S(1)}, u32[]{:S(2)}, u32[]{:S(2)}) %all-to-all-start) | async-done | bytes 163872 | tf_op jit(solution)/shard_map/all_to_all | solution.py:592
  27.2 0.1 slice_convert_fusion
  27.3 0.1 reshape.75
  27.4 0.7 %reshape.71.tab_ref = f32[3,16,16]{2,1,0:T(8,128)} reshape(f32[3,4,4,4,4]{4,3,2,1,0:T(4,128)S(1)} %copy.15) | data formatting | bytes 6144 | tf_op jit(solution)/shard_map/reshape | solution.py:596
  28.1 0.3 reshape.78
  28.4 0.2 copy.27
  28.6 0.2 reshape.76
  28.8 0.2 copy.17
  29.0 0.9 %reshape.72.src_ref = f32[16,8,512]{2,1,0:T(8,128)} reshape(f32[4,4,2,2,2,512]{5,4,3,2,1,0:T(2,128)S(1)} %copy.17) | data formatting | bytes 524288 | tf_op jit(solution)/shard_map/convert_element_type | solution.py:603
  29.9 9.7 %shard_map.64.src_ref = f32[16,8,512]{2,1,0:T(8,128)} custom-call(f32[3,16,16]{2,1,0:T(8,128)} %reshape.71.tab_ref, f32[1]{0:T(128)} %bitcast.5.emitted_ref, f32[64]{0:T(128)} %spectrum_ref.1, f32[2,64]{1,0:T(2,128)} %attenuation_ref.1, f32[16,8,512]{2,1,0:T(8,128)} %reshape.72.src_ref, f32[8,8,512]{2,1,0:T(8,128)} %reshape.67.target_ref), custom_call_target="tpu_custom_call" | custom-call | tf_op jit(solution)/shard_map/pallas_call | solution.py:609
  39.6 5.5 %shard_map.65 = f32[32,4,512]{2,1,0:T(4,128)} custom-call(f32[3,16,16]{2,1,0:T(8,128)} %reshape.71.tab_ref, f32[16,8,512]{2,1,0:T(8,128)} %shard_map.64.src_ref), custom_call_target="tpu_custom_call" | custom-call | tf_op jit(solution)/shard_map/pallas_call | solution.py:621
  45.1 13.0 %all_to_all.15 = f32[8,2,2,4,512]{4,3,2,1,0:T(4,128)S(1)} all-to-all(f32[8,2,2,4,512]{4,3,2,1,0:T(4,128)} %bitcast.25), channel_id=1, replica_groups=mesh['views'=4,'depth'=4,'lat'=2] {'depth','lat'}, dimensions={0} | all-to-all | bytes 524288 | tf_op jit(solution)/shard_map/all_to_all | solution.py:633
  58.1 0.7 %copy.29 = f32[16,2,4,512]{3,2,1,0:T(4,128)} copy(f32[16,2,4,512]{3,2,1,0:T(4,128)S(1)} %bitcast.28) | data formatting | bytes 524288
  (13 shorter events, 0.2 us)
Async XLA Ops:
  1.3 6.0 %copy-start = (bf16[64,2,4,512]{3,2,1,0:T(4,128)(2,1)S(1)}, bf16[64,2,4,512]{3,2,1,0:T(4,128)(2,1)}, u32[]{:S(2)}) copy-start(bf16[64,2,4,512]{3,2,1,0:T(4,128)(2,1)} %param.6) | copy-start | bytes 1572868
  2.1 10.7 %all-to-all-start.1 = ((f32[8,8,512]{2,1,0:T(8,128)}), f32[8,8,512]{2,1,0:T(8,128)S(1)}, u32[]{:S(2)}, u32[]{:S(2)}) async-start(f32[8,8,512]{2,1,0:T(8,128)} %reshape.65), calls=%async_computation.1 | async-start | bytes 262144 | tf_op jit(solution)/shard_map/all_to_all | solution.py:580
  8.4 0.7 %copy-start.2 = (f32[4,4]{1,0:T(4,128)S(1)}, f32[4,4]{1,0:T(4,128)}, u32[]{:S(2)}) copy-start(f32[4,4]{1,0:T(4,128)} %param.9) | copy-start | bytes 196
  9.1 0.7 %copy-start.1 = (s32[4,4]{1,0:T(4,128)S(1)}, s32[4,4]{1,0:T(4,128)}, u32[]{:S(2)}) copy-start(s32[4,4]{1,0:T(4,128)} %param.8) | copy-start | bytes 196
  10.8 6.3 %copy-start.3 = (f32[64]{0:T(128)S(1)}, f32[64]{0:T(128)}, u32[]{:S(2)}) copy-start(f32[64]{0:T(128)} %spectrum_ref.1) | copy-start | bytes 772
  12.8 14.3 %all-to-all-start = ((bf16[32,5,512]{2,1,0:T(8,128)(2,1)}), bf16[32,5,512]{2,1,0:T(8,128)(2,1)S(1)}, u32[]{:S(2)}, u32[]{:S(2)}) async-start(bf16[32,5,512]{2,1,0:T(8,128)(2,1)} %pad_maximum_fusion), calls=%async_computation | async-start | bytes 524288 | tf_op jit(solution)/shard_map/all_to_all | solution.py:592

commit v13 on v12

--- a/solution.py
+++ b/solution.py
@@ -413,7 +413,7 @@
             return (intensity + counts, first + a0 * counts, second + a1 * counts)
 
         zero = jnp.zeros((channels, width), jnp.float32)
-        intensity, first, second = lax.fori_loop(0, energies, one_energy, (zero, zero, zero), unroll=8)
+        intensity, first, second = lax.fori_loop(0, energies, one_energy, (zero, zero, zero), unroll=True)
         residual = emitted_ref[0] - jnp.log(intensity) - target_ref[p]
         factor = residual / intensity / views_all
         first = (first * factor).astype(jnp.bfloat16).astype(jnp.float32)

time: 59.3 us -> 58.8 us (level)
  no operation moved by 1% of the time
where the time goes in v13:
time: 58.8 us; the launch traced here: 58.3 us
  Pallas kernels  14.7 us (25%)
  blocking collectives  13 us (22%)
  waiting for transfers between devices  9.75 us (17%)
  starting transfers between devices  9.52 us (16%)
  local copies, waits for them, and re-layouts  9.04 us (15%)
  other arithmetic  1.51 us (3%)
  between operations  0.78 us (1%)
    all_to_all x1, blocking collectives, per_device_wide(): layers = lax.all_to_all(layers, ('depth', 'lat'), 0, 0, tiled=True)  13 us
    pallas_call x1, Pallas kernels, per_device_wide(): pl.pallas_call(functools.partial(forward_kernel, rows_here, halves, depth...  9.19 us
    all_to_all x1, waiting for transfers between devices, per_device_wide(): mine = lax.all_to_all(mine, ('views', 'depth', 'lat'), 0, 0, tiled=True)  7.75 us
    pallas_call x1, Pallas kernels, per_device_wide(): pl.pallas_call(functools.partial(backward_kernel, rows_here, halves), out...  5.5 us
    all_to_all x1, starting transfers between devices, per_device_wide(): observed = lax.all_to_all(observed, ('views', 'lat'), 0, 0, tiled=True)  5.2 us
    all_to_all x1, starting transfers between devices, per_device_wide(): mine = lax.all_to_all(mine, ('views', 'depth', 'lat'), 0, 0, tiled=True)  4.32 us
    all_to_all x1, waiting for transfers between devices, per_device_wide(): observed = lax.all_to_all(observed, ('views', 'lat'), 0, 0, tiled=True)  2 us
    unnamed x9, local copies, waits for them, and re-layouts  1.98 us
  transfers between devices with their start and end apart: 2, of which 2 were waited for; matrix products, arithmetic and copies ran while one was open for 6% of the time, Pallas kernels for 0%

profile of v13, /device:TPU:0, one launch (start us, length us, event | category | flops | bytes accessed | tf_op | source)
XLA Modules:
  0.0 58.3 jit_solution(7957831936994947879)
XLA Ops:
  0.0 1.3 %reshape.64 = f32[4,4,4,2,2,512]{5,4,3,2,1,0:T(2,128)S(1)} reshape(f32[4,64,512]{2,1,0:T(8,128)} %param.7) | data formatting | bytes 1048576 | tf_op jit(solution)/shard_map/reshape | solution.py:575
  1.3 0.0 copy-start
  1.4 0.7 %reshape.65 = f32[8,8,512]{2,1,0:T(8,128)} reshape(f32[4,2,4,2,512]{4,3,2,1,0:T(2,128)S(1)} %copy_bitcast_fusion.1) | data formatting | bytes 262144 | tf_op jit(solution)/shard_map/reshape | solution.py:577
  2.1 5.2 %all-to-all-start.1 = ((f32[8,8,512]{2,1,0:T(8,128)}), f32[8,8,512]{2,1,0:T(8,128)S(1)}, u32[]{:S(2)}, u32[]{:S(2)}) async-start(f32[8,8,512]{2,1,0:T(8,128)} %reshape.65), calls=%async_computation.1 | async-start | bytes 262144 | tf_op jit(solution)/shard_map/all_to_all | solution.py:580
  7.3 0.3 reshape.56
  7.7 0.8 %dynamic-slice_reduce_fusion = bf16[32,2048]{1,0:T(8,128)(2,1)S(1)} fusion(bf16[32,4,2048]{2,1,0:T(4,128)(2,1)S(1)} %reshape.56, s32[]{:T(128)S(6)} %select_n.8), kind=kLoop, calls=%fused_computation.2 | loop fusion | bytes 262148 | tf_op jit(solution)/shard_map/jit(dynamic_index_in_dim)/dynamic_slice | solution.py:587
  8.4 0.0 copy-start.2
  8.5 0.1 reshape.57
  8.5 0.6 %copy-done.2 = f32[4,4]{1,0:T(4,128)S(1)} copy-done((f32[4,4]{1,0:T(4,128)S(1)}, f32[4,4]{1,0:T(4,128)}, u32[]{:S(2)}) %copy-start.2) | copy-done | bytes 88
  9.1 0.7 %copy-done.1 = s32[4,4]{1,0:T(4,128)S(1)} copy-done((s32[4,4]{1,0:T(4,128)S(1)}, s32[4,4]{1,0:T(4,128)}, u32[]{:S(2)}) %copy-start.1) | copy-done | bytes 88
  9.8 0.1 reshape.58
  10.0 0.8 %pad_maximum_fusion = bf16[32,5,512]{2,1,0:T(8,128)(2,1)} fusion(bf16[32,1,512]{2,1,0:T(2,128)(2,1)S(1)} %broadcast_in_dim.9, bf16[32,4,512]{2,1,0:T(4,128)(2,1)S(1)} %reshape.57), kind=kLoop, calls=%fused_computation | loop fusion | flops 327680 | bytes 327680 | tf_op jit(solution)/shard_map/concatenate | solution.py:591
  10.8 2.0 %all-to-all-done.1 = f32[8,8,512]{2,1,0:T(8,128)S(1)} async-done(((f32[8,8,512]{2,1,0:T(8,128)}), f32[8,8,512]{2,1,0:T(8,128)S(1)}, u32[]{:S(2)}, u32[]{:S(2)}) %all-to-all-start.1) | async-done | bytes 131104 | tf_op jit(solution)/shard_map/all_to_all | solution.py:580
  12.8 4.3 %all-to-all-start = ((bf16[32,5,512]{2,1,0:T(8,128)(2,1)}), bf16[32,5,512]{2,1,0:T(8,128)(2,1)S(1)}, u32[]{:S(2)}, u32[]{:S(2)}) async-start(bf16[32,5,512]{2,1,0:T(8,128)(2,1)} %pad_maximum_fusion), calls=%async_computation | async-start | bytes 524288 | tf_op jit(solution)/shard_map/all_to_all | solution.py:592
  17.2 0.6 %reduce_sum.9 = f32[]{:T(128)} reduce(f32[64]{0:T(128)S(1)} %copy-done.3, f32[]{:T(128)} %constant.25.clone.1), dimensions={0}, to_apply=%region_0.1 | reduce | flops 63 | bytes 264 | tf_op jit(solution)/shard_map/reduce_sum | solution.py:606
  18.4 0.1 reshape.66
  18.5 0.1 copy.19
  18.6 0.1 copy.20
  18.7 0.7 %reshape.67.target_ref = f32[8,8,512]{2,1,0:T(8,128)} reshape(f32[8,2,2,2,512]{4,3,2,1,0:T(2,128)S(1)} %copy.20) | data formatting | bytes 262144 | tf_op jit(solution)/shard_map/reshape | solution.py:605
  19.4 7.8 %all-to-all-done = bf16[32,5,512]{2,1,0:T(8,128)(2,1)S(1)} async-done(((bf16[32,5,512]{2,1,0:T(8,128)(2,1)}), bf16[32,5,512]{2,1,0:T(8,128)(2,1)S(1)}, u32[]{:S(2)}, u32[]{:S(2)}) %all-to-all-start) | async-done | bytes 163872 | tf_op jit(solution)/shard_map/all_to_all | solution.py:592
  27.2 0.1 slice_convert_fusion
  27.3 0.1 reshape.75
  27.4 0.7 %reshape.71.tab_ref = f32[3,16,16]{2,1,0:T(8,128)} reshape(f32[3,4,4,4,4]{4,3,2,1,0:T(4,128)S(1)} %copy.15) | data formatting | bytes 6144 | tf_op jit(solution)/shard_map/reshape | solution.py:596
  28.1 0.3 reshape.78
  28.4 0.2 copy.27
  28.6 0.2 reshape.76
  28.8 0.2 copy.17
  29.0 0.9 %reshape.72.src_ref = f32[16,8,512]{2,1,0:T(8,128)} reshape(f32[4,4,2,2,2,512]{5,4,3,2,1,0:T(2,128)S(1)} %copy.17) | data formatting | bytes 524288 | tf_op jit(solution)/shard_map/convert_element_type | solution.py:603
  29.9 9.2 %shard_map.64.src_ref = f32[16,8,512]{2,1,0:T(8,128)} custom-call(f32[3,16,16]{2,1,0:T(8,128)} %reshape.71.tab_ref, f32[1]{0:T(128)} %bitcast.5.emitted_ref, f32[64]{0:T(128)} %spectrum_ref.1, f32[2,64]{1,0:T(2,128)} %attenuation_ref.1, f32[16,8,512]{2,1,0:T(8,128)} %reshape.72.src_ref, f32[8,8,512]{2,1,0:T(8,128)} %reshape.67.target_ref), custom_call_target="tpu_custom_call" | custom-call | tf_op jit(solution)/shard_map/pallas_call | solution.py:609
  39.1 5.5 %shard_map.65 = f32[32,4,512]{2,1,0:T(4,128)} custom-call(f32[3,16,16]{2,1,0:T(8,128)} %reshape.71.tab_ref, f32[16,8,512]{2,1,0:T(8,128)} %shard_map.64.src_ref), custom_call_target="tpu_custom_call" | custom-call | tf_op jit(solution)/shard_map/pallas_call | solution.py:621
  44.6 13.0 %all_to_all.15 = f32[8,2,2,4,512]{4,3,2,1,0:T(4,128)S(1)} all-to-all(f32[8,2,2,4,512]{4,3,2,1,0:T(4,128)} %bitcast.25), channel_id=1, replica_groups=mesh['views'=4,'depth'=4,'lat'=2] {'depth','lat'}, dimensions={0} | all-to-all | bytes 524288 | tf_op jit(solution)/shard_map/all_to_all | solution.py:633
  57.6 0.7 %copy.29 = f32[16,2,4,512]{3,2,1,0:T(4,128)} copy(f32[16,2,4,512]{3,2,1,0:T(4,128)S(1)} %bitcast.28) | data formatting | bytes 524288
  (13 shorter events, 0.2 us)
Async XLA Ops:
  1.3 6.0 %copy-start = (bf16[64,2,4,512]{3,2,1,0:T(4,128)(2,1)S(1)}, bf16[64,2,4,512]{3,2,1,0:T(4,128)(2,1)}, u32[]{:S(2)}) copy-start(bf16[64,2,4,512]{3,2,1,0:T(4,128)(2,1)} %param.6) | copy-start | bytes 1572868
  2.1 10.7 %all-to-all-start.1 = ((f32[8,8,512]{2,1,0:T(8,128)}), f32[8,8,512]{2,1,0:T(8,128)S(1)}, u32[]{:S(2)}, u32[]{:S(2)}) async-start(f32[8,8,512]{2,1,0:T(8,128)} %reshape.65), calls=%async_computation.1 | async-start | bytes 262144 | tf_op jit(solution)/shard_map/all_to_all | solution.py:580
  8.4 0.7 %copy-start.2 = (f32[4,4]{1,0:T(4,128)S(1)}, f32[4,4]{1,0:T(4,128)}, u32[]{:S(2)}) copy-start(f32[4,4]{1,0:T(4,128)} %param.9) | copy-start | bytes 196
  9.1 0.7 %copy-start.1 = (s32[4,4]{1,0:T(4,128)S(1)}, s32[4,4]{1,0:T(4,128)}, u32[]{:S(2)}) copy-start(s32[4,4]{1,0:T(4,128)} %param.8) | copy-start | bytes 196
  10.8 6.3 %copy-start.3 = (f32[64]{0:T(128)S(1)}, f32[64]{0:T(128)}, u32[]{:S(2)}) copy-start(f32[64]{0:T(128)} %spectrum_ref.1) | copy-start | bytes 772
  12.8 14.3 %all-to-all-start = ((bf16[32,5,512]{2,1,0:T(8,128)(2,1)}), bf16[32,5,512]{2,1,0:T(8,128)(2,1)S(1)}, u32[]{:S(2)}, u32[]{:S(2)}) async-start(bf16[32,5,512]{2,1,0:T(8,128)(2,1)} %pad_maximum_fusion), calls=%async_computation | async-start | bytes 524288 | tf_op jit(solution)/shard_map/all_to_all | solution.py:592

commit v14 on v13

--- a/solution.py
+++ b/solution.py
@@ -409,7 +409,7 @@
             intensity, first, second = sums
             a0 = attenuation_ref[0, e]
             a1 = attenuation_ref[1, e]
-            counts = spectrum_ref[e] * jnp.exp(-(a0 * water + a1 * bone))
+            counts = spectrum_ref[e] * jnp.exp((-a0) * water + (-a1) * bone)
             return (intensity + counts, first + a0 * counts, second + a1 * counts)
 
         zero = jnp.zeros((channels, width), jnp.float32)

time: 58.8 us -> 58.7 us (level)
  no operation moved by 1% of the time
where the time goes in v14:
time: 58.7 us; the launch traced here: 58.2 us
  Pallas kernels  14.6 us (25%)
  blocking collectives  13 us (22%)
  waiting for transfers between devices  9.75 us (17%)
  starting transfers between devices  9.52 us (16%)
  local copies, waits for them, and re-layouts  9.04 us (15%)
  other arithmetic  1.51 us (3%)
  between operations  0.78 us (1%)
    all_to_all x1, blocking collectives, per_device_wide(): layers = lax.all_to_all(layers, ('depth', 'lat'), 0, 0, tiled=True)  13 us
    pallas_call x1, Pallas kernels, per_device_wide(): pl.pallas_call(functools.partial(forward_kernel, rows_here, halves, depth...  9.06 us
    all_to_all x1, waiting for transfers between devices, per_device_wide(): mine = lax.all_to_all(mine, ('views', 'depth', 'lat'), 0, 0, tiled=True)  7.75 us
    pallas_call x1, Pallas kernels, per_device_wide(): pl.pallas_call(functools.partial(backward_kernel, rows_here, halves), out...  5.5 us
    all_to_all x1, starting transfers between devices, per_device_wide(): observed = lax.all_to_all(observed, ('views', 'lat'), 0, 0, tiled=True)  5.2 us
    all_to_all x1, starting transfers between devices, per_device_wide(): mine = lax.all_to_all(mine, ('views', 'depth', 'lat'), 0, 0, tiled=True)  4.32 us
    all_to_all x1, waiting for transfers between devices, per_device_wide(): observed = lax.all_to_all(observed, ('views', 'lat'), 0, 0, tiled=True)  2 us
    unnamed x9, local copies, waits for them, and re-layouts  1.98 us
  transfers between devices with their start and end apart: 2, of which 2 were waited for; matrix products, arithmetic and copies ran while one was open for 6% of the time, Pallas kernels for 0%

profile of v14, /device:TPU:0, one launch (start us, length us, event | category | flops | bytes accessed | tf_op | source)
XLA Modules:
  0.0 58.2 jit_solution(1938864009236244891)
XLA Ops:
  0.0 1.3 %reshape.64 = f32[4,4,4,2,2,512]{5,4,3,2,1,0:T(2,128)S(1)} reshape(f32[4,64,512]{2,1,0:T(8,128)} %param.7) | data formatting | bytes 1048576 | tf_op jit(solution)/shard_map/reshape | solution.py:575
  1.3 0.0 copy-start
  1.4 0.7 %reshape.65 = f32[8,8,512]{2,1,0:T(8,128)} reshape(f32[4,2,4,2,512]{4,3,2,1,0:T(2,128)S(1)} %copy_bitcast_fusion.1) | data formatting | bytes 262144 | tf_op jit(solution)/shard_map/reshape | solution.py:577
  2.1 5.2 %all-to-all-start.1 = ((f32[8,8,512]{2,1,0:T(8,128)}), f32[8,8,512]{2,1,0:T(8,128)S(1)}, u32[]{:S(2)}, u32[]{:S(2)}) async-start(f32[8,8,512]{2,1,0:T(8,128)} %reshape.65), calls=%async_computation.1 | async-start | bytes 262144 | tf_op jit(solution)/shard_map/all_to_all | solution.py:580
  7.3 0.3 reshape.56
  7.7 0.8 %dynamic-slice_reduce_fusion = bf16[32,2048]{1,0:T(8,128)(2,1)S(1)} fusion(bf16[32,4,2048]{2,1,0:T(4,128)(2,1)S(1)} %reshape.56, s32[]{:T(128)S(6)} %select_n.8), kind=kLoop, calls=%fused_computation.2 | loop fusion | bytes 262148 | tf_op jit(solution)/shard_map/jit(dynamic_index_in_dim)/dynamic_slice | solution.py:587
  8.4 0.0 copy-start.2
  8.5 0.1 reshape.57
  8.5 0.6 %copy-done.2 = f32[4,4]{1,0:T(4,128)S(1)} copy-done((f32[4,4]{1,0:T(4,128)S(1)}, f32[4,4]{1,0:T(4,128)}, u32[]{:S(2)}) %copy-start.2) | copy-done | bytes 88
  9.1 0.7 %copy-done.1 = s32[4,4]{1,0:T(4,128)S(1)} copy-done((s32[4,4]{1,0:T(4,128)S(1)}, s32[4,4]{1,0:T(4,128)}, u32[]{:S(2)}) %copy-start.1) | copy-done | bytes 88
  9.8 0.1 reshape.58
  10.0 0.8 %pad_maximum_fusion = bf16[32,5,512]{2,1,0:T(8,128)(2,1)} fusion(bf16[32,1,512]{2,1,0:T(2,128)(2,1)S(1)} %broadcast_in_dim.9, bf16[32,4,512]{2,1,0:T(4,128)(2,1)S(1)} %reshape.57), kind=kLoop, calls=%fused_computation | loop fusion | flops 327680 | bytes 327680 | tf_op jit(solution)/shard_map/concatenate | solution.py:591
  10.8 2.0 %all-to-all-done.1 = f32[8,8,512]{2,1,0:T(8,128)S(1)} async-done(((f32[8,8,512]{2,1,0:T(8,128)}), f32[8,8,512]{2,1,0:T(8,128)S(1)}, u32[]{:S(2)}, u32[]{:S(2)}) %all-to-all-start.1) | async-done | bytes 131104 | tf_op jit(solution)/shard_map/all_to_all | solution.py:580
  12.8 4.3 %all-to-all-start = ((bf16[32,5,512]{2,1,0:T(8,128)(2,1)}), bf16[32,5,512]{2,1,0:T(8,128)(2,1)S(1)}, u32[]{:S(2)}, u32[]{:S(2)}) async-start(bf16[32,5,512]{2,1,0:T(8,128)(2,1)} %pad_maximum_fusion), calls=%async_computation | async-start | bytes 524288 | tf_op jit(solution)/shard_map/all_to_all | solution.py:592
  17.2 0.6 %reduce_sum.9 = f32[]{:T(128)} reduce(f32[64]{0:T(128)S(1)} %copy-done.3, f32[]{:T(128)} %constant.25.clone.1), dimensions={0}, to_apply=%region_0.1 | reduce | flops 63 | bytes 264 | tf_op jit(solution)/shard_map/reduce_sum | solution.py:606
  18.4 0.1 reshape.66
  18.5 0.1 copy.19
  18.6 0.1 copy.20
  18.7 0.7 %reshape.67.target_ref = f32[8,8,512]{2,1,0:T(8,128)} reshape(f32[8,2,2,2,512]{4,3,2,1,0:T(2,128)S(1)} %copy.20) | data formatting | bytes 262144 | tf_op jit(solution)/shard_map/reshape | solution.py:605
  19.4 7.8 %all-to-all-done = bf16[32,5,512]{2,1,0:T(8,128)(2,1)S(1)} async-done(((bf16[32,5,512]{2,1,0:T(8,128)(2,1)}), bf16[32,5,512]{2,1,0:T(8,128)(2,1)S(1)}, u32[]{:S(2)}, u32[]{:S(2)}) %all-to-all-start) | async-done | bytes 163872 | tf_op jit(solution)/shard_map/all_to_all | solution.py:592
  27.2 0.1 slice_convert_fusion
  27.3 0.1 reshape.75
  27.4 0.7 %reshape.71.tab_ref = f32[3,16,16]{2,1,0:T(8,128)} reshape(f32[3,4,4,4,4]{4,3,2,1,0:T(4,128)S(1)} %copy.15) | data formatting | bytes 6144 | tf_op jit(solution)/shard_map/reshape | solution.py:596
  28.1 0.3 reshape.78
  28.4 0.2 copy.27
  28.6 0.2 reshape.76
  28.8 0.2 copy.17
  29.0 0.9 %reshape.72.src_ref = f32[16,8,512]{2,1,0:T(8,128)} reshape(f32[4,4,2,2,2,512]{5,4,3,2,1,0:T(2,128)S(1)} %copy.17) | data formatting | bytes 524288 | tf_op jit(solution)/shard_map/convert_element_type | solution.py:603
  29.9 9.1 %shard_map.64.src_ref = f32[16,8,512]{2,1,0:T(8,128)} custom-call(f32[3,16,16]{2,1,0:T(8,128)} %reshape.71.tab_ref, f32[1]{0:T(128)} %bitcast.5.emitted_ref, f32[64]{0:T(128)} %spectrum_ref.1, f32[2,64]{1,0:T(2,128)} %attenuation_ref.1, f32[16,8,512]{2,1,0:T(8,128)} %reshape.72.src_ref, f32[8,8,512]{2,1,0:T(8,128)} %reshape.67.target_ref), custom_call_target="tpu_custom_call" | custom-call | tf_op jit(solution)/shard_map/pallas_call | solution.py:609
  39.0 5.5 %shard_map.65 = f32[32,4,512]{2,1,0:T(4,128)} custom-call(f32[3,16,16]{2,1,0:T(8,128)} %reshape.71.tab_ref, f32[16,8,512]{2,1,0:T(8,128)} %shard_map.64.src_ref), custom_call_target="tpu_custom_call" | custom-call | tf_op jit(solution)/shard_map/pallas_call | solution.py:621
  44.5 13.0 %all_to_all.15 = f32[8,2,2,4,512]{4,3,2,1,0:T(4,128)S(1)} all-to-all(f32[8,2,2,4,512]{4,3,2,1,0:T(4,128)} %bitcast.25), channel_id=1, replica_groups=mesh['views'=4,'depth'=4,'lat'=2] {'depth','lat'}, dimensions={0} | all-to-all | bytes 524288 | tf_op jit(solution)/shard_map/all_to_all | solution.py:633
  57.5 0.7 %copy.29 = f32[16,2,4,512]{3,2,1,0:T(4,128)} copy(f32[16,2,4,512]{3,2,1,0:T(4,128)S(1)} %bitcast.28) | data formatting | bytes 524288
  (13 shorter events, 0.2 us)
Async XLA Ops:
  1.3 6.0 %copy-start = (bf16[64,2,4,512]{3,2,1,0:T(4,128)(2,1)S(1)}, bf16[64,2,4,512]{3,2,1,0:T(4,128)(2,1)}, u32[]{:S(2)}) copy-start(bf16[64,2,4,512]{3,2,1,0:T(4,128)(2,1)} %param.6) | copy-start | bytes 1572868
  2.1 10.7 %all-to-all-start.1 = ((f32[8,8,512]{2,1,0:T(8,128)}), f32[8,8,512]{2,1,0:T(8,128)S(1)}, u32[]{:S(2)}, u32[]{:S(2)}) async-start(f32[8,8,512]{2,1,0:T(8,128)} %reshape.65), calls=%async_computation.1 | async-start | bytes 262144 | tf_op jit(solution)/shard_map/all_to_all | solution.py:580
  8.4 0.7 %copy-start.2 = (f32[4,4]{1,0:T(4,128)S(1)}, f32[4,4]{1,0:T(4,128)}, u32[]{:S(2)}) copy-start(f32[4,4]{1,0:T(4,128)} %param.9) | copy-start | bytes 196
  9.1 0.7 %copy-start.1 = (s32[4,4]{1,0:T(4,128)S(1)}, s32[4,4]{1,0:T(4,128)}, u32[]{:S(2)}) copy-start(s32[4,4]{1,0:T(4,128)} %param.8) | copy-start | bytes 196
  10.8 6.3 %copy-start.3 = (f32[64]{0:T(128)S(1)}, f32[64]{0:T(128)}, u32[]{:S(2)}) copy-start(f32[64]{0:T(128)} %spectrum_ref.1) | copy-start | bytes 772
  12.8 14.3 %all-to-all-start = ((bf16[32,5,512]{2,1,0:T(8,128)(2,1)}), bf16[32,5,512]{2,1,0:T(8,128)(2,1)S(1)}, u32[]{:S(2)}, u32[]{:S(2)}) async-start(bf16[32,5,512]{2,1,0:T(8,128)(2,1)} %pad_maximum_fusion), calls=%async_computation | async-start | bytes 524288 | tf_op jit(solution)/shard_map/all_to_all | solution.py:592

commit v15 on v14

--- a/solution.py
+++ b/solution.py
@@ -572,9 +572,15 @@
     upper_weight = shear_frac.astype(jnp.bfloat16).astype(jnp.float32)
     block = jnp.stack([shear_shift.astype(jnp.float32), lower_weight, upper_weight])
     entries = block.size
-    observed = measured.reshape(views_here, groups, depth_count, halves, rows_here, tile_width)
-    observed = lax.dynamic_index_in_dim(observed, slab, 2, keepdims=False)
-    observed = jnp.transpose(observed, (1, 2, 0, 3, 4)).reshape(
+    span = halves * rows_here
+    observed = jnp.stack(
+        [
+            lax.dynamic_slice_in_dim(measured, (g * depth_count + slab) * span, span, 1)
+            for g in range(groups)
+        ]
+    )
+    observed = observed.reshape(groups, views_here, halves, rows_here, tile_width)
+    observed = jnp.transpose(observed, (0, 2, 1, 3, 4)).reshape(
         groups * halves, views_here * rows_here, tile_width
     )
     observed = lax.all_to_all(observed, ("views", "lat"), 0, 0, tiled=True)

time: 58.7 us -> 58.5 us (level)
    reshape x2 -> x1, local copies, waits for them, and re-layouts: 2.09 us -> 0.73 us  [per_device_wide(): jnp.transpose(observed, (0, 2, 1, 3, 4))]
    dynamic_slice x0 -> x5, local copies, waits for them, and re-layouts: none -> 1.02 us  [per_device_wide(): lax.dynamic_slice_in_dim(measured, (g * depth_count + slab) * span, span, 1)]
  transfers between devices with their start and end apart: 2 -> 2, of which waited for: 2 -> 2; matrix products, arithmetic and copies ran while one was open for 6% -> 7% of each run, Pallas kernels for 0% -> 0%
where the time goes in v15:
time: 58.5 us; the launch traced here: 58 us
  Pallas kernels  14.5 us (25%)
  blocking collectives  13 us (22%)
  starting transfers between devices  9.61 us (16%)
  waiting for transfers between devices  9.52 us (16%)
  local copies, waits for them, and re-layouts  8.8 us (15%)
  other arithmetic  1.61 us (3%)
  between operations  0.92 us (2%)
    all_to_all x1, blocking collectives, per_device_wide(): layers = lax.all_to_all(layers, ('depth', 'lat'), 0, 0, tiled=True)  13 us
    pallas_call x1, Pallas kernels, per_device_wide(): pl.pallas_call(functools.partial(forward_kernel, rows_here, halves, depth...  9.05 us
    all_to_all x1, waiting for transfers between devices, per_device_wide(): mine = lax.all_to_all(mine, ('views', 'depth', 'lat'), 0, 0, tiled=True)  7.59 us
    pallas_call x1, Pallas kernels, per_device_wide(): pl.pallas_call(functools.partial(backward_kernel, rows_here, halves), out...  5.5 us
    all_to_all x1, starting transfers between devices, per_device_wide(): observed = lax.all_to_all(observed, ('views', 'lat'), 0, 0, tiled=True)  5.2 us
    all_to_all x1, starting transfers between devices, per_device_wide(): mine = lax.all_to_all(mine, ('views', 'depth', 'lat'), 0, 0, tiled=True)  4.41 us
    unnamed x9, local copies, waits for them, and re-layouts  2.07 us
    all_to_all x1, waiting for transfers between devices, per_device_wide(): observed = lax.all_to_all(observed, ('views', 'lat'), 0, 0, tiled=True)  1.92 us
  transfers between devices with their start and end apart: 2, of which 2 were waited for; matrix products, arithmetic and copies ran while one was open for 7% of the time, Pallas kernels for 0%

profile of v15, /device:TPU:0, one launch (start us, length us, event | category | flops | bytes accessed | tf_op | source)
XLA Modules:
  0.0 58.0 jit_solution(1299871019568657441)
XLA Ops:
  0.0 1.0 %constant_dynamic-slice_fusion.3 = (f32[4,4,512]{2,1,0:T(4,128)S(1)}, f32[4,4,512]{2,1,0:T(4,128)S(1)}, f32[4,4,512]{2,1,0:T(4,128)S(1)}, f32[4,4,512]{2,1,0:T(4,128)S(1)}) fusion(f32[4,64,512]{2,1,0:T(8,128)} %param.7, s32[]{:T(128)S(6)} %select_n.17, s32[]{:T(128)S(6)} %select_n.18, s32[]{:T(128)S(6)} %select_n.20, s32[]{:T(128)S(6)} %select_n.19), kind=kLoop, calls=%fused_computation.13 | loop fusion | bytes 262160 | tf_op jit(solution)/shard_map/dynamic_slice | solution.py:578
  1.1 0.0 copy-start
  1.1 0.1 copy.21
  1.2 0.7 %reshape.70 = f32[8,8,512]{2,1,0:T(8,128)} reshape(f32[4,2,4,2,512]{4,3,2,1,0:T(2,128)S(1)} %copy.21) | data formatting | bytes 262144 | tf_op jit(solution)/shard_map/reshape | solution.py:583
  1.9 5.2 %all-to-all-start.1 = ((f32[8,8,512]{2,1,0:T(8,128)}), f32[8,8,512]{2,1,0:T(8,128)S(1)}, u32[]{:S(2)}, u32[]{:S(2)}) async-start(f32[8,8,512]{2,1,0:T(8,128)} %reshape.70), calls=%async_computation.1 | async-start | bytes 262144 | tf_op jit(solution)/shard_map/all_to_all | solution.py:586
  7.1 0.7 %copy-done.2 = f32[4,4]{1,0:T(4,128)S(1)} copy-done((f32[4,4]{1,0:T(4,128)S(1)}, f32[4,4]{1,0:T(4,128)}, u32[]{:S(2)}) %copy-start.2) | copy-done | bytes 88
  7.8 0.7 %copy-done.1 = s32[4,4]{1,0:T(4,128)S(1)} copy-done((s32[4,4]{1,0:T(4,128)S(1)}, s32[4,4]{1,0:T(4,128)}, u32[]{:S(2)}) %copy-start.1) | copy-done | bytes 88
  8.5 0.1 reshape.64
  8.6 0.3 reshape.62
  9.0 0.8 %dynamic-slice_reduce_fusion = bf16[32,2048]{1,0:T(8,128)(2,1)S(1)} fusion(bf16[32,4,2048]{2,1,0:T(4,128)(2,1)S(1)} %reshape.62, s32[]{:T(128)S(6)} %select_n.16), kind=kLoop, calls=%fused_computation.2 | loop fusion | bytes 262148 | tf_op jit(solution)/shard_map/jit(dynamic_index_in_dim)/dynamic_slice | solution.py:593
  9.7 0.1 reshape.63
  9.9 0.8 %pad_maximum_fusion = bf16[32,5,512]{2,1,0:T(8,128)(2,1)} fusion(bf16[32,1,512]{2,1,0:T(2,128)(2,1)S(1)} %broadcast_in_dim.9, bf16[32,4,512]{2,1,0:T(4,128)(2,1)S(1)} %reshape.63), kind=kLoop, calls=%fused_computation | loop fusion | flops 327680 | bytes 327680 | tf_op jit(solution)/shard_map/concatenate | solution.py:597
  10.7 1.9 %all-to-all-done.1 = f32[8,8,512]{2,1,0:T(8,128)S(1)} async-done(((f32[8,8,512]{2,1,0:T(8,128)}), f32[8,8,512]{2,1,0:T(8,128)S(1)}, u32[]{:S(2)}, u32[]{:S(2)}) %all-to-all-start.1) | async-done | bytes 131104 | tf_op jit(solution)/shard_map/all_to_all | solution.py:586
  12.6 4.4 %all-to-all-start = ((bf16[32,5,512]{2,1,0:T(8,128)(2,1)}), bf16[32,5,512]{2,1,0:T(8,128)(2,1)S(1)}, u32[]{:S(2)}, u32[]{:S(2)}) async-start(bf16[32,5,512]{2,1,0:T(8,128)(2,1)} %pad_maximum_fusion), calls=%async_computation | async-start | bytes 524288 | tf_op jit(solution)/shard_map/all_to_all | solution.py:598
  17.0 0.7 %reduce_sum.9 = f32[]{:T(128)} reduce(f32[64]{0:T(128)S(1)} %copy-done.3, f32[]{:T(128)} %constant.25.clone.1), dimensions={0}, to_apply=%region_0.1 | reduce | flops 63 | bytes 264 | tf_op jit(solution)/shard_map/reduce_sum | solution.py:612
  18.4 0.1 reshape.71
  18.5 0.1 copy.22
  18.6 0.1 copy.23
  18.7 0.7 %reshape.72.target_ref = f32[8,8,512]{2,1,0:T(8,128)} reshape(f32[8,2,2,2,512]{4,3,2,1,0:T(2,128)S(1)} %copy.23) | data formatting | bytes 262144 | tf_op jit(solution)/shard_map/reshape | solution.py:611
  19.4 7.6 %all-to-all-done = bf16[32,5,512]{2,1,0:T(8,128)(2,1)S(1)} async-done(((bf16[32,5,512]{2,1,0:T(8,128)(2,1)}), bf16[32,5,512]{2,1,0:T(8,128)(2,1)S(1)}, u32[]{:S(2)}, u32[]{:S(2)}) %all-to-all-start) | async-done | bytes 163872 | tf_op jit(solution)/shard_map/all_to_all | solution.py:598
  27.0 0.1 slice_convert_fusion
  27.1 0.1 reshape.80
  27.3 0.7 %reshape.76.tab_ref = f32[3,16,16]{2,1,0:T(8,128)} reshape(f32[3,4,4,4,4]{4,3,2,1,0:T(4,128)S(1)} %copy.14) | data formatting | bytes 6144 | tf_op jit(solution)/shard_map/reshape | solution.py:602
  28.0 0.3 reshape.83
  28.2 0.2 copy.29
  28.4 0.2 reshape.81
  28.7 0.2 copy.16
  28.9 0.9 %reshape.77.src_ref = f32[16,8,512]{2,1,0:T(8,128)} reshape(f32[4,4,2,2,2,512]{5,4,3,2,1,0:T(2,128)S(1)} %copy.16) | data formatting | bytes 524288 | tf_op jit(solution)/shard_map/convert_element_type | solution.py:609
  29.7 9.1 %shard_map.64.src_ref = f32[16,8,512]{2,1,0:T(8,128)} custom-call(f32[3,16,16]{2,1,0:T(8,128)} %reshape.76.tab_ref, f32[1]{0:T(128)} %bitcast.5.emitted_ref, f32[64]{0:T(128)} %spectrum_ref.1, f32[2,64]{1,0:T(2,128)} %attenuation_ref.1, f32[16,8,512]{2,1,0:T(8,128)} %reshape.77.src_ref, f32[8,8,512]{2,1,0:T(8,128)} %reshape.72.target_ref), custom_call_target="tpu_custom_call" | custom-call | tf_op jit(solution)/shard_map/pallas_call | solution.py:615
  38.8 5.5 %shard_map.65 = f32[32,4,512]{2,1,0:T(4,128)} custom-call(f32[3,16,16]{2,1,0:T(8,128)} %reshape.76.tab_ref, f32[16,8,512]{2,1,0:T(8,128)} %shard_map.64.src_ref), custom_call_target="tpu_custom_call" | custom-call | tf_op jit(solution)/shard_map/pallas_call | solution.py:627
  44.3 13.0 %all_to_all.15 = f32[8,2,2,4,512]{4,3,2,1,0:T(4,128)S(1)} all-to-all(f32[8,2,2,4,512]{4,3,2,1,0:T(4,128)} %bitcast.27), channel_id=1, replica_groups=mesh['views'=4,'depth'=4,'lat'=2] {'depth','lat'}, dimensions={0} | all-to-all | bytes 524288 | tf_op jit(solution)/shard_map/all_to_all | solution.py:639
  57.3 0.7 %copy.31 = f32[16,2,4,512]{3,2,1,0:T(4,128)} copy(f32[16,2,4,512]{3,2,1,0:T(4,128)S(1)} %bitcast.30) | data formatting | bytes 524288
  (18 shorter events, 0.2 us)
Async XLA Ops:
  1.1 7.6 %copy-start = (bf16[64,2,4,512]{3,2,1,0:T(4,128)(2,1)S(1)}, bf16[64,2,4,512]{3,2,1,0:T(4,128)(2,1)}, u32[]{:S(2)}) copy-start(bf16[64,2,4,512]{3,2,1,0:T(4,128)(2,1)} %param.6) | copy-start | bytes 1572868
  1.9 10.7 %all-to-all-start.1 = ((f32[8,8,512]{2,1,0:T(8,128)}), f32[8,8,512]{2,1,0:T(8,128)S(1)}, u32[]{:S(2)}, u32[]{:S(2)}) async-start(f32[8,8,512]{2,1,0:T(8,128)} %reshape.70), calls=%async_computation.1 | async-start | bytes 262144 | tf_op jit(solution)/shard_map/all_to_all | solution.py:586
  7.1 0.7 %copy-start.2 = (f32[4,4]{1,0:T(4,128)S(1)}, f32[4,4]{1,0:T(4,128)}, u32[]{:S(2)}) copy-start(f32[4,4]{1,0:T(4,128)} %param.9) | copy-start | bytes 196
  7.8 0.7 %copy-start.1 = (s32[4,4]{1,0:T(4,128)S(1)}, s32[4,4]{1,0:T(4,128)}, u32[]{:S(2)}) copy-start(s32[4,4]{1,0:T(4,128)} %param.8) | copy-start | bytes 196
  10.7 6.3 %copy-start.3 = (f32[64]{0:T(128)S(1)}, f32[64]{0:T(128)}, u32[]{:S(2)}) copy-start(f32[64]{0:T(128)} %spectrum_ref.1) | copy-start | bytes 772
  12.6 14.4 %all-to-all-start = ((bf16[32,5,512]{2,1,0:T(8,128)(2,1)}), bf16[32,5,512]{2,1,0:T(8,128)(2,1)S(1)}, u32[]{:S(2)}, u32[]{:S(2)}) async-start(bf16[32,5,512]{2,1,0:T(8,128)(2,1)} %pad_maximum_fusion), calls=%async_computation | async-start | bytes 524288 | tf_op jit(solution)/shard_map/all_to_all | solution.py:598

commit v16 on v15

--- a/solution.py
+++ b/solution.py
@@ -575,13 +575,12 @@
     span = halves * rows_here
     observed = jnp.stack(
         [
-            lax.dynamic_slice_in_dim(measured, (g * depth_count + slab) * span, span, 1)
+            lax.dynamic_slice_in_dim(
+                measured, (g * depth_count + slab) * span + h * rows_here, rows_here, 1
+            ).reshape(views_here * rows_here, tile_width)
             for g in range(groups)
+            for h in range(halves)
         ]
-    )
-    observed = observed.reshape(groups, views_here, halves, rows_here, tile_width)
-    observed = jnp.transpose(observed, (0, 2, 1, 3, 4)).reshape(
-        groups * halves, views_here * rows_here, tile_width
     )
     observed = lax.all_to_all(observed, ("views", "lat"), 0, 0, tiled=True)
     observed = observed.reshape(groups, halves, views_here, rows_here, tile_width)

time: 58.5 us -> 62.9 us (1.075)
  local copies, waits for them, and re-layouts: 8.8 us -> 13.1 us
    unnamed x9 -> x16, local copies, waits for them, and re-layouts: 2.07 us -> 6.27 us
    reshape x1 -> x0, local copies, waits for them, and re-layouts: 0.73 us -> none  [per_device_wide(): jnp.transpose(observed, (0, 2, 1, 3, 4))]
    another operation x0 -> x9, local copies, waits for them, and re-layouts: none -> 0.72 us  [per_device_wide(): jnp.stack([lax.dynamic_slice_in_dim(measured, (g * depth_count + slab) *...]
  transfers between devices with their start and end apart: 2 -> 2, of which waited for: 2 -> 2; matrix products, arithmetic and copies ran while one was open for 7% -> 6% of each run, Pallas kernels for 0% -> 0%
where the time goes in v16:
time: 62.9 us; the launch traced here: 62.4 us
  Pallas kernels  14.5 us (23%)
  local copies, waits for them, and re-layouts  13.1 us (21%)
  blocking collectives  13 us (21%)
  starting transfers between devices  9.76 us (16%)
  waiting for transfers between devices  9.52 us (15%)
  other arithmetic  1.57 us (2%)
  between operations  0.91 us (1%)
    all_to_all x1, blocking collectives, per_device_wide(): layers = lax.all_to_all(layers, ('depth', 'lat'), 0, 0, tiled=True)  13 us
    pallas_call x1, Pallas kernels, per_device_wide(): pl.pallas_call(functools.partial(forward_kernel, rows_here, halves, depth...  9.05 us
    all_to_all x1, waiting for transfers between devices, per_device_wide(): mine = lax.all_to_all(mine, ('views', 'depth', 'lat'), 0, 0, tiled=True)  7.59 us
    unnamed x16, local copies, waits for them, and re-layouts  6.27 us
    pallas_call x1, Pallas kernels, per_device_wide(): pl.pallas_call(functools.partial(backward_kernel, rows_here, halves), out...  5.5 us
    all_to_all x1, starting transfers between devices, per_device_wide(): observed = lax.all_to_all(observed, ('views', 'lat'), 0, 0, tiled=True)  5.2 us
    all_to_all x1, starting transfers between devices, per_device_wide(): mine = lax.all_to_all(mine, ('views', 'depth', 'lat'), 0, 0, tiled=True)  4.56 us
    all_to_all x1, waiting for transfers between devices, per_device_wide(): observed = lax.all_to_all(observed, ('views', 'lat'), 0, 0, tiled=True)  1.92 us
  transfers between devices with their start and end apart: 2, of which 2 were waited for; matrix products, arithmetic and copies ran while one was open for 6% of the time, Pallas kernels for 0%

profile of v16, /device:TPU:0, one launch (start us, length us, event | category | flops | bytes accessed | tf_op | source)
XLA Modules:
  0.0 62.4 jit_solution(18000956079739709165)
XLA Ops:
  0.0 1.2 %constant_dynamic-slice_fusion = (f32[4,2,512]{2,1,0:T(2,128)S(1)}, f32[4,2,512]{2,1,0:T(2,128)S(1)}, f32[4,2,512]{2,1,0:T(2,128)S(1)}, f32[4,2,512]{2,1,0:T(2,1...) fusion(f32[4,64,512]{2,1,0:T(8,128)} %param.7, ...), kind=kLoop, calls=%fused_computation.14 | loop fusion | bytes 262176 | tf_op jit(solution)/shard_map/dynamic_slice | solution.py:578
  1.2 0.6 constant_dynamic-update-slice_fusion.7
  1.9 0.6 constant_dynamic-update-slice_fusion.6
  2.6 0.6 constant_dynamic-update-slice_fusion.5
  3.2 0.6 constant_dynamic-update-slice_fusion.4
  3.7 0.6 constant_dynamic-update-slice_fusion.3
  4.3 0.6 constant_dynamic-update-slice_fusion.2
  5.0 0.6 constant_dynamic-update-slice_fusion.1
  5.6 0.6 constant_dynamic-update-slice_fusion
  6.1 5.2 %all-to-all-start.1 = ((f32[8,8,512]{2,1,0:T(8,128)}), f32[8,8,512]{2,1,0:T(8,128)S(1)}, u32[]{:S(2)}, u32[]{:S(2)}) async-start(f32[8,8,512]{2,1,0:T(8,128)} %constant_dynamic-update-slice_fusion), calls=%async_computation.1 | async-start | bytes 262144 | tf_op jit(solution)/shard_map/all_to_all | solution.py:585
  11.4 0.7 %copy-done.2 = f32[4,4]{1,0:T(4,128)S(1)} copy-done((f32[4,4]{1,0:T(4,128)S(1)}, f32[4,4]{1,0:T(4,128)}, u32[]{:S(2)}) %copy-start.2) | copy-done | bytes 88
  12.0 0.7 %copy-done.1 = s32[4,4]{1,0:T(4,128)S(1)} copy-done((s32[4,4]{1,0:T(4,128)S(1)}, s32[4,4]{1,0:T(4,128)}, u32[]{:S(2)}) %copy-start.1) | copy-done | bytes 88
  12.9 0.3 reshape.50
  13.2 0.8 %dynamic-slice_reduce_fusion = bf16[32,2048]{1,0:T(8,128)(2,1)S(1)} fusion(bf16[32,4,2048]{2,1,0:T(4,128)(2,1)S(1)} %reshape.50, s32[]{:T(128)S(6)} %select_n.28), kind=kLoop, calls=%fused_computation.2 | loop fusion | bytes 262148 | tf_op jit(solution)/shard_map/jit(dynamic_index_in_dim)/dynamic_slice | solution.py:592
  14.1 0.8 %pad_maximum_fusion = bf16[32,5,512]{2,1,0:T(8,128)(2,1)} fusion(bf16[32,1,512]{2,1,0:T(2,128)(2,1)S(1)} %broadcast_in_dim.9, bf16[32,4,512]{2,1,0:T(4,128)(2,1)S(1)} %reshape.51), kind=kLoop, calls=%fused_computation | loop fusion | flops 327680 | bytes 327680 | tf_op jit(solution)/shard_map/concatenate | solution.py:596
  14.9 1.9 %all-to-all-done.1 = f32[8,8,512]{2,1,0:T(8,128)S(1)} async-done(((f32[8,8,512]{2,1,0:T(8,128)}), f32[8,8,512]{2,1,0:T(8,128)S(1)}, u32[]{:S(2)}, u32[]{:S(2)}) %all-to-all-start.1) | async-done | bytes 131104 | tf_op jit(solution)/shard_map/all_to_all | solution.py:585
  16.8 4.6 %all-to-all-start = ((bf16[32,5,512]{2,1,0:T(8,128)(2,1)}), bf16[32,5,512]{2,1,0:T(8,128)(2,1)S(1)}, u32[]{:S(2)}, u32[]{:S(2)}) async-start(bf16[32,5,512]{2,1,0:T(8,128)(2,1)} %pad_maximum_fusion), calls=%async_computation | async-start | bytes 524288 | tf_op jit(solution)/shard_map/all_to_all | solution.py:597
  21.4 0.7 %reduce_sum.9 = f32[]{:T(128)} reduce(f32[64]{0:T(128)S(1)} %copy-done.3, f32[]{:T(128)} %constant.30.clone.1), dimensions={0}, to_apply=%region_0.1 | reduce | flops 63 | bytes 264 | tf_op jit(solution)/shard_map/reduce_sum | solution.py:611
  22.9 0.1 copy.17
  23.1 0.7 %reshape.59.target_ref = f32[8,8,512]{2,1,0:T(8,128)} reshape(f32[8,2,2,2,512]{4,3,2,1,0:T(2,128)S(1)} %copy.18) | data formatting | bytes 262144 | tf_op jit(solution)/shard_map/reshape | solution.py:610
  23.8 7.6 %all-to-all-done = bf16[32,5,512]{2,1,0:T(8,128)(2,1)S(1)} async-done(((bf16[32,5,512]{2,1,0:T(8,128)(2,1)}), bf16[32,5,512]{2,1,0:T(8,128)(2,1)S(1)}, u32[]{:S(2)}, u32[]{:S(2)}) %all-to-all-start) | async-done | bytes 163872 | tf_op jit(solution)/shard_map/all_to_all | solution.py:597
  31.5 0.1 reshape.67
  31.7 0.7 %reshape.63.tab_ref = f32[3,16,16]{2,1,0:T(8,128)} reshape(f32[3,4,4,4,4]{4,3,2,1,0:T(4,128)S(1)} %copy.14) | data formatting | bytes 6144 | tf_op jit(solution)/shard_map/reshape | solution.py:601
  32.4 0.3 reshape.70
  32.6 0.2 copy.24
  32.8 0.2 reshape.68
  33.0 0.2 copy.16
  33.3 0.9 %reshape.64.src_ref = f32[16,8,512]{2,1,0:T(8,128)} reshape(f32[4,4,2,2,2,512]{5,4,3,2,1,0:T(2,128)S(1)} %copy.16) | data formatting | bytes 524288 | tf_op jit(solution)/shard_map/convert_element_type | solution.py:608
  34.1 9.1 %shard_map.64.src_ref = f32[16,8,512]{2,1,0:T(8,128)} custom-call(f32[3,16,16]{2,1,0:T(8,128)} %reshape.63.tab_ref, f32[1]{0:T(128)} %bitcast.5.emitted_ref, f32[64]{0:T(128)} %spectrum_ref.1, f32[2,64]{1,0:T(2,128)} %attenuation_ref.1, f32[16,8,512]{2,1,0:T(8,128)} %reshape.64.src_ref, f32[8,8,512]{2,1,0:T(8,128)} %reshape.59.target_ref), custom_call_target="tpu_custom_call" | custom-call | tf_op jit(solution)/shard_map/pallas_call | solution.py:614
  43.2 5.5 %shard_map.65 = f32[32,4,512]{2,1,0:T(4,128)} custom-call(f32[3,16,16]{2,1,0:T(8,128)} %reshape.63.tab_ref, f32[16,8,512]{2,1,0:T(8,128)} %shard_map.64.src_ref), custom_call_target="tpu_custom_call" | custom-call | tf_op jit(solution)/shard_map/pallas_call | solution.py:626
  48.7 13.0 %all_to_all.15 = f32[8,2,2,4,512]{4,3,2,1,0:T(4,128)S(1)} all-to-all(f32[8,2,2,4,512]{4,3,2,1,0:T(4,128)} %bitcast.21), channel_id=1, replica_groups=mesh['views'=4,'depth'=4,'lat'=2] {'depth','lat'}, dimensions={0} | all-to-all | bytes 524288 | tf_op jit(solution)/shard_map/all_to_all | solution.py:638
  61.7 0.7 %copy.33 = f32[16,2,4,512]{3,2,1,0:T(4,128)} copy(f32[16,2,4,512]{3,2,1,0:T(4,128)S(1)} %bitcast.24) | data formatting | bytes 524288
  (27 shorter events, 0.6 us)
Async XLA Ops:
  0.0 12.8 %copy-start = (bf16[64,2,4,512]{3,2,1,0:T(4,128)(2,1)S(1)}, bf16[64,2,4,512]{3,2,1,0:T(4,128)(2,1)}, u32[]{:S(2)}) copy-start(bf16[64,2,4,512]{3,2,1,0:T(4,128)(2,1)} %param.6) | copy-start | bytes 1572868
  6.1 10.7 %all-to-all-start.1 = ((f32[8,8,512]{2,1,0:T(8,128)}), f32[8,8,512]{2,1,0:T(8,128)S(1)}, u32[]{:S(2)}, u32[]{:S(2)}) async-start(f32[8,8,512]{2,1,0:T(8,128)} %constant_dynamic-update-slice_fusion), calls=%async_computation.1 | async-start | bytes 262144 | tf_op jit(solution)/shard_map/all_to_all | solution.py:585
  11.3 0.7 %copy-start.2 = (f32[4,4]{1,0:T(4,128)S(1)}, f32[4,4]{1,0:T(4,128)}, u32[]{:S(2)}) copy-start(f32[4,4]{1,0:T(4,128)} %param.9) | copy-start | bytes 196
  12.0 0.7 %copy-start.1 = (s32[4,4]{1,0:T(4,128)S(1)}, s32[4,4]{1,0:T(4,128)}, u32[]{:S(2)}) copy-start(s32[4,4]{1,0:T(4,128)} %param.8) | copy-start | bytes 196
  14.9 6.5 %copy-start.3 = (f32[64]{0:T(128)S(1)}, f32[64]{0:T(128)}, u32[]{:S(2)}) copy-start(f32[64]{0:T(128)} %spectrum_ref.1) | copy-start | bytes 772
  16.8 14.6 %all-to-all-start = ((bf16[32,5,512]{2,1,0:T(8,128)(2,1)}), bf16[32,5,512]{2,1,0:T(8,128)(2,1)S(1)}, u32[]{:S(2)}, u32[]{:S(2)}) async-start(bf16[32,5,512]{2,1,0:T(8,128)(2,1)} %pad_maximum_fusion), calls=%async_computation | async-start | bytes 524288 | tf_op jit(solution)/shard_map/all_to_all | solution.py:597

commit v17 on v15

--- a/solution.py
+++ b/solution.py
@@ -422,7 +422,7 @@
         out_ref[2 * p + 1] = jnp.where(low, pltpu.roll(first, split, 0), second)
         return carry
 
-    lax.fori_loop(0, out_ref.shape[0] // 2, one_pair, 0)
+    lax.fori_loop(0, out_ref.shape[0] // 2, one_pair, 0, unroll=True)
 
 
 def backward_kernel(rows_here, halves, tab_ref, src_ref, out_ref, cols_ref, nexts_ref):

time: 58.5 us -> 58 us (level)
  no operation moved by 1% of the time
where the time goes in v17:
time: 58 us; the launch traced here: 57.5 us
  Pallas kernels  14 us (24%)
  blocking collectives  13 us (22%)
  starting transfers between devices  9.61 us (17%)
  waiting for transfers between devices  9.52 us (16%)
  local copies, waits for them, and re-layouts  8.8 us (15%)
  other arithmetic  1.61 us (3%)
  between operations  0.92 us (2%)
    all_to_all x1, blocking collectives, per_device_wide(): layers = lax.all_to_all(layers, ('depth', 'lat'), 0, 0, tiled=True)  13 us
    pallas_call x1, Pallas kernels, per_device_wide(): pl.pallas_call(functools.partial(forward_kernel, rows_here, halves, depth...  8.54 us
    all_to_all x1, waiting for transfers between devices, per_device_wide(): mine = lax.all_to_all(mine, ('views', 'depth', 'lat'), 0, 0, tiled=True)  7.59 us
    pallas_call x1, Pallas kernels, per_device_wide(): pl.pallas_call(functools.partial(backward_kernel, rows_here, halves), out...  5.5 us
    all_to_all x1, starting transfers between devices, per_device_wide(): observed = lax.all_to_all(observed, ('views', 'lat'), 0, 0, tiled=True)  5.2 us
    all_to_all x1, starting transfers between devices, per_device_wide(): mine = lax.all_to_all(mine, ('views', 'depth', 'lat'), 0, 0, tiled=True)  4.41 us
    unnamed x9, local copies, waits for them, and re-layouts  2.07 us
    all_to_all x1, waiting for transfers between devices, per_device_wide(): observed = lax.all_to_all(observed, ('views', 'lat'), 0, 0, tiled=True)  1.92 us
  transfers between devices with their start and end apart: 2, of which 2 were waited for; matrix products, arithmetic and copies ran while one was open for 7% of the time, Pallas kernels for 0%

profile of v17, /device:TPU:0, one launch (start us, length us, event | category | flops | bytes accessed | tf_op | source)
XLA Modules:
  0.0 57.5 jit_solution(11451710162054577659)
XLA Ops:
  0.0 1.0 %constant_dynamic-slice_fusion.3 = (f32[4,4,512]{2,1,0:T(4,128)S(1)}, f32[4,4,512]{2,1,0:T(4,128)S(1)}, f32[4,4,512]{2,1,0:T(4,128)S(1)}, f32[4,4,512]{2,1,0:T(4,128)S(1)}) fusion(f32[4,64,512]{2,1,0:T(8,128)} %param.7, s32[]{:T(128)S(6)} %select_n.17, s32[]{:T(128)S(6)} %select_n.18, s32[]{:T(128)S(6)} %select_n.20, s32[]{:T(128)S(6)} %select_n.19), kind=kLoop, calls=%fused_computation.13 | loop fusion | bytes 262160 | tf_op jit(solution)/shard_map/dynamic_slice | solution.py:578
  1.1 0.0 copy-start
  1.1 0.1 copy.21
  1.2 0.7 %reshape.70 = f32[8,8,512]{2,1,0:T(8,128)} reshape(f32[4,2,4,2,512]{4,3,2,1,0:T(2,128)S(1)} %copy.21) | data formatting | bytes 262144 | tf_op jit(solution)/shard_map/reshape | solution.py:583
  1.9 5.2 %all-to-all-start.1 = ((f32[8,8,512]{2,1,0:T(8,128)}), f32[8,8,512]{2,1,0:T(8,128)S(1)}, u32[]{:S(2)}, u32[]{:S(2)}) async-start(f32[8,8,512]{2,1,0:T(8,128)} %reshape.70), calls=%async_computation.1 | async-start | bytes 262144 | tf_op jit(solution)/shard_map/all_to_all | solution.py:586
  7.1 0.7 %copy-done.2 = f32[4,4]{1,0:T(4,128)S(1)} copy-done((f32[4,4]{1,0:T(4,128)S(1)}, f32[4,4]{1,0:T(4,128)}, u32[]{:S(2)}) %copy-start.2) | copy-done | bytes 88
  7.8 0.7 %copy-done.1 = s32[4,4]{1,0:T(4,128)S(1)} copy-done((s32[4,4]{1,0:T(4,128)S(1)}, s32[4,4]{1,0:T(4,128)}, u32[]{:S(2)}) %copy-start.1) | copy-done | bytes 88
  8.5 0.1 reshape.64
  8.6 0.3 reshape.62
  9.0 0.8 %dynamic-slice_reduce_fusion = bf16[32,2048]{1,0:T(8,128)(2,1)S(1)} fusion(bf16[32,4,2048]{2,1,0:T(4,128)(2,1)S(1)} %reshape.62, s32[]{:T(128)S(6)} %select_n.16), kind=kLoop, calls=%fused_computation.2 | loop fusion | bytes 262148 | tf_op jit(solution)/shard_map/jit(dynamic_index_in_dim)/dynamic_slice | solution.py:593
  9.7 0.1 reshape.63
  9.9 0.8 %pad_maximum_fusion = bf16[32,5,512]{2,1,0:T(8,128)(2,1)} fusion(bf16[32,1,512]{2,1,0:T(2,128)(2,1)S(1)} %broadcast_in_dim.9, bf16[32,4,512]{2,1,0:T(4,128)(2,1)S(1)} %reshape.63), kind=kLoop, calls=%fused_computation | loop fusion | flops 327680 | bytes 327680 | tf_op jit(solution)/shard_map/concatenate | solution.py:597
  10.7 1.9 %all-to-all-done.1 = f32[8,8,512]{2,1,0:T(8,128)S(1)} async-done(((f32[8,8,512]{2,1,0:T(8,128)}), f32[8,8,512]{2,1,0:T(8,128)S(1)}, u32[]{:S(2)}, u32[]{:S(2)}) %all-to-all-start.1) | async-done | bytes 131104 | tf_op jit(solution)/shard_map/all_to_all | solution.py:586
  12.6 4.4 %all-to-all-start = ((bf16[32,5,512]{2,1,0:T(8,128)(2,1)}), bf16[32,5,512]{2,1,0:T(8,128)(2,1)S(1)}, u32[]{:S(2)}, u32[]{:S(2)}) async-start(bf16[32,5,512]{2,1,0:T(8,128)(2,1)} %pad_maximum_fusion), calls=%async_computation | async-start | bytes 524288 | tf_op jit(solution)/shard_map/all_to_all | solution.py:598
  17.0 0.7 %reduce_sum.9 = f32[]{:T(128)} reduce(f32[64]{0:T(128)S(1)} %copy-done.3, f32[]{:T(128)} %constant.25.clone.1), dimensions={0}, to_apply=%region_0.1 | reduce | flops 63 | bytes 264 | tf_op jit(solution)/shard_map/reduce_sum | solution.py:612
  18.4 0.1 reshape.71
  18.5 0.1 copy.22
  18.6 0.1 copy.23
  18.7 0.7 %reshape.72.target_ref = f32[8,8,512]{2,1,0:T(8,128)} reshape(f32[8,2,2,2,512]{4,3,2,1,0:T(2,128)S(1)} %copy.23) | data formatting | bytes 262144 | tf_op jit(solution)/shard_map/reshape | solution.py:611
  19.4 7.6 %all-to-all-done = bf16[32,5,512]{2,1,0:T(8,128)(2,1)S(1)} async-done(((bf16[32,5,512]{2,1,0:T(8,128)(2,1)}), bf16[32,5,512]{2,1,0:T(8,128)(2,1)S(1)}, u32[]{:S(2)}, u32[]{:S(2)}) %all-to-all-start) | async-done | bytes 163872 | tf_op jit(solution)/shard_map/all_to_all | solution.py:598
  27.0 0.1 slice_convert_fusion
  27.1 0.1 reshape.80
  27.3 0.7 %reshape.76.tab_ref = f32[3,16,16]{2,1,0:T(8,128)} reshape(f32[3,4,4,4,4]{4,3,2,1,0:T(4,128)S(1)} %copy.14) | data formatting | bytes 6144 | tf_op jit(solution)/shard_map/reshape | solution.py:602
  28.0 0.3 reshape.83
  28.2 0.2 copy.29
  28.4 0.2 reshape.81
  28.7 0.2 copy.16
  28.9 0.9 %reshape.77.src_ref = f32[16,8,512]{2,1,0:T(8,128)} reshape(f32[4,4,2,2,2,512]{5,4,3,2,1,0:T(2,128)S(1)} %copy.16) | data formatting | bytes 524288 | tf_op jit(solution)/shard_map/convert_element_type | solution.py:609
  29.7 8.5 %shard_map.64.src_ref = f32[16,8,512]{2,1,0:T(8,128)} custom-call(f32[3,16,16]{2,1,0:T(8,128)} %reshape.76.tab_ref, f32[1]{0:T(128)} %bitcast.5.emitted_ref, f32[64]{0:T(128)} %spectrum_ref.1, f32[2,64]{1,0:T(2,128)} %attenuation_ref.1, f32[16,8,512]{2,1,0:T(8,128)} %reshape.77.src_ref, f32[8,8,512]{2,1,0:T(8,128)} %reshape.72.target_ref), custom_call_target="tpu_custom_call" | custom-call | tf_op jit(solution)/shard_map/pallas_call | solution.py:615
  38.3 5.5 %shard_map.65 = f32[32,4,512]{2,1,0:T(4,128)} custom-call(f32[3,16,16]{2,1,0:T(8,128)} %reshape.76.tab_ref, f32[16,8,512]{2,1,0:T(8,128)} %shard_map.64.src_ref), custom_call_target="tpu_custom_call" | custom-call | tf_op jit(solution)/shard_map/pallas_call | solution.py:627
  43.8 13.0 %all_to_all.15 = f32[8,2,2,4,512]{4,3,2,1,0:T(4,128)S(1)} all-to-all(f32[8,2,2,4,512]{4,3,2,1,0:T(4,128)} %bitcast.27), channel_id=1, replica_groups=mesh['views'=4,'depth'=4,'lat'=2] {'depth','lat'}, dimensions={0} | all-to-all | bytes 524288 | tf_op jit(solution)/shard_map/all_to_all | solution.py:639
  56.8 0.7 %copy.31 = f32[16,2,4,512]{3,2,1,0:T(4,128)} copy(f32[16,2,4,512]{3,2,1,0:T(4,128)S(1)} %bitcast.30) | data formatting | bytes 524288
  (18 shorter events, 0.2 us)
Async XLA Ops:
  1.1 7.6 %copy-start = (bf16[64,2,4,512]{3,2,1,0:T(4,128)(2,1)S(1)}, bf16[64,2,4,512]{3,2,1,0:T(4,128)(2,1)}, u32[]{:S(2)}) copy-start(bf16[64,2,4,512]{3,2,1,0:T(4,128)(2,1)} %param.6) | copy-start | bytes 1572868
  1.9 10.7 %all-to-all-start.1 = ((f32[8,8,512]{2,1,0:T(8,128)}), f32[8,8,512]{2,1,0:T(8,128)S(1)}, u32[]{:S(2)}, u32[]{:S(2)}) async-start(f32[8,8,512]{2,1,0:T(8,128)} %reshape.70), calls=%async_computation.1 | async-start | bytes 262144 | tf_op jit(solution)/shard_map/all_to_all | solution.py:586
  7.1 0.7 %copy-start.2 = (f32[4,4]{1,0:T(4,128)S(1)}, f32[4,4]{1,0:T(4,128)}, u32[]{:S(2)}) copy-start(f32[4,4]{1,0:T(4,128)} %param.9) | copy-start | bytes 196
  7.8 0.7 %copy-start.1 = (s32[4,4]{1,0:T(4,128)S(1)}, s32[4,4]{1,0:T(4,128)}, u32[]{:S(2)}) copy-start(s32[4,4]{1,0:T(4,128)} %param.8) | copy-start | bytes 196
  10.7 6.3 %copy-start.3 = (f32[64]{0:T(128)S(1)}, f32[64]{0:T(128)}, u32[]{:S(2)}) copy-start(f32[64]{0:T(128)} %spectrum_ref.1) | copy-start | bytes 772
  12.6 14.4 %all-to-all-start = ((bf16[32,5,512]{2,1,0:T(8,128)(2,1)}), bf16[32,5,512]{2,1,0:T(8,128)(2,1)S(1)}, u32[]{:S(2)}, u32[]{:S(2)}) async-start(bf16[32,5,512]{2,1,0:T(8,128)(2,1)} %pad_maximum_fusion), calls=%async_computation | async-start | bytes 524288 | tf_op jit(solution)/shard_map/all_to_all | solution.py:598

commit v18 on v17

--- a/solution.py
+++ b/solution.py
@@ -308,7 +308,7 @@
             nexts_ref[o, :, k * LANES : (k + 1) * LANES] = nexts[k]
         return carry
 
-    lax.fori_loop(0, outer_count, prepare, 0)
+    lax.fori_loop(0, outer_count, prepare, 0, unroll=True)
 
     for i in range(inner_count):
 
@@ -359,7 +359,7 @@
             nexts_ref[o, :, k * LANES : (k + 1) * LANES] = nexts[k]
         return carry
 
-    lax.fori_loop(0, outer_count, prepare, 0)
+    lax.fori_loop(0, outer_count, prepare, 0, unroll=True)
     inner_count = tab_ref.shape[2]
 
     for i in range(inner_count):
@@ -391,6 +391,12 @@
             out_ref[target, level : level + 1, :] = value[c : c + 1, :]
 
 
+def scaled(value, count):
+    if count & (count - 1) == 0:
+        return value * (1.0 / count)
+    return value / count
+
+
 def forward_kernel(rows_here, halves, depth_all, views_all, tab_ref, emitted_ref, spectrum_ref,
                    attenuation_ref, src_ref, target_ref, out_ref, sums_ref, cols_ref, nexts_ref):
     shear_pass(True, rows_here, halves, tab_ref, src_ref, sums_ref, cols_ref, nexts_ref)
@@ -400,8 +406,8 @@
     low = lax.broadcasted_iota(jnp.int32, (channels, width), 0) < split
 
     def one_pair(p, carry):
-        first_view = sums_ref[2 * p] / depth_all
-        second_view = sums_ref[2 * p + 1] / depth_all
+        first_view = scaled(sums_ref[2 * p], depth_all)
+        second_view = scaled(sums_ref[2 * p + 1], depth_all)
         water = jnp.where(low, first_view, pltpu.roll(second_view, split, 0))
         bone = jnp.where(low, pltpu.roll(first_view, split, 0), second_view)
 
@@ -415,7 +421,7 @@
         zero = jnp.zeros((channels, width), jnp.float32)
         intensity, first, second = lax.fori_loop(0, energies, one_energy, (zero, zero, zero), unroll=True)
         residual = emitted_ref[0] - jnp.log(intensity) - target_ref[p]
-        factor = residual / intensity / views_all
+        factor = scaled(residual / intensity, views_all)
         first = (first * factor).astype(jnp.bfloat16).astype(jnp.float32)
         second = (second * factor).astype(jnp.bfloat16).astype(jnp.float32)
         out_ref[2 * p] = jnp.where(low, first, pltpu.roll(second, split, 0))

time: 58 us -> 54.8 us (0.945)
  Pallas kernels: 14 us -> 10.8 us
    pallas_call x1, Pallas kernels: 8.54 us -> 6.91 us  [per_device_wide(): pl.pallas_call(functools.partial(forward_kernel, rows_here, halves, depth...]
    pallas_call x1, Pallas kernels: 5.5 us -> 3.93 us  [per_device_wide(): pl.pallas_call(functools.partial(backward_kernel, rows_here, halves), out...]
where the time goes in v18:
time: 54.8 us; the launch traced here: 54.3 us
  blocking collectives  13 us (24%)
  Pallas kernels  10.8 us (20%)
  starting transfers between devices  9.61 us (18%)
  waiting for transfers between devices  9.52 us (17%)
  local copies, waits for them, and re-layouts  8.8 us (16%)
  other arithmetic  1.61 us (3%)
  between operations  0.92 us (2%)
    all_to_all x1, blocking collectives, per_device_wide(): layers = lax.all_to_all(layers, ('depth', 'lat'), 0, 0, tiled=True)  13 us
    all_to_all x1, waiting for transfers between devices, per_device_wide(): mine = lax.all_to_all(mine, ('views', 'depth', 'lat'), 0, 0, tiled=True)  7.59 us
    pallas_call x1, Pallas kernels, per_device_wide(): pl.pallas_call(functools.partial(forward_kernel, rows_here, halves, depth...  6.91 us
    all_to_all x1, starting transfers between devices, per_device_wide(): observed = lax.all_to_all(observed, ('views', 'lat'), 0, 0, tiled=True)  5.2 us
    all_to_all x1, starting transfers between devices, per_device_wide(): mine = lax.all_to_all(mine, ('views', 'depth', 'lat'), 0, 0, tiled=True)  4.41 us
    pallas_call x1, Pallas kernels, per_device_wide(): pl.pallas_call(functools.partial(backward_kernel, rows_here, halves), out...  3.93 us
    unnamed x9, local copies, waits for them, and re-layouts  2.07 us
    all_to_all x1, waiting for transfers between devices, per_device_wide(): observed = lax.all_to_all(observed, ('views', 'lat'), 0, 0, tiled=True)  1.92 us
  transfers between devices with their start and end apart: 2, of which 2 were waited for; matrix products, arithmetic and copies ran while one was open for 7% of the time, Pallas kernels for 0%

profile of v18, /device:TPU:0, one launch (start us, length us, event | category | flops | bytes accessed | tf_op | source)
XLA Modules:
  0.0 54.3 jit_solution(9998623046256293927)
XLA Ops:
  0.0 1.0 %constant_dynamic-slice_fusion.3 = (f32[4,4,512]{2,1,0:T(4,128)S(1)}, f32[4,4,512]{2,1,0:T(4,128)S(1)}, f32[4,4,512]{2,1,0:T(4,128)S(1)}, f32[4,4,512]{2,1,0:T(4,128)S(1)}) fusion(f32[4,64,512]{2,1,0:T(8,128)} %param.7, s32[]{:T(128)S(6)} %select_n.17, s32[]{:T(128)S(6)} %select_n.18, s32[]{:T(128)S(6)} %select_n.20, s32[]{:T(128)S(6)} %select_n.19), kind=kLoop, calls=%fused_computation.13 | loop fusion | bytes 262160 | tf_op jit(solution)/shard_map/dynamic_slice | solution.py:584
  1.1 0.0 copy-start
  1.1 0.1 copy.21
  1.2 0.7 %reshape.70 = f32[8,8,512]{2,1,0:T(8,128)} reshape(f32[4,2,4,2,512]{4,3,2,1,0:T(2,128)S(1)} %copy.21) | data formatting | bytes 262144 | tf_op jit(solution)/shard_map/reshape | solution.py:589
  1.9 5.2 %all-to-all-start.1 = ((f32[8,8,512]{2,1,0:T(8,128)}), f32[8,8,512]{2,1,0:T(8,128)S(1)}, u32[]{:S(2)}, u32[]{:S(2)}) async-start(f32[8,8,512]{2,1,0:T(8,128)} %reshape.70), calls=%async_computation.1 | async-start | bytes 262144 | tf_op jit(solution)/shard_map/all_to_all | solution.py:592
  7.1 0.7 %copy-done.2 = f32[4,4]{1,0:T(4,128)S(1)} copy-done((f32[4,4]{1,0:T(4,128)S(1)}, f32[4,4]{1,0:T(4,128)}, u32[]{:S(2)}) %copy-start.2) | copy-done | bytes 88
  7.8 0.7 %copy-done.1 = s32[4,4]{1,0:T(4,128)S(1)} copy-done((s32[4,4]{1,0:T(4,128)S(1)}, s32[4,4]{1,0:T(4,128)}, u32[]{:S(2)}) %copy-start.1) | copy-done | bytes 88
  8.5 0.1 reshape.64
  8.6 0.3 reshape.62
  9.0 0.8 %dynamic-slice_reduce_fusion = bf16[32,2048]{1,0:T(8,128)(2,1)S(1)} fusion(bf16[32,4,2048]{2,1,0:T(4,128)(2,1)S(1)} %reshape.62, s32[]{:T(128)S(6)} %select_n.16), kind=kLoop, calls=%fused_computation.2 | loop fusion | bytes 262148 | tf_op jit(solution)/shard_map/jit(dynamic_index_in_dim)/dynamic_slice | solution.py:599
  9.7 0.1 reshape.63
  9.9 0.8 %pad_maximum_fusion = bf16[32,5,512]{2,1,0:T(8,128)(2,1)} fusion(bf16[32,1,512]{2,1,0:T(2,128)(2,1)S(1)} %broadcast_in_dim.9, bf16[32,4,512]{2,1,0:T(4,128)(2,1)S(1)} %reshape.63), kind=kLoop, calls=%fused_computation | loop fusion | flops 327680 | bytes 327680 | tf_op jit(solution)/shard_map/concatenate | solution.py:603
  10.7 1.9 %all-to-all-done.1 = f32[8,8,512]{2,1,0:T(8,128)S(1)} async-done(((f32[8,8,512]{2,1,0:T(8,128)}), f32[8,8,512]{2,1,0:T(8,128)S(1)}, u32[]{:S(2)}, u32[]{:S(2)}) %all-to-all-start.1) | async-done | bytes 131104 | tf_op jit(solution)/shard_map/all_to_all | solution.py:592
  12.6 4.4 %all-to-all-start = ((bf16[32,5,512]{2,1,0:T(8,128)(2,1)}), bf16[32,5,512]{2,1,0:T(8,128)(2,1)S(1)}, u32[]{:S(2)}, u32[]{:S(2)}) async-start(bf16[32,5,512]{2,1,0:T(8,128)(2,1)} %pad_maximum_fusion), calls=%async_computation | async-start | bytes 524288 | tf_op jit(solution)/shard_map/all_to_all | solution.py:604
  17.0 0.7 %reduce_sum.9 = f32[]{:T(128)} reduce(f32[64]{0:T(128)S(1)} %copy-done.3, f32[]{:T(128)} %constant.25.clone.1), dimensions={0}, to_apply=%region_0.1 | reduce | flops 63 | bytes 264 | tf_op jit(solution)/shard_map/reduce_sum | solution.py:618
  18.4 0.1 reshape.71
  18.5 0.1 copy.22
  18.6 0.1 copy.23
  18.7 0.7 %reshape.72.target_ref = f32[8,8,512]{2,1,0:T(8,128)} reshape(f32[8,2,2,2,512]{4,3,2,1,0:T(2,128)S(1)} %copy.23) | data formatting | bytes 262144 | tf_op jit(solution)/shard_map/reshape | solution.py:617
  19.4 7.6 %all-to-all-done = bf16[32,5,512]{2,1,0:T(8,128)(2,1)S(1)} async-done(((bf16[32,5,512]{2,1,0:T(8,128)(2,1)}), bf16[32,5,512]{2,1,0:T(8,128)(2,1)S(1)}, u32[]{:S(2)}, u32[]{:S(2)}) %all-to-all-start) | async-done | bytes 163872 | tf_op jit(solution)/shard_map/all_to_all | solution.py:604
  27.0 0.1 slice_convert_fusion
  27.1 0.1 reshape.80
  27.3 0.7 %reshape.76.tab_ref = f32[3,16,16]{2,1,0:T(8,128)} reshape(f32[3,4,4,4,4]{4,3,2,1,0:T(4,128)S(1)} %copy.14) | data formatting | bytes 6144 | tf_op jit(solution)/shard_map/reshape | solution.py:608
  28.0 0.3 reshape.83
  28.2 0.2 copy.29
  28.4 0.2 reshape.81
  28.7 0.2 copy.16
  28.9 0.9 %reshape.77.src_ref = f32[16,8,512]{2,1,0:T(8,128)} reshape(f32[4,4,2,2,2,512]{5,4,3,2,1,0:T(2,128)S(1)} %copy.16) | data formatting | bytes 524288 | tf_op jit(solution)/shard_map/convert_element_type | solution.py:615
  29.7 6.9 %shard_map.64.src_ref = f32[16,8,512]{2,1,0:T(8,128)} custom-call(f32[3,16,16]{2,1,0:T(8,128)} %reshape.76.tab_ref, f32[1]{0:T(128)} %bitcast.5.emitted_ref, f32[64]{0:T(128)} %spectrum_ref.1, f32[2,64]{1,0:T(2,128)} %attenuation_ref.1, f32[16,8,512]{2,1,0:T(8,128)} %reshape.77.src_ref, f32[8,8,512]{2,1,0:T(8,128)} %reshape.72.target_ref), custom_call_target="tpu_custom_call" | custom-call | tf_op jit(solution)/shard_map/pallas_call | solution.py:621
  36.7 3.9 %shard_map.65 = f32[32,4,512]{2,1,0:T(4,128)} custom-call(f32[3,16,16]{2,1,0:T(8,128)} %reshape.76.tab_ref, f32[16,8,512]{2,1,0:T(8,128)} %shard_map.64.src_ref), custom_call_target="tpu_custom_call" | custom-call | tf_op jit(solution)/shard_map/pallas_call | solution.py:633
  40.6 13.0 %all_to_all.15 = f32[8,2,2,4,512]{4,3,2,1,0:T(4,128)S(1)} all-to-all(f32[8,2,2,4,512]{4,3,2,1,0:T(4,128)} %bitcast.27), channel_id=1, replica_groups=mesh['views'=4,'depth'=4,'lat'=2] {'depth','lat'}, dimensions={0} | all-to-all | bytes 524288 | tf_op jit(solution)/shard_map/all_to_all | solution.py:645
  53.6 0.7 %copy.31 = f32[16,2,4,512]{3,2,1,0:T(4,128)} copy(f32[16,2,4,512]{3,2,1,0:T(4,128)S(1)} %bitcast.30) | data formatting | bytes 524288
  (18 shorter events, 0.2 us)
Async XLA Ops:
  1.1 7.6 %copy-start = (bf16[64,2,4,512]{3,2,1,0:T(4,128)(2,1)S(1)}, bf16[64,2,4,512]{3,2,1,0:T(4,128)(2,1)}, u32[]{:S(2)}) copy-start(bf16[64,2,4,512]{3,2,1,0:T(4,128)(2,1)} %param.6) | copy-start | bytes 1572868
  1.9 10.7 %all-to-all-start.1 = ((f32[8,8,512]{2,1,0:T(8,128)}), f32[8,8,512]{2,1,0:T(8,128)S(1)}, u32[]{:S(2)}, u32[]{:S(2)}) async-start(f32[8,8,512]{2,1,0:T(8,128)} %reshape.70), calls=%async_computation.1 | async-start | bytes 262144 | tf_op jit(solution)/shard_map/all_to_all | solution.py:592
  7.1 0.7 %copy-start.2 = (f32[4,4]{1,0:T(4,128)S(1)}, f32[4,4]{1,0:T(4,128)}, u32[]{:S(2)}) copy-start(f32[4,4]{1,0:T(4,128)} %param.9) | copy-start | bytes 196
  7.8 0.7 %copy-start.1 = (s32[4,4]{1,0:T(4,128)S(1)}, s32[4,4]{1,0:T(4,128)}, u32[]{:S(2)}) copy-start(s32[4,4]{1,0:T(4,128)} %param.8) | copy-start | bytes 196
  10.7 6.3 %copy-start.3 = (f32[64]{0:T(128)S(1)}, f32[64]{0:T(128)}, u32[]{:S(2)}) copy-start(f32[64]{0:T(128)} %spectrum_ref.1) | copy-start | bytes 772
  12.6 14.4 %all-to-all-start = ((bf16[32,5,512]{2,1,0:T(8,128)(2,1)}), bf16[32,5,512]{2,1,0:T(8,128)(2,1)S(1)}, u32[]{:S(2)}, u32[]{:S(2)}) async-start(bf16[32,5,512]{2,1,0:T(8,128)(2,1)} %pad_maximum_fusion), calls=%async_computation | async-start | bytes 524288 | tf_op jit(solution)/shard_map/all_to_all | solution.py:604

commit v19 on v18

--- a/solution.py
+++ b/solution.py
@@ -290,6 +290,15 @@
     return cols
 
 
+def table_entry(tab_ref, kind, view, level, views_here, depth_here):
+    block = views_here * depth_here
+    return tab_ref[
+        view // views_here,
+        level // depth_here,
+        kind * block + (view % views_here) * depth_here + level % depth_here,
+    ]
+
+
 def shear_pass(forward, rows_here, halves, tab_ref, src_ref, acc_ref, cols_ref, nexts_ref):
     outer_count, channels, width = src_ref.shape
     inner_count = acc_ref.shape[0]
@@ -310,18 +319,24 @@
 
     lax.fori_loop(0, outer_count, prepare, 0, unroll=True)
 
+    views_here = tab_ref.shape[2] // 3 // (outer_count // tab_ref.shape[1] if forward else inner_count // tab_ref.shape[1])
+    depth_here = (outer_count if forward else inner_count) // tab_ref.shape[1]
+
+    def tab(kind, view, level):
+        return table_entry(tab_ref, kind, view, level, views_here, depth_here)
+
     for i in range(inner_count):
 
         def one_input(o, acc):
             if forward:
-                shift = tab_ref[0, i, o].astype(jnp.int32)
-                wa = tab_ref[1, i, o]
-                wb = tab_ref[2, i, o]
+                shift = tab(0, i, o).astype(jnp.int32)
+                wa = tab(1, i, o)
+                wb = tab(2, i, o)
                 offset = shift + HALO
             else:
-                shift = tab_ref[0, o, i].astype(jnp.int32)
-                wa = tab_ref[2, o, i]
-                wb = tab_ref[1, o, i]
+                shift = tab(0, o, i).astype(jnp.int32)
+                wa = tab(2, o, i)
+                wb = tab(1, o, i)
                 offset = HALO - 1 - shift
             limit = LANES - offset
             amount = jnp.where(limit == LANES, 0, limit)
@@ -360,15 +375,19 @@
         return carry
 
     lax.fori_loop(0, outer_count, prepare, 0, unroll=True)
-    inner_count = tab_ref.shape[2]
+    inner_count = tab_ref.shape[1] * depth_here
+    views_here = tab_ref.shape[2] // 3 // depth_here
+
+    def tab(kind, view, z):
+        return table_entry(tab_ref, kind, view, z, views_here, depth_here)
 
     for i in range(inner_count):
         slab, level = divmod(i, depth_here)
 
         def one_view(o, acc):
-            shift = tab_ref[0, o, i].astype(jnp.int32)
-            wa = tab_ref[2, o, i]
-            wb = tab_ref[1, o, i]
+            shift = tab(0, o, i).astype(jnp.int32)
+            wa = tab(2, o, i)
+            wb = tab(1, o, i)
             offset = HALO - 1 - shift
             limit = LANES - offset
             amount = jnp.where(limit == LANES, 0, limit)
@@ -604,8 +623,6 @@
     mine = lax.all_to_all(mine, ("views", "depth", "lat"), 0, 0, tiled=True)
     mine = mine.reshape(groups, depth_count, halves, piece // tile_width + 1, tile_width)
     table = mine[:, :, 0, piece // tile_width, :entries].astype(jnp.float32)
-    table = table.reshape(groups, depth_count, 3, views_here, depth_here)
-    table = jnp.transpose(table, (2, 0, 3, 1, 4)).reshape(3, views_all, depth_all)
     mine = mine[:, :, :, : piece // tile_width].reshape(groups, depth_count, halves, piece)
     mine = jnp.transpose(mine, (1, 2, 0, 3)).reshape(
         depth_count, halves, rows_here, materials, depth_here, tile_width

time: 54.8 us -> 54.2 us (0.989)
  local copies, waits for them, and re-layouts: 8.8 us -> 7.83 us
    reshape x3 -> x0, local copies, waits for them, and re-layouts: 0.85 us -> none  [per_device_wide(): jnp.transpose(table, (2, 0, 3, 1, 4)).reshape(3, views_all, depth_all)]
    convert_element_type x0 -> x1, other arithmetic: none -> 0.61 us  [per_device_wide(): table = mine[:, :, 0, piece // tile_width, :entries].astype(jnp.float32)]
    convert_element_type x5 -> x4, local copies, waits for them, and re-layouts: 1.74 us -> 1.62 us  [per_device_wide(): mine = mine.astype(jnp.float32)]
where the time goes in v19:
time: 54.2 us; the launch traced here: 53.7 us
  blocking collectives  13 us (24%)
  Pallas kernels  10.6 us (20%)
  waiting for transfers between devices  9.68 us (18%)
  starting transfers between devices  9.61 us (18%)
  local copies, waits for them, and re-layouts  7.83 us (14%)
  other arithmetic  2.15 us (4%)
  between operations  0.79 us (1%)
    all_to_all x1, blocking collectives, per_device_wide(): layers = lax.all_to_all(layers, ('depth', 'lat'), 0, 0, tiled=True)  13 us
    all_to_all x1, waiting for transfers between devices, per_device_wide(): mine = lax.all_to_all(mine, ('views', 'depth', 'lat'), 0, 0, tiled=True)  7.76 us
    pallas_call x1, Pallas kernels, per_device_wide(): pl.pallas_call(functools.partial(forward_kernel, rows_here, halves, depth...  6.8 us
    all_to_all x1, starting transfers between devices, per_device_wide(): observed = lax.all_to_all(observed, ('views', 'lat'), 0, 0, tiled=True)  5.2 us
    all_to_all x1, starting transfers between devices, per_device_wide(): mine = lax.all_to_all(mine, ('views', 'depth', 'lat'), 0, 0, tiled=True)  4.41 us
    pallas_call x1, Pallas kernels, per_device_wide(): pl.pallas_call(functools.partial(backward_kernel, rows_here, halves), out...  3.83 us
    unnamed x9, local copies, waits for them, and re-layouts  2.07 us
    all_to_all x1, waiting for transfers between devices, per_device_wide(): observed = lax.all_to_all(observed, ('views', 'lat'), 0, 0, tiled=True)  1.92 us
  transfers between devices with their start and end apart: 2, of which 2 were waited for; matrix products, arithmetic and copies ran while one was open for 7% of the time, Pallas kernels for 0%

profile of v19, /device:TPU:0, one launch (start us, length us, event | category | flops | bytes accessed | tf_op | source)
XLA Modules:
  0.0 53.7 jit_solution(14607507576041051632)
XLA Ops:
  0.0 1.0 %constant_dynamic-slice_fusion.3 = (f32[4,4,512]{2,1,0:T(4,128)S(1)}, f32[4,4,512]{2,1,0:T(4,128)S(1)}, f32[4,4,512]{2,1,0:T(4,128)S(1)}, f32[4,4,512]{2,1,0:T(4,128)S(1)}) fusion(f32[4,64,512]{2,1,0:T(8,128)} %param.7, s32[]{:T(128)S(6)} %select_n.17, s32[]{:T(128)S(6)} %select_n.18, s32[]{:T(128)S(6)} %select_n.20, s32[]{:T(128)S(6)} %select_n.19), kind=kLoop, calls=%fused_computation.13 | loop fusion | bytes 262160 | tf_op jit(solution)/shard_map/dynamic_slice | solution.py:603
  1.1 0.0 copy-start
  1.1 0.1 copy.36
  1.2 0.7 %reshape.61 = f32[8,8,512]{2,1,0:T(8,128)} reshape(f32[4,2,4,2,512]{4,3,2,1,0:T(2,128)S(1)} %copy.36) | data formatting | bytes 262144 | tf_op jit(solution)/shard_map/reshape | solution.py:608
  1.9 5.2 %all-to-all-start.1 = ((f32[8,8,512]{2,1,0:T(8,128)}), f32[8,8,512]{2,1,0:T(8,128)S(1)}, u32[]{:S(2)}, u32[]{:S(2)}) async-start(f32[8,8,512]{2,1,0:T(8,128)} %reshape.61), calls=%async_computation.1 | async-start | bytes 262144 | tf_op jit(solution)/shard_map/all_to_all | solution.py:611
  7.1 0.7 %copy-done.2 = f32[4,4]{1,0:T(4,128)S(1)} copy-done((f32[4,4]{1,0:T(4,128)S(1)}, f32[4,4]{1,0:T(4,128)}, u32[]{:S(2)}) %copy-start.2) | copy-done | bytes 88
  7.8 0.7 %copy-done.1 = s32[4,4]{1,0:T(4,128)S(1)} copy-done((s32[4,4]{1,0:T(4,128)S(1)}, s32[4,4]{1,0:T(4,128)}, u32[]{:S(2)}) %copy-start.1) | copy-done | bytes 88
  8.5 0.1 reshape.57
  8.6 0.0 copy-done
  8.6 0.3 reshape.55
  9.0 0.8 %dynamic-slice_reduce_fusion = bf16[32,2048]{1,0:T(8,128)(2,1)S(1)} fusion(bf16[32,4,2048]{2,1,0:T(4,128)(2,1)S(1)} %reshape.55, s32[]{:T(128)S(6)} %select_n.16), kind=kLoop, calls=%fused_computation.1 | loop fusion | bytes 262148 | tf_op jit(solution)/shard_map/jit(dynamic_index_in_dim)/dynamic_slice | solution.py:618
  9.7 0.1 reshape.56
  9.9 0.8 %pad_maximum_fusion = bf16[32,5,512]{2,1,0:T(8,128)(2,1)} fusion(bf16[32,1,512]{2,1,0:T(2,128)(2,1)S(1)} %broadcast_in_dim.9, bf16[32,4,512]{2,1,0:T(4,128)(2,1)S(1)} %reshape.56), kind=kLoop, calls=%fused_computation | loop fusion | flops 327680 | bytes 327680 | tf_op jit(solution)/shard_map/concatenate | solution.py:622
  10.7 1.9 %all-to-all-done.1 = f32[8,8,512]{2,1,0:T(8,128)S(1)} async-done(((f32[8,8,512]{2,1,0:T(8,128)}), f32[8,8,512]{2,1,0:T(8,128)S(1)}, u32[]{:S(2)}, u32[]{:S(2)}) %all-to-all-start.1) | async-done | bytes 131104 | tf_op jit(solution)/shard_map/all_to_all | solution.py:611
  12.6 4.4 %all-to-all-start = ((bf16[32,5,512]{2,1,0:T(8,128)(2,1)}), bf16[32,5,512]{2,1,0:T(8,128)(2,1)S(1)}, u32[]{:S(2)}, u32[]{:S(2)}) async-start(bf16[32,5,512]{2,1,0:T(8,128)(2,1)} %pad_maximum_fusion), calls=%async_computation | async-start | bytes 524288 | tf_op jit(solution)/shard_map/all_to_all | solution.py:623
  17.0 0.0 copy-done.3
  17.0 0.6 %reduce_sum.9 = f32[]{:T(128)} reduce(f32[64]{0:T(128)S(1)} %copy-done.3, f32[]{:T(128)} %constant.25.clone.1), dimensions={0}, to_apply=%region_0.1 | reduce | flops 63 | bytes 264 | tf_op jit(solution)/shard_map/reduce_sum | solution.py:635
  18.3 0.1 reshape.62
  18.3 0.1 copy.37
  18.4 0.1 copy.38
  18.5 0.7 %reshape.63.target_ref = f32[8,8,512]{2,1,0:T(8,128)} reshape(f32[8,2,2,2,512]{4,3,2,1,0:T(2,128)S(1)} %copy.38) | data formatting | bytes 262144 | tf_op jit(solution)/shard_map/reshape | solution.py:634
  19.3 7.8 %all-to-all-done = bf16[32,5,512]{2,1,0:T(8,128)(2,1)S(1)} async-done(((bf16[32,5,512]{2,1,0:T(8,128)(2,1)}), bf16[32,5,512]{2,1,0:T(8,128)(2,1)S(1)}, u32[]{:S(2)}, u32[]{:S(2)}) %all-to-all-start) | async-done | bytes 163872 | tf_op jit(solution)/shard_map/all_to_all | solution.py:623
  27.0 0.1 slice_convert_fusion
  27.1 0.6 %fusion.tab_ref = f32[4,4,48]{2,1,0:T(4,128)} fusion(bf16[4,4,1,1,48]{4,3,2,1,0:T(2,128)(2,1)S(1)} %slice.8), kind=kLoop, calls=%fused_computation.5 | loop fusion | flops 768 | bytes 4608 | tf_op jit(solution)/shard_map/convert_element_type | solution.py:625
  27.7 0.3 reshape.69
  28.0 0.3 reshape.70
  28.3 0.2 copy.31
  28.5 0.9 %reshape.67.src_ref = f32[16,8,512]{2,1,0:T(8,128)} reshape(f32[4,4,2,2,2,512]{5,4,3,2,1,0:T(2,128)S(1)} %copy.31) | data formatting | bytes 524288 | tf_op jit(solution)/shard_map/convert_element_type | solution.py:632
  29.3 6.8 %shard_map.64.src_ref = f32[16,8,512]{2,1,0:T(8,128)} custom-call(f32[4,4,48]{2,1,0:T(4,128)} %fusion.tab_ref, f32[1]{0:T(128)} %bitcast.6.emitted_ref, f32[64]{0:T(128)} %spectrum_ref.1, f32[2,64]{1,0:T(2,128)} %attenuation_ref.1, f32[16,8,512]{2,1,0:T(8,128)} %reshape.67.src_ref, f32[8,8,512]{2,1,0:T(8,128)} %reshape.63.target_ref), custom_call_target="tpu_custom_call" | custom-call | tf_op jit(solution)/shard_map/pallas_call | solution.py:638
  36.2 3.8 %shard_map.65 = f32[32,4,512]{2,1,0:T(4,128)} custom-call(f32[4,4,48]{2,1,0:T(4,128)} %fusion.tab_ref, f32[16,8,512]{2,1,0:T(8,128)} %shard_map.64.src_ref), custom_call_target="tpu_custom_call" | custom-call | tf_op jit(solution)/shard_map/pallas_call | solution.py:650
  40.0 13.0 %all_to_all.15 = f32[8,2,2,4,512]{4,3,2,1,0:T(4,128)S(1)} all-to-all(f32[8,2,2,4,512]{4,3,2,1,0:T(4,128)} %bitcast.30), channel_id=1, replica_groups=mesh['views'=4,'depth'=4,'lat'=2] {'depth','lat'}, dimensions={0} | all-to-all | bytes 524288 | tf_op jit(solution)/shard_map/all_to_all | solution.py:662
  53.0 0.7 %copy.49 = f32[16,2,4,512]{3,2,1,0:T(4,128)} copy(f32[16,2,4,512]{3,2,1,0:T(4,128)S(1)} %bitcast.33) | data formatting | bytes 524288
  (14 shorter events, 0.2 us)
Async XLA Ops:
  1.1 7.6 %copy-start = (bf16[64,2,4,512]{3,2,1,0:T(4,128)(2,1)S(1)}, bf16[64,2,4,512]{3,2,1,0:T(4,128)(2,1)}, u32[]{:S(2)}) copy-start(bf16[64,2,4,512]{3,2,1,0:T(4,128)(2,1)} %param.6) | copy-start | bytes 1572868
  1.9 10.7 %all-to-all-start.1 = ((f32[8,8,512]{2,1,0:T(8,128)}), f32[8,8,512]{2,1,0:T(8,128)S(1)}, u32[]{:S(2)}, u32[]{:S(2)}) async-start(f32[8,8,512]{2,1,0:T(8,128)} %reshape.61), calls=%async_computation.1 | async-start | bytes 262144 | tf_op jit(solution)/shard_map/all_to_all | solution.py:611
  7.1 0.7 %copy-start.2 = (f32[4,4]{1,0:T(4,128)S(1)}, f32[4,4]{1,0:T(4,128)}, u32[]{:S(2)}) copy-start(f32[4,4]{1,0:T(4,128)} %param.9) | copy-start | bytes 196
  7.8 0.7 %copy-start.1 = (s32[4,4]{1,0:T(4,128)S(1)}, s32[4,4]{1,0:T(4,128)}, u32[]{:S(2)}) copy-start(s32[4,4]{1,0:T(4,128)} %param.8) | copy-start | bytes 196
  10.7 6.3 %copy-start.3 = (f32[64]{0:T(128)S(1)}, f32[64]{0:T(128)}, u32[]{:S(2)}) copy-start(f32[64]{0:T(128)} %spectrum_ref.1) | copy-start | bytes 772
  12.6 14.4 %all-to-all-start = ((bf16[32,5,512]{2,1,0:T(8,128)(2,1)}), bf16[32,5,512]{2,1,0:T(8,128)(2,1)S(1)}, u32[]{:S(2)}, u32[]{:S(2)}) async-start(bf16[32,5,512]{2,1,0:T(8,128)(2,1)} %pad_maximum_fusion), calls=%async_computation | async-start | bytes 524288 | tf_op jit(solution)/shard_map/all_to_all | solution.py:623
